TPU v7x, 32 devices: a whole 2x2x4 slice. The times are simulated.
32 devices in a mesh: section: 8 (over z, y), tensor: 4 (over x, core).
Axes of the slice: x: 2, y: 2, z: 4, core: 2. Of those that a mesh axis runs over, the one named last changes fastest.
Arguments:
- vision_tokens: bfloat16 [2048, 1664], P('section'), may hold values from -6 to 6
- key_weight: bfloat16 [3328, 8192], P('section', 'tensor'), may hold values from -0.15625 to 0.15625
- value_weight: bfloat16 [3328, 8192], P('section', 'tensor'), may hold values from -0.15625 to 0.15625
- queries: bfloat16 [8, 1024, 8192], P('section', None, 'tensor'), may hold values from -6 to 6
- gate: float32 [2], replicated, may hold values from 0.3 to 1.5
- visible: int32 [4, 4, 4], replicated, may hold values from -1 to 1, as said below
- out_grad: bfloat16 [8, 1024, 8192], P('section', None, 'tensor'), may hold values from -6 to 6
Outputs:
- attended: bfloat16 [8, 1024, 8192], P('section', None, 'tensor')
- vision_grad: bfloat16 [2048, 1664], P('section')
Inputs may be any that keep to these rules, and one draw needn't show every extreme that they name: `visible`: each row of 4 entries is non-decreasing, and every image index 0 to 1 occurs in every row.
All inputs are finite; a program needn't handle non-finite values.
Results may differ from a plain program's by a relative error of at most 0.029.
Values may be sent and summed in bfloat16 or wider, within the bound.
No kernel may reach another device: no remote copies, remote signals or barrier semaphores. Data moves between devices by JAX's collectives and lax.ppermute only.
A program may use at most 128 MiB of HBM per device.

v0:
```python
import jax
import jax.numpy as jnp
from jax import lax
from jax.sharding import PartitionSpec as P

HD = 128
IMG_TOK = 64
TBLOCK = 64
IMGS = 2
MICRO = 4


def from_partner(value, axis, distance):
    mask = 2**distance
    pairs = [(source, source ^ mask) for source in range(lax.axis_size(axis))]
    return lax.ppermute(value, axis, pairs)


def block_index(visible):
    samples = visible.shape[0]
    base = jnp.arange(samples, dtype=jnp.int32)[:, None] * IMGS
    seen = (base + jnp.maximum(visible, 0)).reshape(-1)
    validf = (visible >= 0).reshape(-1).astype(jnp.float32)
    return (seen, validf)


def local_layer(key_rows, value_rows, query, gate_value, cotangent, visible, heads):
    width = heads * HD
    seen, validf = block_index(visible)
    images = key_rows.shape[0] // IMG_TOK
    key_img = jnp.take(key_rows.reshape(images, IMG_TOK, heads, HD), seen, axis=0)
    val_img = jnp.take(value_rows.reshape(images, IMG_TOK, heads, HD), seen, axis=0)
    blocks = seen.shape[0]
    query_b = query.reshape(blocks, TBLOCK, heads, HD)
    scale = 1.0 / HD**0.5
    scores = (
        jnp.einsum("bqhd,bkhd->bhqk", query_b, key_img, preferred_element_type=jnp.float32) * scale
    )
    exponent = jnp.exp(scores)
    probs = exponent / jnp.sum(exponent, axis=-1, keepdims=True) * validf[:, None, None, None]
    probs_b = probs.astype(jnp.bfloat16)
    mixed = jnp.einsum("bhqk,bkhd->bqhd", probs_b, val_img, preferred_element_type=jnp.float32)
    factor = jnp.tanh(gate_value)
    attended = (factor * mixed).astype(jnp.bfloat16).reshape(-1, width)
    head_grad = (
        (factor * cotangent.astype(jnp.float32))
        .astype(jnp.bfloat16)
        .reshape(blocks, TBLOCK, heads, HD)
    )
    vgrad_blk = jnp.einsum(
        "bhqk,bqhd->bkhd", probs_b, head_grad, preferred_element_type=jnp.float32
    )
    prob_grad = jnp.einsum(
        "bqhd,bkhd->bhqk", head_grad, val_img, preferred_element_type=jnp.float32
    )
    delta = jnp.sum(probs * prob_grad, axis=-1, keepdims=True)
    score_grad = (probs * (prob_grad - delta) * scale).astype(jnp.bfloat16)
    kgrad_blk = jnp.einsum(
        "bhqk,bqhd->bkhd", score_grad, query_b, preferred_element_type=jnp.float32
    )
    onehot = (seen[:, None] == jnp.arange(images, dtype=jnp.int32)[None, :]).astype(jnp.float32)
    key_grad = (
        jnp.einsum("bi,bkhd->ikhd", onehot, kgrad_blk).reshape(-1, width).astype(jnp.bfloat16)
    )
    value_grad = (
        jnp.einsum("bi,bkhd->ikhd", onehot, vgrad_blk).reshape(-1, width).astype(jnp.bfloat16)
    )
    return (attended, key_grad, value_grad)


def back_product(grad_rows, weight):
    return lax.dot_general(
        grad_rows, weight, (((1,), (1,)), ((), ())), preferred_element_type=jnp.float32
    )


def upper_bit(position, bit):
    return position // 2**bit % 2 == 1


def join_pair(mine, partner, upper, axis):
    low_first = jnp.concatenate([mine, partner], axis=axis)
    high_first = jnp.concatenate([partner, mine], axis=axis)
    return jnp.where(upper, high_first, low_first)


def split_pair(values, upper):
    half = values.shape[0] // 2
    lower_rows = values[:half]
    upper_rows = values[half:]
    keep = jnp.where(upper, upper_rows, lower_rows)
    give = jnp.where(upper, lower_rows, upper_rows)
    return (keep, give)


def reduce_first(values, position, layer_bits):
    for bit in reversed(range(layer_bits)):
        keep, give = split_pair(values, upper_bit(position, bit))
        values = keep + from_partner(give.astype(jnp.bfloat16), "section", bit).astype(give.dtype)
    return values


def shards(vision_tokens, key_weight, value_weight, queries, gate, visible, out_grad):
    position = lax.axis_index("section")
    layers = lax.axis_size("section") // MICRO
    layer_bits = layers.bit_length() - 1
    layer = position % layers
    micro = position // layers
    stacked = jnp.stack([key_weight, value_weight])
    for offset in range(2):
        bit = layer_bits + offset
        partner = from_partner(stacked, "section", bit)
        stacked = join_pair(stacked, partner, upper_bit(position, bit), 1)
    w_key = stacked[0]
    w_value = stacked[1]
    width = w_key.shape[1]
    heads = width // HD
    gate_value = lax.dynamic_index_in_dim(gate, layer, 0, keepdims=False)
    own_visible = lax.dynamic_index_in_dim(visible, micro, 0, keepdims=False)
    all_rows = vision_tokens
    for bit in range(layer_bits):
        partner = from_partner(all_rows, "section", bit)
        all_rows = join_pair(all_rows, partner, upper_bit(position, bit), 0)
    key_rows = jnp.dot(all_rows, w_key, preferred_element_type=jnp.float32).astype(jnp.bfloat16)
    value_rows = jnp.dot(all_rows, w_value, preferred_element_type=jnp.float32).astype(jnp.bfloat16)
    attended, key_grad, value_grad = local_layer(
        key_rows, value_rows, queries[0], gate_value, out_grad[0], own_visible, heads
    )
    term = back_product(key_grad, w_key) + back_product(value_grad, w_value)
    summed = lax.psum(term.astype(jnp.bfloat16), "tensor").astype(jnp.float32)
    owned = reduce_first(summed, position, layer_bits).astype(jnp.bfloat16)
    return (attended[None], owned)


def solution(mesh):
    placed = (
        P("section", None),
        P("section", "tensor"),
        P("section", "tensor"),
        P("section", None, "tensor"),
        P(),
        P(),
        P("section", None, "tensor"),
    )
    return jax.shard_map(
        shards,
        mesh=mesh,
        in_specs=placed,
        out_specs=(P("section", None, "tensor"), P("section", None)),
        check_vma=False,
    )
```

profile of v0, /device:TPU:0, one launch (start us, length us, event | category | flops | bytes accessed | tf_op | source)
XLA Modules:
  0.0 583.1 jit_solution(2185115910670889162)
XLA Ops:
  7.2 0.0 all-reduce.2.cloned.1.call-start
  7.2 4.2 pad_maximum_fusion
  11.4 3.1 collective-permute-start.1
  14.5 74.0 %collective-permute-done.1 = bf16[2,416,2048]{2,1,0:T(8,128)(2,1)} collective-permute-done((bf16[2,416,2048]{2,1,0:T(8,128)(2,1)}, bf16[2,416,2048]{2,1,0:T(8,128)(2,1)}, u32[]{:S(2)}, u32[]{:S(2)}) %collective-permute-start.1) | collective-permute-done | bytes 3407904 | tf_op jit(solution)/shard_map/ppermute | solution.py:16
  88.5 7.5 %maximum_select_fusion.1 = bf16[2,832,2048]{2,1,0:T(8,128)(2,1)} fusion(bf16[1,416,2048]{2,1,0:T(8,128)(2,1)S(1)} %bitcast.97, bf16[1,416,2048]{2,1,0:T(8,128)(2,1)S(1)} %bitcast.99, bf16[2,416,2048]{2,1,0:T(8,128)(2,1)} %collective-permute-done.1, pred[]{:T(512)S(6)} %eq.31), kind=kLoop, calls=%fused_computation.21 | loop fusion | flops 44302336 | bytes 13631489 | tf_op jit(solution)/shard_map/jit(_where)/select_n | solution.py:84
  96.0 2.8 collective-permute-start.2
  98.8 1.5 collective-permute-start
  100.3 0.6 dynamic_slice.8
  101.6 0.1 add.53
  101.7 0.1 add.54
  101.8 0.1 reshape.64
  101.8 0.1 max.12
  101.9 5.7 copy.29
  107.6 1.7 fusion.19
  109.4 3.4 copy.30
  112.8 278.4 %collective-permute-done.2 = bf16[2,832,2048]{2,1,0:T(8,128)(2,1)} collective-permute-done((bf16[2,832,2048]{2,1,0:T(8,128)(2,1)}, bf16[2,832,2048]{2,1,0:T(8,128)(2,1)}, u32[]{:S(2)}, u32[]{:S(2)}) %collective-permute-start.2) | collective-permute-done | bytes 6815776 | tf_op jit(solution)/shard_map/ppermute | solution.py:16
  391.2 12.1 %maximum_select_fusion = bf16[2,1664,2048]{2,1,0:T(8,128)(2,1)S(1)} fusion(bf16[2,832,2048]{2,1,0:T(8,128)(2,1)} %maximum_select_fusion.1, bf16[2,832,2048]{2,1,0:T(8,128)(2,1)} %collective-permute-done.2, pred[]{:T(512)S(6)} %eq.30), kind=kLoop, calls=%fused_computation.3 | loop fusion | flops 61341696 | bytes 27262976 | tf_op jit(solution)/shard_map/jit(_where)/select_n | solution.py:84
  403.4 6.8 %fusion.49 = bf16[64,8,16,128]{3,1,2,0:T(8,128)(2,1)S(1)} fusion(bf16[2,1664,2048]{2,1,0:T(8,128)(2,1)S(1)} %maximum_select_fusion, bf16[256,1664]{1,0:T(8,128)(2,1)} %param.9, bf16[256,1664]{1,0:T(8,128)(2,1)S(1)} %collective-permute-done, pred[]{:T(512)S(6)} %eq.29), kind=kOutput, calls=%fused_computation.59 | convolution fusion | flops 3498377216 | bytes 10616833 | tf_op jit(solution)/shard_map/dot_general | solution.py:124
  410.1 0.6 copy.28
  410.8 5.5 fusion.48
  416.2 2.0 copy.27
  418.2 4.6 gather_fusion
  422.8 3.1 gather_fusion.1
  425.9 4.4 broadcast_select_fusion
  430.3 0.0 copy-start
  430.3 0.2 copy-done.2
  430.6 5.5 bitcast_reduce_fusion
  436.1 5.7 fusion.25
  441.8 7.9 %fusion.23 = bf16[16,16,128,64]{2,3,1,0:T(8,128)(2,1)} fusion(bf16[16,64,16,128]{3,2,1,0:T(8,128)(2,1)S(1)} %bitcast.93, f32[16,16,64,64]{3,2,1,0:T(8,128)} %get-tuple-element.8, f32[16]{0:T(128)S(1)} %reshape.64, f32[16,16,64]{2,1,0:T(8,128)S(1)} %get-tuple-element.7), kind=kOutput, calls=%fused_computation.34 | convolution fusion | flops 272629760 | bytes 12648512 | tf_op jit(solution)/shard_map/bhqk,bqhd->bkhd/dot_general | solution.py:50
  449.7 17.6 %fusion.16 = bf16[16,16,64,128]{3,2,1,0:T(8,128)(2,1)} fusion(f32[16,16,64,64]{2,3,1,0:T(8,128)} %fusion.25, bf16[16,64,16,128]{3,2,1,0:T(8,128)(2,1)} %bitcast.90, f32[16,16,64,64]{3,2,1,0:T(8,128)} %get-tuple-element.8, f32[16]{0:T(128)S(1)} %reshape.64, f32[16,16,64]{2,1,0:T(8,128)S(1)} %get-tuple-element.7), kind=kOutput, calls=%fused_computation.26 | convolution fusion | flops 279986240 | bytes 16842816 | tf_op jit(solution)/shard_map/bhqk,bqhd->bkhd/dot_general | solution.py:58
  467.3 10.6 %fusion.45 = bf16[8,64,16,128]{3,0,2,1:T(8,128)(2,1)S(1)} fusion(bf16[16,16,128,64]{2,3,1,0:T(8,128)(2,1)} %fusion.23, s32[16]{0:T(128)S(1)} %get-tuple-element.4), kind=kOutput, calls=%fused_computation.54 | convolution fusion | flops 33554560 | bytes 6291520 | tf_op jit(solution)/shard_map/bi,bkhd->ikhd/dot_general | solution.py:66
  477.9 8.5 %fusion.42 = bf16[8,64,16,128]{3,0,2,1:T(8,128)(2,1)S(1)} fusion(bf16[16,16,64,128]{3,2,1,0:T(8,128)(2,1)S(1)} %copy-done.8, s32[16]{0:T(128)S(1)} %get-tuple-element.4), kind=kOutput, calls=%fused_computation.53 | convolution fusion | flops 33554560 | bytes 6291520 | tf_op jit(solution)/shard_map/bi,bkhd->ikhd/dot_general | solution.py:63
  486.3 0.3 copy.21
  486.6 0.0 slice-start
  486.6 0.3 copy.22
  486.9 0.0 slice-start.1
  486.9 0.0 slice-start.2
  487.0 7.1 %fusion.9 = f32[512,1664]{1,0:T(8,128)S(1)} fusion(bf16[2,1664,2048]{2,1,0:T(8,128)(2,1)} %copy-done.5, bf16[64,8,16,128]{3,2,1,0:T(8,128)(2,1)S(1)} %bitcast.102), kind=kOutput, calls=%fused_computation.22 | convolution fusion | flops 3489660928 | bytes 12320768 | tf_op jit(solution)/shard_map/dot_general | solution.py:72
  494.1 5.4 add_convert_fusion
  499.5 0.0 all-reduce.2.cloned.1.call-update
  499.6 46.1 %all-reduce.2.cloned.1.call-done = bf16[512,1664]{1,0:T(8,128)(2,1)} async-done(((bf16[512,1664]{1,0:T(8,128)(2,1)}), bf16[512,1664]{1,0:T(8,128)(2,1)}) %all-reduce.2.cloned.1.call-update) | async-done | bytes 1703952 | tf_op jit(solution)/shard_map/psum | solution.py:130
  545.7 1.8 convert_element_type.84
  547.5 1.1 select_convert_fusion
  548.6 1.5 collective-permute-start.3
  550.1 8.5 %fusion.18 = bf16[16,64,16,128]{3,1,2,0:T(8,128)(2,1)} fusion(f32[]{:T(128)} %bitcast, bf16[16,64,16,128]{3,2,1,0:T(8,128)(2,1)S(1)} %copy-done.1, f32[16,16,64,64]{3,2,1,0:T(8,128)} %get-tuple-element.8, f32[16]{0:T(128)S(1)} %reshape.64, f32[16,16,64]{2,1,0:T(8,128)S(1)} %get-tuple-element.7), kind=kOutput, calls=%fused_computation.27 | convolution fusion | flops 276824064 | bytes 12648516 | tf_op jit(solution)/shard_map/bhqk,bkhd->bqhd/dot_general | solution.py:42
  558.6 7.7 %copy.18 = bf16[16,64,16,128]{3,2,1,0:T(8,128)(2,1)} copy(bf16[16,64,16,128]{3,1,2,0:T(8,128)(2,1)} %fusion.18) | data formatting | bytes 8388608 | tf_op jit(solution)/shard_map/convert_element_type | solution.py:44
  566.3 7.3 %broadcast_in_dim_reshape.4 = bf16[1,1024,2048]{2,1,0:T(8,128)(2,1)} reshape(bf16[16,64,16,128]{3,2,1,0:T(8,128)(2,1)} %copy.18) | data formatting | bytes 8388608 | tf_op jit(solution)/shard_map/broadcast_in_dim;reshape | solution.py:132
  573.5 2.3 add_convert_fusion.1
  (36 shorter events, 0.1 us)
Async XLA Ops:
  7.2 81.3 %copy-start.6 = (bf16[416,2048]{1,0:T(8,128)(2,1)S(1)}, bf16[416,2048]{1,0:T(8,128)(2,1)}, u32[]{:S(2)}) copy-start(bf16[416,2048]{1,0:T(8,128)(2,1)} %param.11) | copy-start | bytes 5111812
  7.2 81.3 %copy-start.7 = (bf16[416,2048]{1,0:T(8,128)(2,1)S(1)}, bf16[416,2048]{1,0:T(8,128)(2,1)}, u32[]{:S(2)}) copy-start(bf16[416,2048]{1,0:T(8,128)(2,1)} %param.10) | copy-start | bytes 5111812
  7.2 538.5 %all-reduce.2.cloned.1.call-start = ((), (), s32[]{:S(2)}) async-start(), calls=%async_computation | async-start | bytes 3407872 | tf_op jit(solution)/shard_map/psum | solution.py:130
  11.4 77.1 %collective-permute-start.1 = (bf16[2,416,2048]{2,1,0:T(8,128)(2,1)}, bf16[2,416,2048]{2,1,0:T(8,128)(2,1)}, u32[]{:S(2)}, u32[]{:S(2)}) collective-permute-start(bf16[2,416,2048]{2,1,0:T(8,128)(2,1)} %pad_maximum_fusion), channel_id=1, source_target_pairs={{0,8},{4,12},{8,0},{12,4},{16,24},{20,28},{24,16},{28,20},{1,9},{5... | collective-permute-start | bytes 10223624 | tf_op jit(solution)/shard_map/ppermute | solution.py:16
  14.5 85.8 %copy-start.11 = (f32[2]{0:T(128)S(1)}, f32[2]{0:T(128)}, u32[]{:S(2)}) copy-start(f32[2]{0:T(128)} %param.13) | copy-start | bytes 28
  14.5 87.3 %copy-start.10 = (s32[4,4,4]{2,1,0:T(4,128)S(1)}, s32[4,4,4]{2,1,0:T(4,128)}, u32[]{:S(2)}) copy-start(s32[4,4,4]{2,1,0:T(4,128)} %param.14) | copy-start | bytes 772
  96.0 295.2 %collective-permute-start.2 = (bf16[2,832,2048]{2,1,0:T(8,128)(2,1)}, bf16[2,832,2048]{2,1,0:T(8,128)(2,1)}, u32[]{:S(2)}, u32[]{:S(2)}) collective-permute-start(bf16[2,832,2048]{2,1,0:T(8,128)(2,1)} %maximum_select_fusion.1), channel_id=1, source_target_pairs={{0,16},{4,20},{8,24},{12,28},{16,0},{20,4},{24,8},{28,12},{1,17},{... | collective-permute-start | bytes 20447240 | tf_op jit(solution)/shard_map/ppermute | solution.py:16
  98.8 304.6 %collective-permute-start = (bf16[256,1664]{1,0:T(8,128)(2,1)}, bf16[256,1664]{1,0:T(8,128)(2,1)S(1)}, u32[]{:S(2)}, u32[]{:S(2)}) collective-permute-start(bf16[256,1664]{1,0:T(8,128)(2,1)} %param.9), channel_id=1, source_target_pairs={{0,4},{4,0},{8,12},{12,8},{16,20},{20,16},{24,28},{28,24},{1,5},{5... | collective-permute-start | bytes 2555912 | tf_op jit(solution)/shard_map/ppermute | solution.py:16
  101.9 5.7 copy-start.9
  403.4 7.4 %copy-start.5 = (bf16[2,1664,2048]{2,1,0:T(8,128)(2,1)}, bf16[2,1664,2048]{2,1,0:T(8,128)(2,1)S(1)}, u32[]{:S(2)}) copy-start(bf16[2,1664,2048]{2,1,0:T(8,128)(2,1)S(1)} %maximum_select_fusion) | copy-start | bytes 40894468
  425.9 4.6 copy-start.2
  430.3 5.8 copy-start
  430.6 5.5 copy-start.3
  436.1 5.7 copy-start.4
  467.2 10.6 %copy-start.8 = (bf16[16,16,64,128]{3,2,1,0:T(8,128)(2,1)S(1)}, bf16[16,16,64,128]{3,2,1,0:T(8,128)(2,1)}, u32[]{:S(2)}) copy-start(bf16[16,16,64,128]{3,2,1,0:T(8,128)(2,1)} %fusion.16) | copy-start | bytes 12582916
  486.6 7.4 %slice-start = ((s8[13631488]{0:T(1024)(128)(4,1)}), s8[4194304]{0:T(1024)(128)(4,1)S(1)}, s32[]{:S(2)}) async-start(s8[13631488]{0:T(1024)(128)(4,1)} %bitcast.94), calls=%async_computation.1 | async-start | bytes 8388608
  486.9 7.1 %slice-start.1 = ((s8[13631488]{0:T(1024)(128)(4,1)}), s8[4194304]{0:T(1024)(128)(4,1)S(1)}, s32[]{:S(2)}) async-start(s8[13631488]{0:T(1024)(128)(4,1)} %bitcast.94), calls=%async_computation.2 | async-start | bytes 8388608
  486.9 7.1 %slice-start.2 = ((s8[13631488]{0:T(1024)(128)(4,1)}), s8[4194304]{0:T(1024)(128)(4,1)S(1)}, s32[]{:S(2)}) async-start(s8[13631488]{0:T(1024)(128)(4,1)} %bitcast.94), calls=%async_computation.3 | async-start | bytes 8388608
  486.9 7.1 %slice-start.3 = ((s8[13631488]{0:T(1024)(128)(4,1)}), s8[1048576]{0:T(1024)(128)(4,1)S(1)}, s32[]{:S(2)}) async-start(s8[13631488]{0:T(1024)(128)(4,1)} %bitcast.94), calls=%async_computation.4 | async-start | bytes 2097152
  545.7 4.4 copy-start.1
  548.6 24.9 %collective-permute-start.3 = (bf16[256,1664]{1,0:T(8,128)(2,1)}, bf16[256,1664]{1,0:T(8,128)(2,1)}, u32[]{:S(2)}, u32[]{:S(2)}) collective-permute-start(bf16[256,1664]{1,0:T(8,128)(2,1)} %select_convert_fusion), channel_id=1, source_target_pairs={{0,4},{4,0},{8,12},{12,8},{16,20},{20,16},{24,28},{28,24},{1,5},{5... | collective-permute-start | bytes 2555912 | tf_op jit(solution)/shard_map/ppermute | solution.py:16
Sparse Core Ops, SparseCore 0:
  499.7 45.9 all-reduce.1
where the time goes:
time: 587 us; the launch traced here: 583 us
  waiting for transfers between devices  399 us (68%)
  matrix products  89 us (15%)
  local copies, waits for them, and re-layouts  36.1 us (6%)
  other arithmetic  35.2 us (6%)
  between operations  15.4 us (3%)
  starting transfers between devices  8.84 us (2%)
    ppermute x4, waiting for transfers between devices, from_partner(): return lax.ppermute(value, axis, pairs)  352 us
    psum x1, waiting for transfers between devices, shards(): summed = lax.psum(term.astype(jnp.bfloat16), 'tensor').astype(jnp.float32)  46.1 us
    select_n x2, other arithmetic, join_pair(): return jnp.where(upper, high_first, low_first)  19.7 us
    dot_general x1, matrix products, local_layer(): jnp.einsum('bhqk,bqhd->bkhd', score_grad, query_b, preferred_element_type...  17.6 us
    dot_general x2, matrix products, back_product(): lax.dot_general(grad_rows, weight, (((1,), (1,)), ((), ())), preferred_el...  12.5 us
    unnamed x36, local copies, waits for them, and re-layouts  12 us
  transfers between devices with their start and end apart: 5, of which 3 were waited for; matrix products, arithmetic and copies ran while one was open for 8% of the time, Pallas kernels for 0%

commit v1 on v0

--- a/solution.py
+++ b/solution.py
@@ -1,6 +1,8 @@
 import jax
 import jax.numpy as jnp
+import numpy as np
 from jax import lax
+from jax.sharding import Mesh
 from jax.sharding import PartitionSpec as P
 
 HD = 128
@@ -8,12 +10,6 @@
 TBLOCK = 64
 IMGS = 2
 MICRO = 4
-
-
-def from_partner(value, axis, distance):
-    mask = 2**distance
-    pairs = [(source, source ^ mask) for source in range(lax.axis_size(axis))]
-    return lax.ppermute(value, axis, pairs)
 
 
 def block_index(visible):
@@ -74,78 +70,49 @@
     )
 
 
-def upper_bit(position, bit):
-    return position // 2**bit % 2 == 1
-
-
-def join_pair(mine, partner, upper, axis):
-    low_first = jnp.concatenate([mine, partner], axis=axis)
-    high_first = jnp.concatenate([partner, mine], axis=axis)
-    return jnp.where(upper, high_first, low_first)
-
-
-def split_pair(values, upper):
-    half = values.shape[0] // 2
-    lower_rows = values[:half]
-    upper_rows = values[half:]
-    keep = jnp.where(upper, upper_rows, lower_rows)
-    give = jnp.where(upper, lower_rows, upper_rows)
-    return (keep, give)
-
-
-def reduce_first(values, position, layer_bits):
-    for bit in reversed(range(layer_bits)):
-        keep, give = split_pair(values, upper_bit(position, bit))
-        values = keep + from_partner(give.astype(jnp.bfloat16), "section", bit).astype(give.dtype)
-    return values
-
-
 def shards(vision_tokens, key_weight, value_weight, queries, gate, visible, out_grad):
-    position = lax.axis_index("section")
-    layers = lax.axis_size("section") // MICRO
-    layer_bits = layers.bit_length() - 1
-    layer = position % layers
-    micro = position // layers
+    layer = lax.axis_index("layer")
+    micro = lax.axis_index("micro")
     stacked = jnp.stack([key_weight, value_weight])
-    for offset in range(2):
-        bit = layer_bits + offset
-        partner = from_partner(stacked, "section", bit)
-        stacked = join_pair(stacked, partner, upper_bit(position, bit), 1)
+    stacked = lax.all_gather(stacked, "micro", axis=1, tiled=True)
     w_key = stacked[0]
     w_value = stacked[1]
     width = w_key.shape[1]
     heads = width // HD
     gate_value = lax.dynamic_index_in_dim(gate, layer, 0, keepdims=False)
     own_visible = lax.dynamic_index_in_dim(visible, micro, 0, keepdims=False)
-    all_rows = vision_tokens
-    for bit in range(layer_bits):
-        partner = from_partner(all_rows, "section", bit)
-        all_rows = join_pair(all_rows, partner, upper_bit(position, bit), 0)
+    all_rows = lax.all_gather(vision_tokens, "layer", axis=0, tiled=True)
     key_rows = jnp.dot(all_rows, w_key, preferred_element_type=jnp.float32).astype(jnp.bfloat16)
     value_rows = jnp.dot(all_rows, w_value, preferred_element_type=jnp.float32).astype(jnp.bfloat16)
     attended, key_grad, value_grad = local_layer(
         key_rows, value_rows, queries[0], gate_value, out_grad[0], own_visible, heads
     )
     term = back_product(key_grad, w_key) + back_product(value_grad, w_value)
-    summed = lax.psum(term.astype(jnp.bfloat16), "tensor").astype(jnp.float32)
-    owned = reduce_first(summed, position, layer_bits).astype(jnp.bfloat16)
+    part = lax.psum_scatter(term.astype(jnp.bfloat16), "layer", scatter_dimension=0, tiled=True)
+    owned = lax.psum(part, "tensor")
     return (attended[None], owned)
 
 
 def solution(mesh):
+    sections, tensors = mesh.devices.shape
+    grid = Mesh(
+        np.asarray(mesh.devices).reshape(MICRO, sections // MICRO, tensors),
+        ("micro", "layer", "tensor"),
+    )
+    rows = ("micro", "layer")
     placed = (
-        P("section", None),
-        P("section", "tensor"),
-        P("section", "tensor"),
-        P("section", None, "tensor"),
+        P(rows, None),
+        P(rows, "tensor"),
+        P(rows, "tensor"),
+        P(rows, None, "tensor"),
         P(),
         P(),
-        P("section", None, "tensor"),
+        P(rows, None, "tensor"),
     )
     return jax.shard_map(
         shards,
-        mesh=mesh,
+        mesh=grid,
         in_specs=placed,
-        out_specs=(P("section", None, "tensor"), P("section", None)),
+        out_specs=(P(rows, None, "tensor"), P(rows, None)),
         check_vma=False,
     )

time: 587 us -> 466 us (0.79)
  waiting for transfers between devices: 399 us -> 297 us
  other arithmetic: 35.2 us -> 10.2 us
  local copies, waits for them, and re-layouts: 36.1 us -> 46.2 us
  starting transfers between devices: 8.84 us -> 0.37 us
    ppermute x4 -> x0, waiting for transfers between devices: 352 us -> none  [from_partner(): return lax.ppermute(value, axis, pairs)]
    all_gather x0 -> x2, waiting for transfers between devices: none -> 254 us  [the longest x1 238 us: shards(): stacked = lax.all_gather(stacked, 'micro', axis=1, tiled=True)]
    psum x1, waiting for transfers between devices: 46.1 us -> 17 us  [shards(): owned = lax.psum(part, 'tensor')]
    reduce_scatter x0 -> x1, waiting for transfers between devices: none -> 25.7 us  [shards(): lax.psum_scatter(term.astype(jnp.bfloat16), 'layer', scatter_dimension=0,...]
    select_n x2 -> x0, other arithmetic: 19.7 us -> none  [join_pair(): return jnp.where(upper, high_first, low_first)]
    ppermute x4 -> x0, starting transfers between devices: 8.8 us -> none  [from_partner(): return lax.ppermute(value, axis, pairs)]
    convert_element_type x0 -> x2, local copies, waits for them, and re-layouts: none -> 6.53 us  [the longest x1 3.97 us: shards(): jnp.dot(all_rows, w_value, preferred_element_type=jnp.float32)]
    unnamed x36 -> x31, local copies, waits for them, and re-layouts: 12 us -> 17.6 us
  transfers between devices with their start and end apart: 5 -> 4, of which waited for: 3 -> 4; matrix products, arithmetic and copies ran while one was open for 8% -> 8% of each run, Pallas kernels for 0% -> 0%
where the time goes in v1:
time: 466 us; the launch traced here: 460 us
  waiting for transfers between devices  297 us (64%)
  matrix products  91.3 us (20%)
  local copies, waits for them, and re-layouts  46.2 us (10%)
  between operations  14.9 us (3%)
  other arithmetic  10.2 us (2%)
    all_gather x1, waiting for transfers between devices, shards(): stacked = lax.all_gather(stacked, 'micro', axis=1, tiled=True)  238 us
    reduce_scatter x1, waiting for transfers between devices, shards(): lax.psum_scatter(term.astype(jnp.bfloat16), 'layer', scatter_dimension=0,...  25.7 us
    dot_general x1, matrix products, local_layer(): jnp.einsum('bhqk,bqhd->bkhd', score_grad, query_b, preferred_element_type...  17.8 us
    unnamed x31, local copies, waits for them, and re-layouts  17.6 us
    psum x1, waiting for transfers between devices, shards(): owned = lax.psum(part, 'tensor')  17 us
    all_gather x1, waiting for transfers between devices, shards(): all_rows = lax.all_gather(vision_tokens, 'layer', axis=0, tiled=True)  16.3 us
    dot_general x2, matrix products, back_product(): lax.dot_general(grad_rows, weight, (((1,), (1,)), ((), ())), preferred_el...  12.3 us
    dot_general x1, matrix products, local_layer(): jnp.einsum('bi,bkhd->ikhd', onehot, vgrad_blk).reshape(-1, width)  10.6 us
  transfers between devices with their start and end apart: 4, of which 4 were waited for; matrix products, arithmetic and copies ran while one was open for 8% of the time, Pallas kernels for 0%

profile of v1, /device:TPU:0, one launch (start us, length us, event | category | flops | bytes accessed | tf_op | source)
XLA Modules:
  0.0 460.1 jit_solution(5753307346266345895)
XLA Ops:
  7.2 0.0 all-gather.5.cloned.1.call-start
  7.2 0.7 all-gather.5.cloned.1.call-update
  7.9 0.0 all-gather.3.cloned.1.call-start
  8.0 4.0 pad_maximum_fusion
  12.0 0.0 all-gather.3.cloned.1.call-update
  12.0 0.0 reduce-scatter.2.cloned.1.call-start
  12.1 0.6 dynamic_slice.8
  13.4 0.1 add.34
  13.5 0.1 add.35
  13.5 0.1 reshape.64
  13.6 0.1 max.12
  13.7 5.7 %copy.31 = bf16[128,8,16,128]{3,2,1,0:T(8,128)(2,1)} copy(bf16[128,8,16,128]{3,1,2,0:T(8,128)(2,1)} %bitcast.100) | data formatting | bytes 8388608
  19.4 1.7 fusion.19
  21.2 3.4 copy.32
  24.6 16.3 %all-gather.5.cloned.1.call-done = bf16[512,1664]{1,0:T(8,128)(2,1)} async-done(((bf16[256,1664]{1,0:T(8,128)(2,1)}), bf16[512,1664]{1,0:T(8,128)(2,1)}) %all-gather.5.cloned.1.call-update) | async-done | bytes 1703952 | tf_op jit(solution)/shard_map/all_gather | solution.py:84
  40.9 237.5 %all-gather.3.cloned.1.call-done = bf16[2,1664,2048]{2,1,0:T(8,128)(2,1)} async-done(((bf16[2,416,2048]{2,1,0:T(8,128)(2,1)}), bf16[2,1664,2048]{2,1,0:T(8,128)(2,1)}) %all-gather.3.cloned.1.call-update) | async-done | bytes 13631504 | tf_op jit(solution)/shard_map/all_gather | solution.py:77
  278.4 7.4 %fusion.35 = bf16[512,2048]{0,1:T(8,128)(2,1)S(1)} fusion(bf16[512,1664]{1,0:T(8,128)(2,1)} %all-gather.5.cloned.1.call-done, bf16[2,1664,2048]{2,1,0:T(8,128)(2,1)} %all-gather.3.cloned.1.call-done), kind=kOutput, calls=%fused_computation.46 | convolution fusion | flops 3490709504 | bytes 10616832 | tf_op jit(solution)/shard_map/dot_general | solution.py:85
  285.9 2.6 copy.14
  288.4 2.3 copy.30
  290.8 8.3 %fusion.34 = bf16[512,2048]{0,1:T(8,128)(2,1)} fusion(bf16[512,1664]{1,0:T(8,128)(2,1)S(1)} %copy-done.7, bf16[2,1664,2048]{2,1,0:T(8,128)(2,1)} %all-gather.3.cloned.1.call-done), kind=kOutput, calls=%fused_computation.45 | convolution fusion | flops 3490709504 | bytes 10616832 | tf_op jit(solution)/shard_map/dot_general | solution.py:86
  299.1 4.0 copy.13
  303.0 3.5 copy.29
  306.6 4.6 %gather_fusion = bf16[16,64,16,128]{3,2,1,0:T(8,128)(2,1)} fusion(bf16[8,64,16,128]{3,2,1,0:T(8,128)(2,1)} %bitcast.93, s32[1024]{0:T(1024)S(1)} %pad_clamp_fusion), kind=kCustom, calls=%fused_computation.clone | custom fusion | bytes 8388672 | tf_op jit(solution)/shard_map/jit(_take)/gather | solution.py:28
  311.2 3.1 gather_fusion.1
  314.3 4.4 broadcast_select_fusion
  318.7 0.0 copy-start
  318.7 0.2 copy-done.1
  318.9 5.0 %bitcast_reduce_fusion = (f32[16,16,64]{2,1,0:T(8,128)S(1)}, f32[16,16,64,64]{3,2,1,0:T(8,128)}) fusion(bf16[16,64,16,128]{3,2,1,0:T(8,128)(2,1)S(1)} %bitcast.95, bf16[16,64,16,128]{3,2,1,0:T(8,128)(2,1)S(1)} %get-tuple-element.5), kind=kOutput, calls=%fused_computation.8 | convolution fusion | flops 270516224 | bytes 12648448 | tf_op jit(solution)/shard_map/bqhd,bkhd->bhqk/dot_general | solution.py:33
  324.0 0.2 copy-done
  324.2 5.7 %fusion.25 = f32[16,16,64,64]{2,3,1,0:T(8,128)} fusion(bf16[16,64,16,128]{3,2,1,0:T(8,128)(2,1)S(1)} %bitcast.96, bf16[16,64,16,128]{3,2,1,0:T(8,128)(2,1)S(1)} %get-tuple-element.6), kind=kOutput, calls=%fused_computation.34 | convolution fusion | flops 268435456 | bytes 12582912 | tf_op jit(solution)/shard_map/bqhd,bkhd->bhqk/dot_general | solution.py:49
  329.9 7.9 %fusion.23 = bf16[16,16,128,64]{2,3,1,0:T(8,128)(2,1)} fusion(bf16[16,64,16,128]{3,2,1,0:T(8,128)(2,1)S(1)} %bitcast.97, f32[16,16,64,64]{3,2,1,0:T(8,128)} %get-tuple-element.8, f32[16]{0:T(128)S(1)} %reshape.64, f32[16,16,64]{2,1,0:T(8,128)S(1)} %get-tuple-element.7), kind=kOutput, calls=%fused_computation.32 | convolution fusion | flops 272629760 | bytes 12648512 | tf_op jit(solution)/shard_map/bhqk,bqhd->bkhd/dot_general | solution.py:46
  337.7 17.8 %fusion.16 = bf16[16,16,64,128]{3,2,1,0:T(8,128)(2,1)} fusion(f32[16,16,64,64]{2,3,1,0:T(8,128)} %fusion.25, bf16[16,64,16,128]{3,2,1,0:T(8,128)(2,1)} %bitcast.94, f32[16,16,64,64]{3,2,1,0:T(8,128)} %get-tuple-element.8, f32[16]{0:T(128)S(1)} %reshape.64, f32[16,16,64]{2,1,0:T(8,128)S(1)} %get-tuple-element.7), kind=kOutput, calls=%fused_computation.24 | convolution fusion | flops 279986240 | bytes 16842816 | tf_op jit(solution)/shard_map/bhqk,bqhd->bkhd/dot_general | solution.py:54
  355.6 10.6 %fusion.47 = bf16[8,64,16,128]{3,0,2,1:T(8,128)(2,1)S(1)} fusion(bf16[16,16,128,64]{2,3,1,0:T(8,128)(2,1)} %fusion.23, s32[16]{0:T(128)S(1)} %get-tuple-element.4), kind=kOutput, calls=%fused_computation.54 | convolution fusion | flops 33554560 | bytes 6291520 | tf_op jit(solution)/shard_map/bi,bkhd->ikhd/dot_general | solution.py:62
  366.2 8.4 %fusion.44 = bf16[8,64,16,128]{3,0,2,1:T(8,128)(2,1)S(1)} fusion(bf16[16,16,64,128]{3,2,1,0:T(8,128)(2,1)S(1)} %copy-done.4, s32[16]{0:T(128)S(1)} %get-tuple-element.4), kind=kOutput, calls=%fused_computation.53 | convolution fusion | flops 33554560 | bytes 6291520 | tf_op jit(solution)/shard_map/bi,bkhd->ikhd/dot_general | solution.py:59
  374.6 0.3 copy.23
  374.9 0.0 slice-start
  374.9 0.3 copy.24
  375.2 7.1 %fusion.9 = f32[512,1664]{1,0:T(8,128)S(1)} fusion(bf16[2,1664,2048]{2,1,0:T(8,128)(2,1)} %all-gather.3.cloned.1.call-done, bf16[64,8,16,128]{3,2,1,0:T(8,128)(2,1)S(1)} %bitcast.102), kind=kOutput, calls=%fused_computation.20 | convolution fusion | flops 3489660928 | bytes 12320768 | tf_op jit(solution)/shard_map/dot_general | solution.py:68
  382.4 5.2 %add_convert_fusion = bf16[512,1664]{1,0:T(8,128)(2,1)} fusion(f32[512,1664]{1,0:T(8,128)S(1)} %fusion.9, bf16[2,1664,2048]{2,1,0:T(8,128)(2,1)S(1)} %bitcast.106, bf16[64,8,16,128]{3,2,1,0:T(8,128)(2,1)S(1)} %bitcast.101), kind=kOutput, calls=%fused_computation.42 | convolution fusion | flops 3491364864 | bytes 14024704 | tf_op jit(solution)/shard_map/dot_general | solution.py:68
  387.6 0.0 reduce-scatter.2.cloned.1.call-update
  387.6 0.3 all-reduce.2.cloned.1.call-start
  387.9 25.7 %reduce-scatter.2.cloned.1.call-done = bf16[256,1664]{1,0:T(8,128)(2,1)} async-done(((bf16[512,1664]{1,0:T(8,128)(2,1)}), bf16[256,1664]{1,0:T(8,128)(2,1)}) %reduce-scatter.2.cloned.1.call-update) | async-done | bytes 851984 | tf_op jit(solution)/shard_map/reduce_scatter | solution.py:91
  413.5 0.0 all-reduce.2.cloned.1.call-update
  413.6 7.8 %fusion.18 = bf16[16,64,16,128]{3,1,2,0:T(8,128)(2,1)S(1)} fusion(f32[]{:T(128)} %bitcast, bf16[16,64,16,128]{3,2,1,0:T(8,128)(2,1)} %copy-done, f32[16,16,64,64]{3,2,1,0:T(8,128)} %get-tuple-element.8, f32[16]{0:T(128)S(1)} %reshape.64, f32[16,16,64]{2,1,0:T(8,128)S(1)} %get-tuple-element.7), kind=kOutput, calls=%fused_computation.25 | convolution fusion | flops 276824064 | bytes 12648516 | tf_op jit(solution)/shard_map/bhqk,bkhd->bqhd/dot_general | solution.py:38
  421.4 5.5 %copy.20 = bf16[16,64,16,128]{3,2,1,0:T(8,128)(2,1)} copy(bf16[16,64,16,128]{3,1,2,0:T(8,128)(2,1)S(1)} %fusion.18) | data formatting | bytes 8388608 | tf_op jit(solution)/shard_map/convert_element_type | solution.py:40
  426.9 7.3 %broadcast_in_dim_reshape.4 = bf16[1,1024,2048]{2,1,0:T(8,128)(2,1)} reshape(bf16[16,64,16,128]{3,2,1,0:T(8,128)(2,1)} %copy.20) | data formatting | bytes 8388608 | tf_op jit(solution)/shard_map/broadcast_in_dim;reshape | solution.py:93
  434.2 17.0 %all-reduce.2.cloned.1.call-done = bf16[256,1664]{1,0:T(8,128)(2,1)} async-done(((bf16[256,1664]{1,0:T(8,128)(2,1)}), bf16[256,1664]{1,0:T(8,128)(2,1)}) %all-reduce.2.cloned.1.call-update) | async-done | bytes 851984 | tf_op jit(solution)/shard_map/psum | solution.py:92
  451.3 2.1 copy.76
  (29 shorter events, 0.1 us)
Async XLA Ops:
  7.2 33.8 %all-gather.5.cloned.1.call-start = ((), (), s32[]{:S(2)}) async-start(), calls=%async_computation.2 | async-start | bytes 2555904 | tf_op jit(solution)/shard_map/all_gather | solution.py:84
  7.9 270.5 %all-gather.3.cloned.1.call-start = ((), (), s32[]{:S(2)}) async-start(), calls=%async_computation.1 | async-start | bytes 17039360 | tf_op jit(solution)/shard_map/all_gather | solution.py:77
  7.9 4.1 copy-start.8
  8.0 5.6 %copy-start.6 = (s32[4,4,4]{2,1,0:T(4,128)S(1)}, s32[4,4,4]{2,1,0:T(4,128)}, u32[]{:S(2)}) copy-start(s32[4,4,4]{2,1,0:T(4,128)} %param.14) | copy-start | bytes 772
  12.0 401.5 %reduce-scatter.2.cloned.1.call-start = ((), (), s32[]{:S(2)}) async-start(), calls=%async_computation.3 | async-start | bytes 2555904 | tf_op jit(solution)/shard_map/reduce_scatter | solution.py:91
  13.7 5.7 %copy-start.5 = (bf16[1,1024,2048]{2,1,0:T(8,128)(2,1)S(1)}, bf16[1,1024,2048]{2,1,0:T(8,128)(2,1)}, u32[]{:S(2)}) copy-start(bf16[1,1024,2048]{2,1,0:T(8,128)(2,1)} %param.15) | copy-start | bytes 12582916
  288.4 2.3 copy-start.7
  314.3 4.6 %copy-start.1 = (bf16[128,8,16,128]{3,2,1,0:T(8,128)(2,1)S(1)}, bf16[128,8,16,128]{3,2,1,0:T(8,128)(2,1)}, u32[]{:S(2)}) copy-start(bf16[128,8,16,128]{3,2,1,0:T(8,128)(2,1)} %copy.31) | copy-start | bytes 12582916
  318.7 5.5 %copy-start = (bf16[16,64,16,128]{3,2,1,0:T(8,128)(2,1)}, bf16[16,64,16,128]{3,2,1,0:T(8,128)(2,1)S(1)}, u32[]{:S(2)}) copy-start(bf16[16,64,16,128]{3,2,1,0:T(8,128)(2,1)S(1)} %get-tuple-element.6) | copy-start | bytes 12582916
  318.9 5.2 %copy-start.2 = (bf16[128,8,16,128]{3,2,1,0:T(8,128)(2,1)S(1)}, bf16[128,8,16,128]{3,2,1,0:T(8,128)(2,1)}, u32[]{:S(2)}) copy-start(bf16[128,8,16,128]{3,2,1,0:T(8,128)(2,1)} %copy.32) | copy-start | bytes 12582916
  324.2 5.7 %copy-start.3 = (bf16[128,8,16,128]{3,2,1,0:T(8,128)(2,1)S(1)}, bf16[128,8,16,128]{3,2,1,0:T(8,128)(2,1)}, u32[]{:S(2)}) copy-start(bf16[128,8,16,128]{3,2,1,0:T(8,128)(2,1)} %copy.32) | copy-start | bytes 12582916
  355.5 10.6 %copy-start.4 = (bf16[16,16,64,128]{3,2,1,0:T(8,128)(2,1)S(1)}, bf16[16,16,64,128]{3,2,1,0:T(8,128)(2,1)}, u32[]{:S(2)}) copy-start(bf16[16,16,64,128]{3,2,1,0:T(8,128)(2,1)} %fusion.16) | copy-start | bytes 12582916
  374.9 7.4 %slice-start = ((s8[13631488]{0:T(1024)(128)(4,1)}), s8[4194304]{0:T(1024)(128)(4,1)S(1)}, s32[]{:S(2)}) async-start(s8[13631488]{0:T(1024)(128)(4,1)} %bitcast.105), calls=%async_computation.5 | async-start | bytes 8388608
  375.2 7.1 %slice-start.1 = ((s8[13631488]{0:T(1024)(128)(4,1)}), s8[4194304]{0:T(1024)(128)(4,1)S(1)}, s32[]{:S(2)}) async-start(s8[13631488]{0:T(1024)(128)(4,1)} %bitcast.105), calls=%async_computation.6 | async-start | bytes 8388608
  375.2 7.1 %slice-start.2 = ((s8[13631488]{0:T(1024)(128)(4,1)}), s8[4194304]{0:T(1024)(128)(4,1)S(1)}, s32[]{:S(2)}) async-start(s8[13631488]{0:T(1024)(128)(4,1)} %bitcast.105), calls=%async_computation.7 | async-start | bytes 8388608
  375.2 7.1 %slice-start.3 = ((s8[13631488]{0:T(1024)(128)(4,1)}), s8[1048576]{0:T(1024)(128)(4,1)S(1)}, s32[]{:S(2)}) async-start(s8[13631488]{0:T(1024)(128)(4,1)} %bitcast.105), calls=%async_computation.8 | async-start | bytes 2097152
  387.6 63.6 %all-reduce.2.cloned.1.call-start = ((), (), s32[]{:S(2)}) async-start(), calls=%async_computation.4 | async-start | bytes 1703936 | tf_op jit(solution)/shard_map/psum | solution.py:92
Sparse Core Ops, SparseCore 0:
  9.5 31.3 all-gather.4
  43.1 235.3 all-gather.2
  387.7 25.7 reduce-scatter.1
  415.8 35.4 all-reduce.1

commit v2 on v1

--- a/solution.py
+++ b/solution.py
@@ -10,6 +10,9 @@
 TBLOCK = 64
 IMGS = 2
 MICRO = 4
+CHUNKS = 4
+AHEAD = 4
+RELAY = False
 
 
 def block_index(visible):
@@ -73,21 +76,71 @@
 def shards(vision_tokens, key_weight, value_weight, queries, gate, visible, out_grad):
     layer = lax.axis_index("layer")
     micro = lax.axis_index("micro")
-    stacked = jnp.stack([key_weight, value_weight])
-    stacked = lax.all_gather(stacked, "micro", axis=1, tiled=True)
-    w_key = stacked[0]
-    w_value = stacked[1]
-    width = w_key.shape[1]
+    width = key_weight.shape[1]
     heads = width // HD
+    chunks = min(CHUNKS, heads)
+    step = width // chunks
     gate_value = lax.dynamic_index_in_dim(gate, layer, 0, keepdims=False)
     own_visible = lax.dynamic_index_in_dim(visible, micro, 0, keepdims=False)
     all_rows = lax.all_gather(vision_tokens, "layer", axis=0, tiled=True)
-    key_rows = jnp.dot(all_rows, w_key, preferred_element_type=jnp.float32).astype(jnp.bfloat16)
-    value_rows = jnp.dot(all_rows, w_value, preferred_element_type=jnp.float32).astype(jnp.bfloat16)
-    attended, key_grad, value_grad = local_layer(
-        key_rows, value_rows, queries[0], gate_value, out_grad[0], own_visible, heads
-    )
-    term = back_product(key_grad, w_key) + back_product(value_grad, w_value)
+    term = None
+    pieces = []
+    gathered = {}
+
+    micros = lax.axis_size("micro")
+
+    def line_gather(own):
+        ups, downs = [], []
+        up, down = own, own
+        for r in range(1, micros):
+            up = lax.ppermute(up, "micro", [(i, i + 1) for i in range(r - 1, micros - 1)])
+            down = lax.ppermute(down, "micro", [(i + 1, i) for i in range(r - 1, micros - 1)])
+            ups.append(up)
+            downs.append(down)
+        blocks = []
+        for q in range(micros):
+            which = jnp.where(q == micro, 0, jnp.where(q < micro, micro - q, micros - 1 + q - micro))
+            blocks.append(lax.select_n(which, own, *ups, *downs))
+        return jnp.concatenate(blocks, axis=1)
+
+    def fetch(j, after):
+        cols = slice(j * step, (j + 1) * step)
+        stacked = jnp.stack([key_weight[:, cols], value_weight[:, cols]])
+        if after is not None:
+            stacked, _ = lax.optimization_barrier((stacked, after))
+        if RELAY:
+            gathered[j] = line_gather(stacked)
+        else:
+            gathered[j] = lax.all_gather(stacked, "micro", axis=1, tiled=True)
+
+    for j in range(min(AHEAD, chunks)):
+        fetch(j, None)
+    for j in range(chunks):
+        cols = slice(j * step, (j + 1) * step)
+        stacked = gathered.pop(j)
+        if term is not None:
+            stacked, _ = lax.optimization_barrier((stacked, term))
+        w_key = stacked[0]
+        w_value = stacked[1]
+        key_rows = jnp.dot(all_rows, w_key, preferred_element_type=jnp.float32).astype(jnp.bfloat16)
+        value_rows = jnp.dot(all_rows, w_value, preferred_element_type=jnp.float32).astype(
+            jnp.bfloat16
+        )
+        attended, key_grad, value_grad = local_layer(
+            key_rows,
+            value_rows,
+            queries[0, :, cols],
+            gate_value,
+            out_grad[0, :, cols],
+            own_visible,
+            step // HD,
+        )
+        pieces.append(attended)
+        part = back_product(key_grad, w_key) + back_product(value_grad, w_value)
+        term = part if term is None else term + part
+        if j + AHEAD < chunks:
+            fetch(j + AHEAD, term)
+    attended = jnp.concatenate(pieces, axis=1)
     part = lax.psum_scatter(term.astype(jnp.bfloat16), "layer", scatter_dimension=0, tiled=True)
     owned = lax.psum(part, "tensor")
     return (attended[None], owned)

time: 466 us -> 437 us (0.938)
  waiting for transfers between devices: 297 us -> 225 us
  local copies, waits for them, and re-layouts: 46.2 us -> 79.2 us
  matrix products: 91.3 us -> 102 us
    all_gather x1 -> x4, waiting for transfers between devices: 238 us -> 174 us  [fetch(): gathered[j] = lax.all_gather(stacked, 'micro', axis=1, tiled=True)]
    reshape x0 -> x16, local copies, waits for them, and re-layouts: none -> 25.7 us  [the longest x8 13 us: local_layer(): key_rows.reshape(images, IMG_TOK, heads, HD)]
    all_gather x1, waiting for transfers between devices: 16.3 us -> 2.14 us  [shards(): all_rows = lax.all_gather(vision_tokens, 'layer', axis=0, tiled=True)]
    psum x1, waiting for transfers between devices: 17 us -> 28.6 us  [shards(): owned = lax.psum(part, 'tensor')]
    unnamed x31 -> x71, local copies, waits for them, and re-layouts: 17.6 us -> 9.68 us
    dot_general x1 -> x4, matrix products: 10.6 us -> 3.06 us  [local_layer(): jnp.einsum('bi,bkhd->ikhd', onehot, vgrad_blk).reshape(-1, width)]
    dot_general x1 -> x4, matrix products: 7.43 us -> 14.6 us  [shards(): jnp.dot(all_rows, w_key, preferred_element_type=jnp.float32)]
    reduce_scatter x1, waiting for transfers between devices: 25.7 us -> 19 us  [shards(): lax.psum_scatter(term.astype(jnp.bfloat16), 'layer', scatter_dimension=0,...]
  transfers between devices with their start and end apart: 4 -> 7, of which waited for: 4 -> 7; matrix products, arithmetic and copies ran while one was open for 8% -> 32% of each run, Pallas kernels for 0% -> 0%
where the time goes in v2:
time: 437 us; the launch traced here: 433 us
  waiting for transfers between devices  225 us (51%)
  matrix products  102 us (23%)
  local copies, waits for them, and re-layouts  79.2 us (18%)
  between operations  15.7 us (4%)
  other arithmetic  10.7 us (2%)
    all_gather x4, waiting for transfers between devices, fetch(): gathered[j] = lax.all_gather(stacked, 'micro', axis=1, tiled=True)  174 us
    psum x1, waiting for transfers between devices, shards(): owned = lax.psum(part, 'tensor')  28.6 us
    dot_general x4, matrix products, local_layer(): jnp.einsum('bhqk,bqhd->bkhd', score_grad, query_b, preferred_element_type...  22.8 us
    reduce_scatter x1, waiting for transfers between devices, shards(): lax.psum_scatter(term.astype(jnp.bfloat16), 'layer', scatter_dimension=0,...  19 us
    dot_general x8, matrix products, back_product(): lax.dot_general(grad_rows, weight, (((1,), (1,)), ((), ())), preferred_el...  18.7 us
    dot_general x4, matrix products, shards(): jnp.dot(all_rows, w_key, preferred_element_type=jnp.float32)  14.6 us
    reshape x8, local copies, waits for them, and re-layouts, local_layer(): key_rows.reshape(images, IMG_TOK, heads, HD)  13 us
    reshape x8, local copies, waits for them, and re-layouts, local_layer(): value_rows.reshape(images, IMG_TOK, heads, HD)  12.7 us
  transfers between devices with their start and end apart: 7, of which 7 were waited for; matrix products, arithmetic and copies ran while one was open for 32% of the time, Pallas kernels for 0%

profile of v2, /device:TPU:0, one launch (start us, length us, event | category | flops | bytes accessed | tf_op | source)
XLA Modules:
  0.0 433.1 jit_solution(7696014269345954943)
XLA Ops:
  7.9 2.2 slice_bitcast_fusion.16
  14.7 3.9 fusion.281
  21.0 4.4 %multiply_convert_fusion.1 = (bf16[1,1024,512]{2,1,0:T(8,128)(2,1)S(1)}, bf16[1,1024,512]{2,1,0:T(8,128)(2,1)}, bf16[1,1024,512]{2,1,0:T(8,128)(2,1)}, bf16[1,1024,512]{2,1,0:T(8,128)(2,1)}) fusion(bf16[1,1024,2048]{2,1,0:T(8,128)(2,1)} %param.15, f32[]{:T(128)} %bitcast), kind=kLoop, calls=%fused_computation.56 | loop fusion | flops 6291456 | bytes 8388612 | tf_op jit(solution)/shard_map/convert_element_type | solution.py:46
  26.8 2.2 reshape_squeeze.13
  28.9 2.2 convert_element_type.238
  31.1 2.1 reshape_squeeze.14
  33.2 2.1 convert_element_type.253
  35.4 2.1 reshape_squeeze.15
  38.8 2.1 all-gather.8.cloned.1.call-done
  40.9 69.4 %all-gather.6.cloned.1.call-done = bf16[2,1664,512]{2,1,0:T(8,128)(2,1)} async-done(((bf16[2,416,512]{2,1,0:T(8,128)(2,1)}), bf16[2,1664,512]{2,1,0:T(8,128)(2,1)}) %all-gather.6.cloned.1.call-update) | async-done | bytes 3407888 | tf_op jit(solution)/shard_map/all_gather | solution.py:114
  110.3 3.2 fusion.159
  127.3 5.2 %fusion.45 = bf16[16,4,64,128]{3,2,1,0:T(8,128)(2,1)S(1)} fusion(f32[16,4,64,64]{2,3,1,0:T(8,128)} %fusion.196, bf16[16,64,4,128]{3,2,1,0:T(4,128)(2,1)} %reshape_squeeze.12, f32[16,4,64,64]{3,2,1,0:T(8,128)} %copy-done.27, f32[16]{0:T(128)S(1)} %reshape.146, f32[16,4,64]{2,1,0:T(4,128)S(1)} %get-tuple-element.27), kind=kOutput, calls=%fused_computation.77 | convolution fusion | flops 69996608 | bytes 4210752 | tf_op jit(solution)/shard_map/bhqk,bqhd->bkhd/dot_general | solution.py:57
  133.4 2.8 fusion.78
  137.4 40.9 %all-gather.10.cloned.1.call-done = bf16[2,1664,512]{2,1,0:T(8,128)(2,1)} async-done(((bf16[2,416,512]{2,1,0:T(8,128)(2,1)}), bf16[2,1664,512]{2,1,0:T(8,128)(2,1)}) %all-gather.10.cloned.1.call-update) | async-done | bytes 3407888 | tf_op jit(solution)/shard_map/all_gather | solution.py:114
  178.3 4.4 %fusion.152 = bf16[512,512]{0,1:T(8,128)(2,1)} fusion(bf16[512,1664]{1,0:T(8,128)(2,1)} %all-gather.8.cloned.1.call-done, bf16[2,1664,512]{2,1,0:T(8,128)(2,1)} %all-gather.10.cloned.1.call-done), kind=kOutput, calls=%fused_computation.143 | convolution fusion | flops 872677376 | bytes 3932160 | tf_op jit(solution)/shard_map/dot_general | solution.py:125
  182.6 2.4 reshape.239
  185.0 2.8 copy.31
  187.8 2.8 gather_fusion.3
  190.5 3.9 fusion.155
  194.5 2.4 reshape.238
  196.8 2.7 copy.29
  199.6 2.7 gather_fusion.2
  202.3 2.5 bitcast_reduce_fusion.2
  209.3 6.2 %fusion.48 = bf16[16,4,64,128]{3,2,1,0:T(8,128)(2,1)} fusion(f32[16,4,64,64]{2,3,1,0:T(8,128)} %fusion.190, bf16[16,64,4,128]{3,2,1,0:T(4,128)(2,1)} %reshape_squeeze.13, f32[16,4,64,64]{3,2,1,0:T(8,128)} %copy-done.28, f32[16,4,64]{2,1,0:T(4,128)S(1)} %get-tuple-element.29, f32[16]{0:T(128)S(1)} %reshape.146), kind=kOutput, calls=%fused_computation.78 | convolution fusion | flops 69996608 | bytes 4210752 | tf_op jit(solution)/shard_map/bhqk,bqhd->bkhd/dot_general | solution.py:57
  217.7 2.8 fusion.70
  220.5 2.9 add_add_fusion.1
  223.4 22.7 %all-gather.12.cloned.1.call-done = bf16[2,1664,512]{2,1,0:T(8,128)(2,1)} async-done(((bf16[2,416,512]{2,1,0:T(8,128)(2,1)}), bf16[2,1664,512]{2,1,0:T(8,128)(2,1)}) %all-gather.12.cloned.1.call-update) | async-done | bytes 3407888 | tf_op jit(solution)/shard_map/all_gather | solution.py:114
  246.1 3.1 fusion.146
  263.0 5.2 %fusion.51 = bf16[16,4,64,128]{3,2,1,0:T(8,128)(2,1)S(1)} fusion(f32[16,4,64,64]{2,3,1,0:T(8,128)} %fusion.184, bf16[16,64,4,128]{3,2,1,0:T(4,128)(2,1)} %reshape_squeeze.14, f32[16,4,64,64]{3,2,1,0:T(8,128)} %copy-done.29, f32[16,4,64]{2,1,0:T(4,128)S(1)} %get-tuple-element.31, f32[16]{0:T(128)S(1)} %reshape.146), kind=kOutput, calls=%fused_computation.79 | convolution fusion | flops 69996608 | bytes 4210752 | tf_op jit(solution)/shard_map/bhqk,bqhd->bkhd/dot_general | solution.py:57
  269.1 2.8 fusion.63
  273.2 41.3 %all-gather.14.cloned.1.call-done = bf16[2,1664,512]{2,1,0:T(8,128)(2,1)} async-done(((bf16[2,416,512]{2,1,0:T(8,128)(2,1)}), bf16[2,1664,512]{2,1,0:T(8,128)(2,1)}) %all-gather.14.cloned.1.call-update) | async-done | bytes 3407888 | tf_op jit(solution)/shard_map/all_gather | solution.py:114
  314.5 3.9 fusion.140
  318.4 2.6 reshape.243
  321.0 2.7 copy.53
  323.6 2.7 gather_fusion.7
  326.3 2.4 bitcast_reduce_fusion
  334.7 2.4 reshape.242
  337.1 2.7 copy.51
  339.7 2.7 gather_fusion.6
  342.4 3.7 fusion.178
  346.1 6.2 %fusion.54 = bf16[16,4,64,128]{3,2,1,0:T(8,128)(2,1)} fusion(f32[16,4,64,64]{2,3,1,0:T(8,128)} %fusion.178, bf16[16,64,4,128]{3,2,1,0:T(4,128)(2,1)} %reshape_squeeze.15, f32[16,4,64,64]{3,2,1,0:T(8,128)} %copy-done.31, f32[16,4,64]{2,1,0:T(4,128)S(1)} %get-tuple-element.33, f32[16]{0:T(128)S(1)} %reshape.146), kind=kOutput, calls=%fused_computation.80 | convolution fusion | flops 69996608 | bytes 4210752 | tf_op jit(solution)/shard_map/bhqk,bqhd->bkhd/dot_general | solution.py:57
  354.5 2.8 fusion.56
  357.3 2.3 add_convert_fusion
  360.0 2.9 fusion.93
  367.1 19.0 %reduce-scatter.2.cloned.1.call-done = bf16[256,1664]{1,0:T(8,128)(2,1)} async-done(((bf16[512,1664]{1,0:T(8,128)(2,1)}), bf16[256,1664]{1,0:T(8,128)(2,1)}) %reduce-scatter.2.cloned.1.call-update) | async-done | bytes 851984 | tf_op jit(solution)/shard_map/reduce_scatter | solution.py:144
  386.1 2.4 fusion.92
  393.0 2.3 maximum_bitcast_fusion
  395.3 28.6 %all-reduce.2.cloned.1.call-done = bf16[256,1664]{1,0:T(8,128)(2,1)} async-done(((bf16[256,1664]{1,0:T(8,128)(2,1)}), bf16[256,1664]{1,0:T(8,128)(2,1)}) %all-reduce.2.cloned.1.call-update) | async-done | bytes 851984 | tf_op jit(solution)/shard_map/psum | solution.py:145
  (151 shorter events, 67.0 us)
Async XLA Ops:
  7.2 33.8 %all-gather.8.cloned.1.call-start = ((), (), s32[]{:S(2)}) async-start(), calls=%async_computation.2 | async-start | bytes 2555904 | tf_op jit(solution)/shard_map/all_gather | solution.py:85
  7.9 102.4 %all-gather.6.cloned.1.call-start = ((), (), s32[]{:S(2)}) async-start(), calls=%async_computation.1 | async-start | bytes 4259840 | tf_op jit(solution)/shard_map/all_gather | solution.py:114
  11.1 167.2 %all-gather.10.cloned.1.call-start = ((), (), s32[]{:S(2)}) async-start(), calls=%async_computation.3 | async-start | bytes 4259840 | tf_op jit(solution)/shard_map/all_gather | solution.py:114
  12.1 234.0 %all-gather.12.cloned.1.call-start = ((), (), s32[]{:S(2)}) async-start(), calls=%async_computation.4 | async-start | bytes 4259840 | tf_op jit(solution)/shard_map/all_gather | solution.py:114
  13.2 1.1 copy-start.22
  13.2 301.3 %all-gather.14.cloned.1.call-start = ((), (), s32[]{:S(2)}) async-start(), calls=%async_computation.5 | async-start | bytes 4259840 | tf_op jit(solution)/shard_map/all_gather | solution.py:114
  14.3 371.8 %reduce-scatter.2.cloned.1.call-start = ((), (), s32[]{:S(2)}) async-start(), calls=%async_computation.6 | async-start | bytes 2555904 | tf_op jit(solution)/shard_map/reduce_scatter | solution.py:144
  18.6 1.2 copy-start.26
  117.5 1.3 copy-start.27
  118.9 2.4 copy-start.15
  119.6 2.3 copy-start.23
  125.2 2.1 copy-start.1
  133.4 2.8 copy-start.16
  133.4 2.8 copy-start.18
  202.3 2.5 copy-start.3
  202.3 2.5 copy-start.9
  204.8 2.1 copy-start.28
  217.7 2.8 copy-start.12
  217.7 2.8 copy-start.19
  251.3 3.5 copy-start.8
  253.4 1.4 copy-start.29
  254.8 2.6 copy-start.10
  255.5 2.2 copy-start.24
  260.9 2.1 copy-start.4
  268.2 3.8 copy-start.11
  269.1 2.9 copy-start
  269.1 2.9 copy-start.17
  326.3 3.7 copy-start.7
  328.7 1.3 copy-start.31
  330.1 2.4 copy-start.13
  330.8 2.0 copy-start.25
  354.5 2.8 copy-start.14
  354.5 2.8 copy-start.20
  359.7 3.2 copy-start.5
  359.7 64.2 %all-reduce.2.cloned.1.call-start = ((), (), s32[]{:S(2)}) async-start(), calls=%async_computation.7 | async-start | bytes 1703936 | tf_op jit(solution)/shard_map/psum | solution.py:145
  360.0 2.9 copy-start.30
  362.9 1.2 copy-start.6
  362.9 2.3 copy-start.32
  365.2 20.8 %copy-start.2 = (bf16[16,64,4,128]{3,1,2,0:T(8,128)(2,1)S(1)}, bf16[16,64,4,128]{3,1,2,0:T(8,128)(2,1)}, u32[]{:S(2)}) copy-start(bf16[16,64,4,128]{3,1,2,0:T(8,128)(2,1)} %copy-done.1) | copy-start | bytes 3145732
  389.6 1.2 copy-start.21
Sparse Core Ops, SparseCore 0:
  9.5 31.3 all-gather.7
  42.5 67.7 all-gather.5
  111.9 66.3 all-gather.9
  179.7 66.3 all-gather.11
  248.1 66.3 all-gather.13
  359.8 26.1 reduce-scatter.1
  388.4 35.4 all-reduce.1

commit v3 on v2

--- a/solution.py
+++ b/solution.py
@@ -73,6 +73,32 @@
     )
 
 
+def exchange(value, axis, swap):
+    return lax.ppermute(value.astype(jnp.bfloat16), axis, swap).astype(jnp.float32)
+
+
+def chip_reduce(term, layer, swap):
+    core = lax.axis_index("core")
+    quarter = term.shape[0] // 4
+    rows = term.reshape(4, quarter, term.shape[1])
+    even = rows[0::2]
+    odd = rows[1::2]
+    keep = jnp.where(core == 0, even, odd)
+    give = jnp.where(core == 0, odd, even)
+    halves = keep + exchange(give, "core", swap)
+    mine = jnp.where(layer == 0, halves[0], halves[1])
+    other = jnp.where(layer == 0, halves[1], halves[0])
+    summed = mine + exchange(other, "layer", swap)
+    rounded = summed.astype(jnp.bfloat16).astype(jnp.float32)
+    total = (rounded + exchange(summed, "tx", swap)).astype(jnp.bfloat16)
+    partner = lax.ppermute(total, "core", swap)
+    return jnp.where(
+        core == 0,
+        jnp.concatenate([total, partner], axis=0),
+        jnp.concatenate([partner, total], axis=0),
+    )
+
+
 def shards(vision_tokens, key_weight, value_weight, queries, gate, visible, out_grad):
     layer = lax.axis_index("layer")
     micro = lax.axis_index("micro")
@@ -82,7 +108,17 @@
     step = width // chunks
     gate_value = lax.dynamic_index_in_dim(gate, layer, 0, keepdims=False)
     own_visible = lax.dynamic_index_in_dim(visible, micro, 0, keepdims=False)
-    all_rows = lax.all_gather(vision_tokens, "layer", axis=0, tiled=True)
+    swap = [(0, 1), (1, 0)]
+    paired = lax.axis_size("layer") == 2
+    if paired:
+        partner = lax.ppermute(vision_tokens, "layer", swap)
+        all_rows = jnp.where(
+            layer == 0,
+            jnp.concatenate([vision_tokens, partner], axis=0),
+            jnp.concatenate([partner, vision_tokens], axis=0),
+        )
+    else:
+        all_rows = lax.all_gather(vision_tokens, "layer", axis=0, tiled=True)
     term = None
     pieces = []
     gathered = {}
@@ -141,31 +177,37 @@
         if j + AHEAD < chunks:
             fetch(j + AHEAD, term)
     attended = jnp.concatenate(pieces, axis=1)
-    part = lax.psum_scatter(term.astype(jnp.bfloat16), "layer", scatter_dimension=0, tiled=True)
-    owned = lax.psum(part, "tensor")
+    if paired and lax.axis_size("tx") == 2 and lax.axis_size("core") == 2:
+        owned = chip_reduce(term, layer, swap)
+    else:
+        part = lax.psum_scatter(
+            term.astype(jnp.bfloat16), "layer", scatter_dimension=0, tiled=True
+        )
+        owned = lax.psum(part, ("tx", "core"))
     return (attended[None], owned)
 
 
 def solution(mesh):
     sections, tensors = mesh.devices.shape
     grid = Mesh(
-        np.asarray(mesh.devices).reshape(MICRO, sections // MICRO, tensors),
-        ("micro", "layer", "tensor"),
+        np.asarray(mesh.devices).reshape(MICRO, sections // MICRO, tensors // 2, 2),
+        ("micro", "layer", "tx", "core"),
     )
     rows = ("micro", "layer")
+    cols = ("tx", "core")
     placed = (
         P(rows, None),
-        P(rows, "tensor"),
-        P(rows, "tensor"),
-        P(rows, None, "tensor"),
+        P(rows, cols),
+        P(rows, cols),
+        P(rows, None, cols),
         P(),
         P(),
-        P(rows, None, "tensor"),
+        P(rows, None, cols),
     )
     return jax.shard_map(
         shards,
         mesh=grid,
         in_specs=placed,
-        out_specs=(P(rows, None, "tensor"), P(rows, None)),
+        out_specs=(P(rows, None, cols), P(rows, None)),
         check_vma=False,
     )

time: 437 us -> 375 us (0.86)
  waiting for transfers between devices: 225 us -> 165 us
  local copies, waits for them, and re-layouts: 79.2 us -> 65.3 us
  starting transfers between devices: 0.54 us -> 6.43 us
    psum x1 -> x0, waiting for transfers between devices: 28.6 us -> none  [shards(): owned = lax.psum(part, 'tensor')]
    all_gather x4, waiting for transfers between devices: 174 us -> 146 us  [fetch(): gathered[j] = lax.all_gather(stacked, 'micro', axis=1, tiled=True)]
    reduce_scatter x1 -> x0, waiting for transfers between devices: 19 us -> none  [shards(): lax.psum_scatter(term.astype(jnp.bfloat16), 'layer', scatter_dimension=0,...]
    ppermute x0 -> x5, waiting for transfers between devices: none -> 18.6 us  [the longest x3 18.6 us: exchange(): lax.ppermute(value.astype(jnp.bfloat16), axis, swap).astype(jnp.float32)]
    ppermute x0 -> x5, starting transfers between devices: none -> 6.27 us  [the longest x3 3.13 us: exchange(): lax.ppermute(value.astype(jnp.bfloat16), axis, swap).astype(jnp.float32)]
    dot_general x4, matrix products: 8.21 us -> 14.2 us  [shards(): jnp.dot(all_rows, w_value, preferred_element_type=jnp.float32)]
    unnamed x71 -> x68, local copies, waits for them, and re-layouts: 9.68 us -> 4.26 us
    reshape x8, local copies, waits for them, and re-layouts: 13 us -> 8.39 us  [local_layer(): key_rows.reshape(images, IMG_TOK, heads, HD)]
  transfers between devices with their start and end apart: 7 -> 9, of which waited for: 7 -> 7; matrix products, arithmetic and copies ran while one was open for 32% -> 36% of each run, Pallas kernels for 0% -> 0%
where the time goes in v3:
time: 375 us; the launch traced here: 371 us
  waiting for transfers between devices  165 us (44%)
  matrix products  106 us (28%)
  local copies, waits for them, and re-layouts  65.3 us (17%)
  between operations  15.7 us (4%)
  other arithmetic  12.5 us (3%)
  starting transfers between devices  6.43 us (2%)
    all_gather x4, waiting for transfers between devices, fetch(): gathered[j] = lax.all_gather(stacked, 'micro', axis=1, tiled=True)  146 us
    dot_general x4, matrix products, local_layer(): jnp.einsum('bhqk,bqhd->bkhd', score_grad, query_b, preferred_element_type...  22.6 us
    ppermute x3, waiting for transfers between devices, exchange(): lax.ppermute(value.astype(jnp.bfloat16), axis, swap).astype(jnp.float32)  18.6 us
    dot_general x8, matrix products, back_product(): lax.dot_general(grad_rows, weight, (((1,), (1,)), ((), ())), preferred_el...  17.7 us
    dot_general x4, matrix products, shards(): jnp.dot(all_rows, w_key, preferred_element_type=jnp.float32)  16.1 us
    dot_general x4, matrix products, shards(): jnp.dot(all_rows, w_value, preferred_element_type=jnp.float32)  14.2 us
    dot_general x4, matrix products, local_layer(): jnp.einsum('bqhd,bkhd->bhqk', head_grad, val_img, preferred_element_type=...  11.6 us
    dot_general x4, matrix products, local_layer(): jnp.einsum('bqhd,bkhd->bhqk', query_b, key_img, preferred_element_type=jn...  8.88 us
  transfers between devices with their start and end apart: 9, of which 7 were waited for; matrix products, arithmetic and copies ran while one was open for 36% of the time, Pallas kernels for 0%

profile of v3, /device:TPU:0, one launch (start us, length us, event | category | flops | bytes accessed | tf_op | source)
XLA Modules:
  0.0 370.6 jit_solution(12969933258920285109)
XLA Ops:
  7.2 2.2 slice_bitcast_fusion.12
  12.6 3.1 collective-permute-start
  17.0 3.9 %fusion.263 = (bf16[1,1024,512]{2,1,0:T(8,128)(2,1)}, bf16[1,1024,512]{2,1,0:T(8,128)(2,1)}, bf16[1,1024,512]{2,1,0:T(8,128)(2,1)S(1)}, bf16[1,1024,512]{2,1,0:T(8,128)(2,1)}) fusion(bf16[1,1024,2048]{2,1,0:T(8,128)(2,1)} %param.12), kind=kLoop, calls=%fused_computation.272 | loop fusion | bytes 8388608 | tf_op jit(solution)/shard_map/slice | solution.py:168
  23.4 4.3 %multiply_convert_fusion.1 = (bf16[1,1024,512]{2,1,0:T(8,128)(2,1)S(1)}, bf16[1,1024,512]{2,1,0:T(8,128)(2,1)}, bf16[1,1024,512]{2,1,0:T(8,128)(2,1)}, bf16[1,1024,512]{2,1,0:T(8,128)(2,1)}) fusion(bf16[1,1024,2048]{2,1,0:T(8,128)(2,1)} %param.15, f32[]{:T(128)} %bitcast), kind=kLoop, calls=%fused_computation.56 | loop fusion | flops 6291456 | bytes 8388612 | tf_op jit(solution)/shard_map/convert_element_type | solution.py:46
  29.2 2.2 reshape_squeeze.13
  31.3 2.2 convert_element_type.235
  33.6 2.2 reshape_squeeze.14
  35.8 2.2 convert_element_type.248
  37.9 2.2 reshape_squeeze.15
  41.7 39.4 %all-gather.5.cloned.1.call-done = bf16[2,1664,512]{2,1,0:T(8,128)(2,1)} async-done(((bf16[2,416,512]{2,1,0:T(8,128)(2,1)}), bf16[2,1664,512]{2,1,0:T(8,128)(2,1)}) %all-gather.5.cloned.1.call-update) | async-done | bytes 3407888 | tf_op jit(solution)/shard_map/all_gather | solution.py:150
  81.1 3.6 fusion.96
  85.7 2.0 bitcast_reduce_fusion.3
  90.9 3.1 fusion.97
  95.1 2.1 fusion.176
  97.1 5.2 %fusion.45 = bf16[16,4,64,128]{3,2,1,0:T(8,128)(2,1)S(1)} fusion(f32[16,4,64,64]{2,3,1,0:T(8,128)} %fusion.176, bf16[16,64,4,128]{3,2,1,0:T(4,128)(2,1)} %reshape_squeeze.12, f32[16,4,64,64]{3,2,1,0:T(8,128)} %copy-done.24, f32[16]{0:T(128)S(1)} %reshape.155, f32[16,4,64]{2,1,0:T(4,128)S(1)} %get-tuple-element.27), kind=kOutput, calls=%fused_computation.77 | convolution fusion | flops 69996608 | bytes 4210752 | tf_op jit(solution)/shard_map/bhqk,bqhd->bkhd/dot_general | solution.py:57
  103.3 2.8 fusion.78
  107.3 41.8 %all-gather.7.cloned.1.call-done = bf16[2,1664,512]{2,1,0:T(8,128)(2,1)} async-done(((bf16[2,416,512]{2,1,0:T(8,128)(2,1)}), bf16[2,1664,512]{2,1,0:T(8,128)(2,1)}) %all-gather.7.cloned.1.call-update) | async-done | bytes 3407888 | tf_op jit(solution)/shard_map/all_gather | solution.py:150
  149.1 4.4 %fusion.101 = bf16[512,512]{1,0:T(8,128)(2,1)} fusion(bf16[2,1664,512]{2,1,0:T(8,128)(2,1)} %all-gather.7.cloned.1.call-done, bf16[256,1664]{1,0:T(8,128)(2,1)} %collective-permute-done, bf16[256,1664]{1,0:T(8,128)(2,1)} %param.9, pred[]{:T(512)S(6)} %eq.10), kind=kOutput, calls=%fused_computation.129 | convolution fusion | flops 880345088 | bytes 3932161 | tf_op jit(solution)/shard_map/dot_general | solution.py:161
  155.4 2.0 copy.27
  157.4 2.7 gather_fusion.3
  160.1 2.4 bitcast_reduce_fusion.2
  165.6 3.9 %fusion.98 = bf16[512,512]{1,0:T(8,128)(2,1)} fusion(bf16[2,1664,512]{2,1,0:T(8,128)(2,1)S(1)} %copy-done.14, bf16[256,1664]{1,0:T(8,128)(2,1)} %collective-permute-done, bf16[256,1664]{1,0:T(8,128)(2,1)} %param.9, pred[]{:T(512)S(6)} %eq.10), kind=kOutput, calls=%fused_computation.128 | convolution fusion | flops 880345088 | bytes 3932161 | tf_op jit(solution)/shard_map/dot_general | solution.py:162
  171.5 2.0 copy.26
  173.4 2.7 gather_fusion.2
  176.2 3.6 fusion.170
  179.8 6.2 %fusion.48 = bf16[16,4,64,128]{3,2,1,0:T(8,128)(2,1)} fusion(f32[16,4,64,64]{2,3,1,0:T(8,128)} %fusion.170, bf16[16,64,4,128]{3,2,1,0:T(4,128)(2,1)} %reshape_squeeze.13, f32[16,4,64,64]{3,2,1,0:T(8,128)} %copy-done.26, f32[16,4,64]{2,1,0:T(4,128)S(1)} %get-tuple-element.29, f32[16]{0:T(128)S(1)} %reshape.155), kind=kOutput, calls=%fused_computation.78 | convolution fusion | flops 69996608 | bytes 4210752 | tf_op jit(solution)/shard_map/bhqk,bqhd->bkhd/dot_general | solution.py:57
  188.2 2.8 fusion.70
  191.0 2.9 add_add_fusion.2
  193.9 23.2 %all-gather.9.cloned.1.call-done = bf16[2,1664,512]{2,1,0:T(8,128)(2,1)} async-done(((bf16[2,416,512]{2,1,0:T(8,128)(2,1)}), bf16[2,1664,512]{2,1,0:T(8,128)(2,1)}) %all-gather.9.cloned.1.call-update) | async-done | bytes 3407888 | tf_op jit(solution)/shard_map/all_gather | solution.py:150
  217.0 3.6 fusion.107
  221.7 2.1 bitcast_reduce_fusion.1
  226.9 3.1 fusion.104
  231.1 2.3 fusion.164
  233.4 5.1 %fusion.51 = bf16[16,4,64,128]{3,2,1,0:T(8,128)(2,1)S(1)} fusion(f32[16,4,64,64]{2,3,1,0:T(8,128)} %fusion.164, bf16[16,64,4,128]{3,2,1,0:T(4,128)(2,1)} %reshape_squeeze.14, f32[16,4,64,64]{3,2,1,0:T(8,128)} %copy-done.28, f32[16,4,64]{2,1,0:T(4,128)S(1)} %get-tuple-element.31, f32[16]{0:T(128)S(1)} %reshape.155), kind=kOutput, calls=%fused_computation.79 | convolution fusion | flops 69996608 | bytes 4210752 | tf_op jit(solution)/shard_map/bhqk,bqhd->bkhd/dot_general | solution.py:57
  239.5 2.8 fusion.63
  243.5 41.9 %all-gather.11.cloned.1.call-done = bf16[2,1664,512]{2,1,0:T(8,128)(2,1)} async-done(((bf16[2,416,512]{2,1,0:T(8,128)(2,1)}), bf16[2,1664,512]{2,1,0:T(8,128)(2,1)}) %all-gather.11.cloned.1.call-update) | async-done | bytes 3407888 | tf_op jit(solution)/shard_map/all_gather | solution.py:150
  285.5 4.5 %fusion.113 = bf16[512,512]{1,0:T(8,128)(2,1)} fusion(bf16[2,1664,512]{2,1,0:T(8,128)(2,1)} %all-gather.11.cloned.1.call-done, bf16[256,1664]{1,0:T(8,128)(2,1)} %collective-permute-done, bf16[256,1664]{1,0:T(8,128)(2,1)} %param.9, pred[]{:T(512)S(6)} %eq.10), kind=kOutput, calls=%fused_computation.133 | convolution fusion | flops 880345088 | bytes 3932161 | tf_op jit(solution)/shard_map/dot_general | solution.py:161
  293.9 2.7 gather_fusion.7
  296.5 2.4 bitcast_reduce_fusion
  302.0 3.9 %fusion.110 = bf16[512,512]{1,0:T(8,128)(2,1)} fusion(bf16[2,1664,512]{2,1,0:T(8,128)(2,1)S(1)} %copy-done.10, bf16[256,1664]{1,0:T(8,128)(2,1)} %collective-permute-done, bf16[256,1664]{1,0:T(8,128)(2,1)} %param.9, pred[]{:T(512)S(6)} %eq.10), kind=kOutput, calls=%fused_computation.132 | convolution fusion | flops 880345088 | bytes 3932161 | tf_op jit(solution)/shard_map/dot_general | solution.py:162
  306.0 2.0 reshape.151
  309.9 2.7 gather_fusion.6
  312.7 3.6 fusion.158
  316.3 6.1 %fusion.54 = bf16[16,4,64,128]{3,2,1,0:T(8,128)(2,1)} fusion(f32[16,4,64,64]{2,3,1,0:T(8,128)} %fusion.158, bf16[16,64,4,128]{3,2,1,0:T(4,128)(2,1)} %reshape_squeeze.15, f32[16,4,64,64]{3,2,1,0:T(8,128)} %copy-done.30, f32[16,4,64]{2,1,0:T(4,128)S(1)} %get-tuple-element.33, f32[16]{0:T(128)S(1)} %reshape.155), kind=kOutput, calls=%fused_computation.80 | convolution fusion | flops 69996608 | bytes 4210752 | tf_op jit(solution)/shard_map/bhqk,bqhd->bkhd/dot_general | solution.py:57
  324.5 3.0 fusion.56
  334.1 9.5 %collective-permute-done.2 = bf16[128,1664]{1,0:T(8,128)(2,1)S(1)} collective-permute-done((bf16[128,1664]{1,0:T(8,128)(2,1)S(1)}, bf16[128,1664]{1,0:T(8,128)(2,1)S(1)}, u32[]{:S(2)}, u32[]{:S(2)}) %collective-permute-start.2) | collective-permute-done | bytes 426016 | tf_op jit(solution)/shard_map/ppermute | solution.py:77
  346.1 8.7 %collective-permute-done.3 = bf16[128,1664]{1,0:T(8,128)(2,1)S(1)} collective-permute-done((bf16[128,1664]{1,0:T(8,128)(2,1)S(1)}, bf16[128,1664]{1,0:T(8,128)(2,1)S(1)}, u32[]{:S(2)}, u32[]{:S(2)}) %collective-permute-start.3) | collective-permute-done | bytes 426016 | tf_op jit(solution)/shard_map/ppermute | solution.py:77
  360.2 2.3 maximum_bitcast_fusion
  (155 shorter events, 59.2 us)
Async XLA Ops:
  7.2 73.9 %all-gather.5.cloned.1.call-start = ((), (), s32[]{:S(2)}) async-start(), calls=%async_computation | async-start | bytes 4259840 | tf_op jit(solution)/shard_map/all_gather | solution.py:150
  10.5 138.6 %all-gather.7.cloned.1.call-start = ((), (), s32[]{:S(2)}) async-start(), calls=%async_computation.1 | async-start | bytes 4259840 | tf_op jit(solution)/shard_map/all_gather | solution.py:150
  11.5 205.5 %all-gather.9.cloned.1.call-start = ((), (), s32[]{:S(2)}) async-start(), calls=%async_computation.2 | async-start | bytes 4259840 | tf_op jit(solution)/shard_map/all_gather | solution.py:150
  12.5 4.2 %copy-start.22 = (s32[4,4,4]{2,1,0:T(4,128)S(1)}, s32[4,4,4]{2,1,0:T(4,128)}, u32[]{:S(2)}) copy-start(s32[4,4,4]{2,1,0:T(4,128)} %param.14) | copy-start | bytes 772
  12.6 272.9 %all-gather.11.cloned.1.call-start = ((), (), s32[]{:S(2)}) async-start(), calls=%async_computation.3 | async-start | bytes 4259840 | tf_op jit(solution)/shard_map/all_gather | solution.py:150
  12.6 29.1 %collective-permute-start = (bf16[256,1664]{1,0:T(8,128)(2,1)}, bf16[256,1664]{1,0:T(8,128)(2,1)}, u32[]{:S(2)}, u32[]{:S(2)}) collective-permute-start(bf16[256,1664]{1,0:T(8,128)(2,1)} %param.9), channel_id=1, source_target_pairs={{0,4},{4,0},{1,5},{5,1},{2,6},{6,2},{3,7},{7,3},{8,12},{12,8},{9,1... | collective-permute-start | bytes 2555912 | tf_op jit(solution)/shard_map/ppermute | solution.py:114
  20.9 1.2 copy-start.23
  87.7 1.4 copy-start.24
  87.8 3.1 copy-start.16
  95.1 2.1 copy-start.1
  103.3 2.8 copy-start.17
  103.3 2.8 copy-start.21
  160.1 2.4 copy-start.9
  162.5 1.3 copy-start.26
  162.6 3.0 copy-start.14
  188.2 2.8 copy-start.15
  188.2 2.8 copy-start.19
  221.7 2.1 copy-start.8
  223.8 1.3 copy-start.28
  223.8 3.1 copy-start.12
  231.1 2.3 copy-start.4
  238.5 3.7 %copy-start.13 = (bf16[2,1664,512]{2,1,0:T(8,128)(2,1)S(1)}, bf16[2,1664,512]{2,1,0:T(8,128)(2,1)}, u32[]{:S(2)}) copy-start(bf16[2,1664,512]{2,1,0:T(8,128)(2,1)} %all-gather.9.cloned.1.call-done) | copy-start | bytes 10223620
  239.5 2.8 copy-start
  239.5 2.9 copy-start.20
  296.5 2.4 copy-start.7
  299.0 1.3 copy-start.30
  299.0 3.1 copy-start.10
  324.5 3.0 copy-start.11
  324.5 3.0 copy-start.18
  327.6 1.6 copy-start.27
  328.7 1.3 copy-start.3
  328.9 2.4 collective-permute-start.1
  330.9 2.3 copy-start.5
  330.9 2.3 copy-start.29
  331.7 11.9 %collective-permute-start.2 = (bf16[128,1664]{1,0:T(8,128)(2,1)S(1)}, bf16[128,1664]{1,0:T(8,128)(2,1)S(1)}, u32[]{:S(2)}, u32[]{:S(2)}) collective-permute-start(bf16[128,1664]{1,0:T(8,128)(2,1)S(1)} %fusion.209), channel_id=1, source_target_pairs={{0,4},{4,0},{1,5},{5,1},{2,6},{6,2},{3,7},{7,3},{8,12},{12,8},{9,1... | collective-permute-start | bytes 1277960 | tf_op jit(solution)/shard_map/ppermute | solution.py:77
  333.2 12.0 %copy-start.31 = (f32[16,4,64,64]{3,2,1,0:T(8,128)S(1)}, f32[16,4,64,64]{3,2,1,0:T(8,128)}, u32[]{:S(2)}) copy-start(f32[16,4,64,64]{3,2,1,0:T(8,128)} %copy-done.30) | copy-start | bytes 3145732
  334.1 11.2 %copy-start.6 = (bf16[16,64,4,128]{3,1,2,0:T(8,128)(2,1)S(1)}, bf16[16,64,4,128]{3,1,2,0:T(8,128)(2,1)}, u32[]{:S(2)}) copy-start(bf16[16,64,4,128]{3,1,2,0:T(8,128)(2,1)} %gather_fusion.6) | copy-start | bytes 3145732
  343.7 11.3 %copy-start.2 = (bf16[16,64,4,128]{3,1,2,0:T(8,128)(2,1)S(1)}, bf16[16,64,4,128]{3,1,2,0:T(8,128)(2,1)}, u32[]{:S(2)}) copy-start(bf16[16,64,4,128]{3,1,2,0:T(8,128)(2,1)} %copy-done.1) | copy-start | bytes 3145732
  343.7 11.3 %copy-start.25 = (f32[16,4,64,64]{3,2,1,0:T(8,128)S(1)}, f32[16,4,64,64]{3,2,1,0:T(8,128)}, u32[]{:S(2)}) copy-start(f32[16,4,64,64]{3,2,1,0:T(8,128)} %copy-done.24) | copy-start | bytes 3145732
  343.7 11.1 %collective-permute-start.3 = (bf16[128,1664]{1,0:T(8,128)(2,1)S(1)}, bf16[128,1664]{1,0:T(8,128)(2,1)S(1)}, u32[]{:S(2)}, u32[]{:S(2)}) collective-permute-start(bf16[128,1664]{1,0:T(8,128)(2,1)S(1)} %fusion.180), channel_id=1, source_target_pairs={{0,2},{2,0},{1,3},{3,1},{4,6},{6,4},{5,7},{7,5},{8,10},{10,8},{9,1... | collective-permute-start | bytes 1277960 | tf_op jit(solution)/shard_map/ppermute | solution.py:77
  354.9 7.6 %collective-permute-start.4 = (bf16[128,1664]{1,0:T(8,128)(2,1)S(1)}, bf16[128,1664]{1,0:T(8,128)(2,1)S(1)}, u32[]{:S(2)}, u32[]{:S(2)}) collective-permute-start(bf16[128,1664]{1,0:T(8,128)(2,1)S(1)} %add_convert_fusion), channel_id=1, source_target_pairs={{0,1},{1,0},{2,3},{3,2},{4,5},{5,4},{6,7},{7,6},{8,9},{9,8},{10,11... | collective-permute-start | bytes 1277960 | tf_op jit(solution)/shard_map/ppermute | solution.py:94
Sparse Core Ops, SparseCore 0:
  10.6 70.4 all-gather.4
  82.7 66.3 all-gather.6
  150.6 66.3 all-gather.8
  219.0 66.3 all-gather.10

commit v4 on v3

--- a/solution.py
+++ b/solution.py
@@ -2,6 +2,8 @@
 import jax.numpy as jnp
 import numpy as np
 from jax import lax
+from jax.experimental import pallas as pl
+from jax.experimental.pallas import tpu as pltpu
 from jax.sharding import Mesh
 from jax.sharding import PartitionSpec as P
 
@@ -11,60 +13,79 @@
 IMGS = 2
 MICRO = 4
 CHUNKS = 4
-AHEAD = 4
+PARTS = (3, 2, 2, 1)
+AHEAD = 8
 RELAY = False
 
 
-def block_index(visible):
-    samples = visible.shape[0]
-    base = jnp.arange(samples, dtype=jnp.int32)[:, None] * IMGS
-    seen = (base + jnp.maximum(visible, 0)).reshape(-1)
-    validf = (visible >= 0).reshape(-1).astype(jnp.float32)
-    return (seen, validf)
-
-
-def local_layer(key_rows, value_rows, query, gate_value, cotangent, visible, heads):
-    width = heads * HD
-    seen, validf = block_index(visible)
-    images = key_rows.shape[0] // IMG_TOK
-    key_img = jnp.take(key_rows.reshape(images, IMG_TOK, heads, HD), seen, axis=0)
-    val_img = jnp.take(value_rows.reshape(images, IMG_TOK, heads, HD), seen, axis=0)
-    blocks = seen.shape[0]
-    query_b = query.reshape(blocks, TBLOCK, heads, HD)
+def attend_kernel(vis_ref, fac_ref, q_ref, k_ref, v_ref, g_ref, att_ref, kg_ref, vg_ref):
+    sample = pl.program_id(0)
+    seq = q_ref.shape[0]
+    keys = k_ref.shape[0]
     scale = 1.0 / HD**0.5
-    scores = (
-        jnp.einsum("bqhd,bkhd->bhqk", query_b, key_img, preferred_element_type=jnp.float32) * scale
-    )
-    exponent = jnp.exp(scores)
-    probs = exponent / jnp.sum(exponent, axis=-1, keepdims=True) * validf[:, None, None, None]
+    factor = fac_ref[0:1, 0:1]
+    q = q_ref[...]
+    k = k_ref[...]
+    v = v_ref[...]
+    rows = lax.broadcasted_iota(jnp.int32, (seq, keys), 0) // TBLOCK
+    image = lax.broadcasted_iota(jnp.int32, (seq, keys), 1) // IMG_TOK
+    sees = jnp.full((seq, keys), -1, jnp.int32)
+    for b in range(seq // TBLOCK):
+        sees = jnp.where(rows == b, vis_ref[sample, b], sees)
+    allowed = image == sees
+    valid = sees >= 0
+    scores = lax.dot_general(q, k, (((1,), (1,)), ((), ())), preferred_element_type=jnp.float32) * scale
+    exponent = jnp.where(allowed, jnp.exp(scores), 0.0)
+    total = jnp.sum(exponent, axis=-1, keepdims=True)
+    probs = jnp.where(valid, exponent / jnp.where(valid, total, 1.0), 0.0)
     probs_b = probs.astype(jnp.bfloat16)
-    mixed = jnp.einsum("bhqk,bkhd->bqhd", probs_b, val_img, preferred_element_type=jnp.float32)
-    factor = jnp.tanh(gate_value)
-    attended = (factor * mixed).astype(jnp.bfloat16).reshape(-1, width)
-    head_grad = (
-        (factor * cotangent.astype(jnp.float32))
-        .astype(jnp.bfloat16)
-        .reshape(blocks, TBLOCK, heads, HD)
-    )
-    vgrad_blk = jnp.einsum(
-        "bhqk,bqhd->bkhd", probs_b, head_grad, preferred_element_type=jnp.float32
-    )
-    prob_grad = jnp.einsum(
-        "bqhd,bkhd->bhqk", head_grad, val_img, preferred_element_type=jnp.float32
+    mixed = jnp.dot(probs_b, v, preferred_element_type=jnp.float32)
+    att_ref[...] = (factor * mixed).astype(att_ref.dtype)
+    head_grad = (factor * g_ref[...].astype(jnp.float32)).astype(jnp.bfloat16)
+    vg_ref[...] = lax.dot_general(
+        probs_b, head_grad, (((0,), (0,)), ((), ())), preferred_element_type=jnp.float32
+    ).astype(vg_ref.dtype)
+    prob_grad = lax.dot_general(
+        head_grad, v, (((1,), (1,)), ((), ())), preferred_element_type=jnp.float32
     )
     delta = jnp.sum(probs * prob_grad, axis=-1, keepdims=True)
     score_grad = (probs * (prob_grad - delta) * scale).astype(jnp.bfloat16)
-    kgrad_blk = jnp.einsum(
-        "bhqk,bqhd->bkhd", score_grad, query_b, preferred_element_type=jnp.float32
-    )
-    onehot = (seen[:, None] == jnp.arange(images, dtype=jnp.int32)[None, :]).astype(jnp.float32)
-    key_grad = (
-        jnp.einsum("bi,bkhd->ikhd", onehot, kgrad_blk).reshape(-1, width).astype(jnp.bfloat16)
-    )
-    value_grad = (
-        jnp.einsum("bi,bkhd->ikhd", onehot, vgrad_blk).reshape(-1, width).astype(jnp.bfloat16)
-    )
-    return (attended, key_grad, value_grad)
+    kg_ref[...] = lax.dot_general(
+        score_grad, q, (((0,), (0,)), ((), ())), preferred_element_type=jnp.float32
+    ).astype(kg_ref.dtype)
+
+
+def attend(key_rows, value_rows, query, cotangent, factor, visible, first_head, heads):
+    samples = visible.shape[0]
+    seq = query.shape[1] // samples
+    keys = key_rows.shape[0] // samples
+    fac = jnp.full((8, 128), factor, jnp.float32)
+    text_spec = pl.BlockSpec((None, seq, HD), lambda s, h, vis: (0, s, first_head + h))
+    image_spec = pl.BlockSpec((keys, HD), lambda s, h, vis: (s, h))
+    return pl.pallas_call(
+        attend_kernel,
+        grid_spec=pltpu.PrefetchScalarGridSpec(
+            num_scalar_prefetch=1,
+            grid=(samples, heads),
+            in_specs=[
+                pl.BlockSpec((8, 128), lambda s, h, vis: (0, 0)),
+                text_spec,
+                image_spec,
+                image_spec,
+                text_spec,
+            ],
+            out_specs=[
+                pl.BlockSpec((seq, HD), lambda s, h, vis: (s, h)),
+                image_spec,
+                image_spec,
+            ],
+        ),
+        out_shape=[
+            jax.ShapeDtypeStruct((query.shape[1], heads * HD), jnp.bfloat16),
+            jax.ShapeDtypeStruct(key_rows.shape, jnp.bfloat16),
+            jax.ShapeDtypeStruct(key_rows.shape, jnp.bfloat16),
+        ],
+    )(visible, fac, query, key_rows, value_rows, cotangent)
 
 
 def back_product(grad_rows, weight):
@@ -104,9 +125,16 @@
     micro = lax.axis_index("micro")
     width = key_weight.shape[1]
     heads = width // HD
-    chunks = min(CHUNKS, heads)
-    step = width // chunks
+    if heads % sum(PARTS) == 0:
+        unit = heads // sum(PARTS)
+        sizes = [part * unit * HD for part in PARTS]
+    else:
+        chunks = min(CHUNKS, heads)
+        sizes = [width // chunks] * chunks
+    chunks = len(sizes)
+    starts = [sum(sizes[:j]) for j in range(chunks)]
     gate_value = lax.dynamic_index_in_dim(gate, layer, 0, keepdims=False)
+    factor = jnp.tanh(gate_value)
     own_visible = lax.dynamic_index_in_dim(visible, micro, 0, keepdims=False)
     swap = [(0, 1), (1, 0)]
     paired = lax.axis_size("layer") == 2
@@ -140,7 +168,7 @@
         return jnp.concatenate(blocks, axis=1)
 
     def fetch(j, after):
-        cols = slice(j * step, (j + 1) * step)
+        cols = slice(starts[j], starts[j] + sizes[j])
         stacked = jnp.stack([key_weight[:, cols], value_weight[:, cols]])
         if after is not None:
             stacked, _ = lax.optimization_barrier((stacked, after))
@@ -152,7 +180,7 @@
     for j in range(min(AHEAD, chunks)):
         fetch(j, None)
     for j in range(chunks):
-        cols = slice(j * step, (j + 1) * step)
+        cols = slice(starts[j], starts[j] + sizes[j])
         stacked = gathered.pop(j)
         if term is not None:
             stacked, _ = lax.optimization_barrier((stacked, term))
@@ -162,14 +190,15 @@
         value_rows = jnp.dot(all_rows, w_value, preferred_element_type=jnp.float32).astype(
             jnp.bfloat16
         )
-        attended, key_grad, value_grad = local_layer(
+        attended, key_grad, value_grad = attend(
             key_rows,
             value_rows,
-            queries[0, :, cols],
-            gate_value,
-            out_grad[0, :, cols],
+            queries,
+            out_grad,
+            factor,
             own_visible,
-            step // HD,
+            starts[j] // HD,
+            sizes[j] // HD,
         )
         pieces.append(attended)
         part = back_product(key_grad, w_key) + back_product(value_grad, w_value)

time: 375 us -> 342 us (0.912)
  local copies, waits for them, and re-layouts: 65.3 us -> 6.44 us
  Pallas kernels: 0 us -> 56.9 us
  matrix products: 106 us -> 50.5 us
  waiting for transfers between devices: 165 us -> 194 us
    dot_general x28 -> x0, matrix products: 57.6 us -> none  [the longest x4 22.6 us: local_layer(): jnp.einsum('bhqk,bqhd->bkhd', score_grad, query_b, preferred_element_type...]
    pallas_call x0 -> x4, Pallas kernels: none -> 56.9 us  [attend(): pl.pallas_call(attend_kernel, grid_spec=pltpu.PrefetchScalarGridSpec(num_...]
    reshape x16 -> x0, local copies, waits for them, and re-layouts: 16.7 us -> none  [the longest x8 8.39 us: local_layer(): key_rows.reshape(images, IMG_TOK, heads, HD)]
    ppermute x1, waiting for transfers between devices: 0.01 us -> 16.4 us  [shards(): partner = lax.ppermute(vision_tokens, 'layer', swap)]
    convert_element_type x17 -> x0, local copies, waits for them, and re-layouts: 15.9 us -> none  [the longest x4 7.28 us: local_layer(): head_grad = (factor * cotangent.astype(jnp.float32)).astype(jnp.bfloat16)...]
    gather x8 -> x0, local copies, waits for them, and re-layouts: 13.8 us -> none  [the longest x4 6.96 us: local_layer(): jnp.take(value_rows.reshape(images, IMG_TOK, heads, HD), seen, axis=0)]
    all_gather x4, waiting for transfers between devices: 146 us -> 155 us  [fetch(): gathered[j] = lax.all_gather(stacked, 'micro', axis=1, tiled=True)]
    another operation x4 -> x0, local copies, waits for them, and re-layouts: 7.65 us -> none  [local_layer(): query_b = query.reshape(blocks, TBLOCK, heads, HD)]
  transfers between devices with their start and end apart: 9 -> 9, of which waited for: 7 -> 8; matrix products, arithmetic and copies ran while one was open for 36% -> 15% of each run, Pallas kernels for 0% -> 14%
where the time goes in v4:
time: 342 us; the launch traced here: 338 us
  waiting for transfers between devices  194 us (57%)
  Pallas kernels  56.9 us (17%)
  matrix products  50.5 us (15%)
  between operations  14.8 us (4%)
  other arithmetic  9.19 us (3%)
  starting transfers between devices  6.45 us (2%)
  local copies, waits for them, and re-layouts  6.44 us (2%)
    all_gather x4, waiting for transfers between devices, fetch(): gathered[j] = lax.all_gather(stacked, 'micro', axis=1, tiled=True)  155 us
    pallas_call x4, Pallas kernels, attend(): pl.pallas_call(attend_kernel, grid_spec=pltpu.PrefetchScalarGridSpec(num_...  56.9 us
    ppermute x3, waiting for transfers between devices, exchange(): lax.ppermute(value.astype(jnp.bfloat16), axis, swap).astype(jnp.float32)  22.3 us
    dot_general x8, matrix products, back_product(): lax.dot_general(grad_rows, weight, (((1,), (1,)), ((), ())), preferred_el...  18.7 us
    dot_general x4, matrix products, shards(): jnp.dot(all_rows, w_value, preferred_element_type=jnp.float32)  18.1 us
    ppermute x1, waiting for transfers between devices, shards(): partner = lax.ppermute(vision_tokens, 'layer', swap)  16.4 us
    dot_general x4, matrix products, shards(): jnp.dot(all_rows, w_key, preferred_element_type=jnp.float32)  13.7 us
  transfers between devices with their start and end apart: 9, of which 8 were waited for; matrix products, arithmetic and copies ran while one was open for 15% of the time, Pallas kernels for 14%

profile of v4, /device:TPU:0, one launch (start us, length us, event | category | flops | bytes accessed | tf_op | source)
XLA Modules:
  0.0 338.2 jit_solution(14996534734166994041)
XLA Ops:
  7.2 1.4 slice_bitcast_fusion.10
  8.6 1.2 pad_maximum_fusion
  9.8 0.7 copy-done.7
  10.5 0.5 copy-done.8
  11.0 1.1 slice_bitcast_fusion.12
  12.1 1.0 pad_maximum_fusion.1
  13.2 2.1 pad_maximum_fusion.2
  15.3 3.1 collective-permute-start
  18.5 0.8 pad_maximum_fusion.3
  19.3 0.6 dynamic_slice.9
  20.6 0.6 dynamic-slice_bitcast_fusion.vis_ref
  21.2 16.4 %collective-permute-done = bf16[256,1664]{1,0:T(8,128)(2,1)} collective-permute-done((bf16[256,1664]{1,0:T(8,128)(2,1)}, bf16[256,1664]{1,0:T(8,128)(2,1)}, u32[]{:S(2)}, u32[]{:S(2)}) %collective-permute-start) | collective-permute-done | bytes 852000 | tf_op jit(solution)/shard_map/ppermute | solution.py:142
  37.7 71.1 %all-gather.5.cloned.1.call-done = bf16[2,1664,768]{2,1,0:T(8,128)(2,1)} async-done(((bf16[2,416,768]{2,1,0:T(8,128)(2,1)}), bf16[2,1664,768]{2,1,0:T(8,128)(2,1)}) %all-gather.5.cloned.1.call-update) | async-done | bytes 5111824 | tf_op jit(solution)/shard_map/all_gather | solution.py:178
  108.8 5.4 %fusion.25.v_ref = bf16[512,768]{1,0:T(8,128)(2,1)} fusion(bf16[2,1664,768]{2,1,0:T(8,128)(2,1)} %all-gather.5.cloned.1.call-done, bf16[256,1664]{1,0:T(8,128)(2,1)} %collective-permute-done, bf16[256,1664]{1,0:T(8,128)(2,1)} %param.7, pred[]{:T(512)S(6)} %eq.4), kind=kOutput, calls=%fused_computation.35 | convolution fusion | flops 1316683776 | bytes 5046273 | tf_op jit(solution)/shard_map/dot_general | solution.py:190
  114.2 4.1 %fusion.26.k_ref = bf16[512,768]{1,0:T(8,128)(2,1)} fusion(bf16[2,1664,768]{2,1,0:T(8,128)(2,1)S(1)} %copy-done.18, bf16[256,1664]{1,0:T(8,128)(2,1)} %collective-permute-done, bf16[256,1664]{1,0:T(8,128)(2,1)S(1)} %copy-done.20, pred[]{:T(512)S(6)} %eq.4), kind=kOutput, calls=%fused_computation.36 | convolution fusion | flops 1316683776 | bytes 5046273 | tf_op jit(solution)/shard_map/dot_general | solution.py:189
  118.3 0.6 broadcast_in_dim.4.fac_ref
  118.9 20.4 %shard_map.86 = (bf16[1024,768]{1,0:T(8,128)(2,1)}, bf16[512,768]{1,0:T(8,128)(2,1)}, bf16[512,768]{1,0:T(8,128)(2,1)}) custom-call(s32[4,4]{1,0:T(4,128)} %dynamic-slice_bitcast_fusion.vis_ref, f32[8,128]{1,0:T(8,128)} %broadcast_in_dim.4.fac_ref, bf16[1,1024,2048]{2,1,0:T(8,128)(2,1)} %q_ref.7, bf16[512,768]{1,0:T(8,128)(2,1)} %fusion.26.k_ref, ...), custom_call_target="tpu_custom_call" | custom-call | tf_op jit(solution)/shard_map/pallas_call | solution.py:65
  139.3 3.7 %fusion = f32[512,1664]{1,0:T(8,128)S(1)} fusion(bf16[512,768]{1,0:T(8,128)(2,1)} %get-tuple-element.18, bf16[2,1664,768]{2,1,0:T(8,128)(2,1)} %all-gather.5.cloned.1.call-done), kind=kOutput, calls=%fused_computation.7 | convolution fusion | flops 1308622848 | bytes 6750208 | tf_op jit(solution)/shard_map/dot_general | solution.py:92
  143.1 3.4 %convolution_add_fusion = f32[512,1664]{1,0:T(8,128)} fusion(f32[512,1664]{1,0:T(8,128)S(1)} %fusion, bf16[512,768]{1,0:T(8,128)(2,1)S(1)} %copy-done.24, bf16[2,1664,768]{2,1,0:T(8,128)(2,1)S(1)} %copy-done.19), kind=kOutput, calls=%fused_computation.4 | convolution fusion | flops 1309474816 | bytes 10158080 | tf_op jit(solution)/shard_map/dot_general | solution.py:92
  146.5 30.0 %all-gather.7.cloned.1.call-done = bf16[2,1664,512]{2,1,0:T(8,128)(2,1)} async-done(((bf16[2,416,512]{2,1,0:T(8,128)(2,1)}), bf16[2,1664,512]{2,1,0:T(8,128)(2,1)}) %all-gather.7.cloned.1.call-update) | async-done | bytes 3407888 | tf_op jit(solution)/shard_map/all_gather | solution.py:178
  176.5 4.6 %fusion.30.v_ref = bf16[512,512]{1,0:T(8,128)(2,1)} fusion(bf16[2,1664,512]{2,1,0:T(8,128)(2,1)} %all-gather.7.cloned.1.call-done, bf16[256,1664]{1,0:T(8,128)(2,1)} %collective-permute-done, bf16[256,1664]{1,0:T(8,128)(2,1)} %param.7, pred[]{:T(512)S(6)} %eq.4), kind=kOutput, calls=%fused_computation.38 | convolution fusion | flops 880345088 | bytes 3932161 | tf_op jit(solution)/shard_map/dot_general | solution.py:190
  181.0 3.4 fusion.27.k_ref
  184.4 14.1 %shard_map.87 = (bf16[1024,512]{1,0:T(8,128)(2,1)}, bf16[512,512]{1,0:T(8,128)(2,1)}, bf16[512,512]{1,0:T(8,128)(2,1)}) custom-call(s32[4,4]{1,0:T(4,128)} %dynamic-slice_bitcast_fusion.vis_ref, f32[8,128]{1,0:T(8,128)} %broadcast_in_dim.4.fac_ref, bf16[1,1024,2048]{2,1,0:T(8,128)(2,1)} %q_ref.7, bf16[512,512]{1,0:T(8,128)(2,1)} %fusion.27.k_ref, ...), custom_call_target="tpu_custom_call" | custom-call | tf_op jit(solution)/shard_map/pallas_call | solution.py:65
  198.6 2.3 fusion.13
  200.9 2.9 add_add_fusion.2
  203.8 41.2 %all-gather.9.cloned.1.call-done = bf16[2,1664,512]{2,1,0:T(8,128)(2,1)} async-done(((bf16[2,416,512]{2,1,0:T(8,128)(2,1)}), bf16[2,1664,512]{2,1,0:T(8,128)(2,1)}) %all-gather.9.cloned.1.call-update) | async-done | bytes 3407888 | tf_op jit(solution)/shard_map/all_gather | solution.py:178
  245.0 4.5 %fusion.36.v_ref = bf16[512,512]{1,0:T(8,128)(2,1)} fusion(bf16[2,1664,512]{2,1,0:T(8,128)(2,1)} %all-gather.9.cloned.1.call-done, bf16[256,1664]{1,0:T(8,128)(2,1)} %collective-permute-done, bf16[256,1664]{1,0:T(8,128)(2,1)} %param.7, pred[]{:T(512)S(6)} %eq.4), kind=kOutput, calls=%fused_computation.40 | convolution fusion | flops 880345088 | bytes 3932161 | tf_op jit(solution)/shard_map/dot_general | solution.py:190
  249.6 3.4 fusion.33.k_ref
  252.9 14.1 %shard_map.88 = (bf16[1024,512]{1,0:T(8,128)(2,1)}, bf16[512,512]{1,0:T(8,128)(2,1)}, bf16[512,512]{1,0:T(8,128)(2,1)}) custom-call(s32[4,4]{1,0:T(4,128)} %dynamic-slice_bitcast_fusion.vis_ref, f32[8,128]{1,0:T(8,128)} %broadcast_in_dim.4.fac_ref, bf16[1,1024,2048]{2,1,0:T(8,128)(2,1)} %q_ref.7, bf16[512,512]{1,0:T(8,128)(2,1)} %fusion.33.k_ref, ...), custom_call_target="tpu_custom_call" | custom-call | tf_op jit(solution)/shard_map/pallas_call | solution.py:65
  267.1 2.3 fusion.6
  269.4 0.8 copy-done.4
  270.3 1.1 add_add_fusion.1
  271.4 12.9 %all-gather.11.cloned.1.call-done = bf16[2,1664,256]{2,1,0:T(8,128)(2,1)} async-done(((bf16[2,416,256]{2,1,0:T(8,128)(2,1)}), bf16[2,1664,256]{2,1,0:T(8,128)(2,1)}) %all-gather.11.cloned.1.call-update) | async-done | bytes 1703952 | tf_op jit(solution)/shard_map/all_gather | solution.py:178
  284.3 3.7 %convolution_convert_fusion.v_ref = bf16[512,256]{1,0:T(8,128)(2,1)} fusion(bf16[2,1664,256]{2,1,0:T(8,128)(2,1)} %all-gather.11.cloned.1.call-done, bf16[256,1664]{1,0:T(8,128)(2,1)} %collective-permute-done, bf16[256,1664]{1,0:T(8,128)(2,1)} %param.7, pred[]{:T(512)S(6)} %eq.4), kind=kOutput, calls=%fused_computation.42 | convolution fusion | flops 444006400 | bytes 2818049 | tf_op jit(solution)/shard_map/dot_general | solution.py:190
  288.0 2.8 convolution_convert_fusion.1.k_ref
  290.8 8.2 %shard_map.89 = (bf16[1024,256]{1,0:T(8,128)(2,1)}, bf16[512,256]{1,0:T(8,128)(2,1)}, bf16[512,256]{1,0:T(8,128)(2,1)}) custom-call(s32[4,4]{1,0:T(4,128)} %dynamic-slice_bitcast_fusion.vis_ref, f32[8,128]{1,0:T(8,128)} %broadcast_in_dim.4.fac_ref, bf16[1,1024,2048]{2,1,0:T(8,128)(2,1)} %q_ref.7, bf16[512,256]{1,0:T(8,128)(2,1)} %convolution_convert_fusion.1.k_ref, ...), custom_call_target="tpu_custom_call" | custom-call | tf_op jit(solution)/shard_map/pallas_call | solution.py:65
  299.0 2.0 fusion.42
  301.1 0.8 add_add_fusion
  301.9 0.2 select_convert_fusion
  302.1 2.4 collective-permute-done.1
  304.5 0.3 convert_add_fusion
  304.9 1.6 collective-permute-start.2
  306.5 10.4 %collective-permute-done.2 = bf16[128,1664]{1,0:T(8,128)(2,1)S(1)} collective-permute-done((bf16[128,1664]{1,0:T(8,128)(2,1)S(1)}, bf16[128,1664]{1,0:T(8,128)(2,1)S(1)}, u32[]{:S(2)}, u32[]{:S(2)}) %collective-permute-start.2) | collective-permute-done | bytes 426016 | tf_op jit(solution)/shard_map/ppermute | solution.py:98
  316.8 0.1 fusion.39
  316.9 1.5 collective-permute-start.3
  318.5 9.5 %collective-permute-done.3 = bf16[128,1664]{1,0:T(8,128)(2,1)S(1)} collective-permute-done((bf16[128,1664]{1,0:T(8,128)(2,1)S(1)}, bf16[128,1664]{1,0:T(8,128)(2,1)S(1)}, u32[]{:S(2)}, u32[]{:S(2)}) %collective-permute-start.3) | collective-permute-done | bytes 426016 | tf_op jit(solution)/shard_map/ppermute | solution.py:98
  328.2 2.3 maximum_bitcast_fusion
  330.6 1.1 maximum_select_fusion.1
  (63 shorter events, 0.8 us)
Async XLA Ops:
  7.2 13.5 %copy-start = (s32[4,4,4]{2,1,0:T(4,128)S(1)}, s32[4,4,4]{2,1,0:T(4,128)}, u32[]{:S(2)}) copy-start(s32[4,4,4]{2,1,0:T(4,128)} %param.12) | copy-start | bytes 772
  7.2 101.6 %all-gather.5.cloned.1.call-start = ((), (), s32[]{:S(2)}) async-start(), calls=%async_computation | async-start | bytes 6389760 | tf_op jit(solution)/shard_map/all_gather | solution.py:178
  8.6 1.9 copy-start.7
  8.6 2.4 copy-start.8
  9.8 166.7 %all-gather.7.cloned.1.call-start = ((), (), s32[]{:S(2)}) async-start(), calls=%async_computation.1 | async-start | bytes 4259840 | tf_op jit(solution)/shard_map/all_gather | solution.py:178
  13.1 6.2 %copy-start.25 = (f32[2]{0:T(128)S(1)}, f32[2]{0:T(128)}, u32[]{:S(2)}) copy-start(f32[2]{0:T(128)} %param.11) | copy-start | bytes 28
  13.1 231.9 %all-gather.9.cloned.1.call-start = ((), (), s32[]{:S(2)}) async-start(), calls=%async_computation.2 | async-start | bytes 4259840 | tf_op jit(solution)/shard_map/all_gather | solution.py:178
  15.3 269.0 %all-gather.11.cloned.1.call-start = ((), (), s32[]{:S(2)}) async-start(), calls=%async_computation.3 | async-start | bytes 2129920 | tf_op jit(solution)/shard_map/all_gather | solution.py:178
  15.3 22.3 %collective-permute-start = (bf16[256,1664]{1,0:T(8,128)(2,1)}, bf16[256,1664]{1,0:T(8,128)(2,1)}, u32[]{:S(2)}, u32[]{:S(2)}) collective-permute-start(bf16[256,1664]{1,0:T(8,128)(2,1)} %param.7), channel_id=1, source_target_pairs={{0,4},{4,0},{1,5},{5,1},{2,6},{6,2},{3,7},{7,3},{8,12},{12,8},{9,1... | collective-permute-start | bytes 2555912 | tf_op jit(solution)/shard_map/ppermute | solution.py:142
  21.2 92.9 %copy-start.20 = (bf16[256,1664]{1,0:T(8,128)(2,1)S(1)}, bf16[256,1664]{1,0:T(8,128)(2,1)}, u32[]{:S(2)}) copy-start(bf16[256,1664]{1,0:T(8,128)(2,1)} %param.7) | copy-start | bytes 2555908
  108.8 5.4 %copy-start.18 = (bf16[2,1664,768]{2,1,0:T(8,128)(2,1)S(1)}, bf16[2,1664,768]{2,1,0:T(8,128)(2,1)}, u32[]{:S(2)}) copy-start(bf16[2,1664,768]{2,1,0:T(8,128)(2,1)} %all-gather.5.cloned.1.call-done) | copy-start | bytes 15335428
  139.3 3.8 %copy-start.19 = (bf16[2,1664,768]{2,1,0:T(8,128)(2,1)S(1)}, bf16[2,1664,768]{2,1,0:T(8,128)(2,1)}, u32[]{:S(2)}) copy-start(bf16[2,1664,768]{2,1,0:T(8,128)(2,1)} %all-gather.5.cloned.1.call-done) | copy-start | bytes 15335428
  139.3 3.8 %copy-start.24 = (bf16[512,768]{1,0:T(8,128)(2,1)S(1)}, bf16[512,768]{1,0:T(8,128)(2,1)}, u32[]{:S(2)}) copy-start(bf16[512,768]{1,0:T(8,128)(2,1)} %get-tuple-element.19) | copy-start | bytes 2359300
  176.5 4.6 %copy-start.5 = (bf16[2,1664,512]{2,1,0:T(8,128)(2,1)S(1)}, bf16[2,1664,512]{2,1,0:T(8,128)(2,1)}, u32[]{:S(2)}) copy-start(bf16[2,1664,512]{2,1,0:T(8,128)(2,1)} %all-gather.7.cloned.1.call-done) | copy-start | bytes 10223620
  176.5 4.6 %copy-start.21 = (bf16[256,1664]{1,0:T(8,128)(2,1)S(1)}, bf16[256,1664]{1,0:T(8,128)(2,1)}, u32[]{:S(2)}) copy-start(bf16[256,1664]{1,0:T(8,128)(2,1)} %param.7) | copy-start | bytes 2555908
  198.6 2.3 copy-start.6
  198.6 2.4 copy-start.15
  245.0 4.5 %copy-start.3 = (bf16[2,1664,512]{2,1,0:T(8,128)(2,1)S(1)}, bf16[2,1664,512]{2,1,0:T(8,128)(2,1)}, u32[]{:S(2)}) copy-start(bf16[2,1664,512]{2,1,0:T(8,128)(2,1)} %all-gather.9.cloned.1.call-done) | copy-start | bytes 10223620
  245.0 4.5 %copy-start.22 = (bf16[256,1664]{1,0:T(8,128)(2,1)S(1)}, bf16[256,1664]{1,0:T(8,128)(2,1)}, u32[]{:S(2)}) copy-start(bf16[256,1664]{1,0:T(8,128)(2,1)} %param.7) | copy-start | bytes 2555908
  267.0 2.4 copy-start.2
  267.0 3.2 copy-start.4
  267.0 3.2 copy-start.16
  284.3 3.7 %copy-start.9 = (bf16[2,1664,256]{2,1,0:T(8,128)(2,1)S(1)}, bf16[2,1664,256]{2,1,0:T(8,128)(2,1)}, u32[]{:S(2)}) copy-start(bf16[2,1664,256]{2,1,0:T(8,128)(2,1)} %all-gather.11.cloned.1.call-done) | copy-start | bytes 5111812
  284.3 3.7 %copy-start.23 = (bf16[256,1664]{1,0:T(8,128)(2,1)S(1)}, bf16[256,1664]{1,0:T(8,128)(2,1)}, u32[]{:S(2)}) copy-start(bf16[256,1664]{1,0:T(8,128)(2,1)} %param.7) | copy-start | bytes 2555908
  299.0 2.1 copy-start.10
  299.0 2.1 copy-start.17
  302.0 2.4 collective-permute-start.1
  304.8 23.4 %copy-start.11 = (bf16[1024,768]{1,0:T(8,128)(2,1)S(1)}, bf16[1024,768]{1,0:T(8,128)(2,1)}, u32[]{:S(2)}) copy-start(bf16[1024,768]{1,0:T(8,128)(2,1)} %get-tuple-element.17) | copy-start | bytes 4718596
  304.8 23.4 %copy-start.12 = (bf16[1024,512]{1,0:T(8,128)(2,1)S(1)}, bf16[1024,512]{1,0:T(8,128)(2,1)}, u32[]{:S(2)}) copy-start(bf16[1024,512]{1,0:T(8,128)(2,1)} %get-tuple-element.21) | copy-start | bytes 3145732
  304.8 23.4 %copy-start.13 = (bf16[1024,512]{1,0:T(8,128)(2,1)S(1)}, bf16[1024,512]{1,0:T(8,128)(2,1)}, u32[]{:S(2)}) copy-start(bf16[1024,512]{1,0:T(8,128)(2,1)} %get-tuple-element.25) | copy-start | bytes 3145732
  304.8 23.4 %copy-start.14 = (bf16[1024,256]{1,0:T(8,128)(2,1)S(1)}, bf16[1024,256]{1,0:T(8,128)(2,1)}, u32[]{:S(2)}) copy-start(bf16[1024,256]{1,0:T(8,128)(2,1)} %get-tuple-element.29) | copy-start | bytes 1572868
  304.9 11.9 %collective-permute-start.2 = (bf16[128,1664]{1,0:T(8,128)(2,1)S(1)}, bf16[128,1664]{1,0:T(8,128)(2,1)S(1)}, u32[]{:S(2)}, u32[]{:S(2)}) collective-permute-start(bf16[128,1664]{1,0:T(8,128)(2,1)S(1)} %fusion.49), channel_id=1, source_target_pairs={{0,4},{4,0},{1,5},{5,1},{2,6},{6,2},{3,7},{7,3},{8,12},{12,8},{9,1... | collective-permute-start | bytes 1277960 | tf_op jit(solution)/shard_map/ppermute | solution.py:98
  316.9 11.1 %collective-permute-start.3 = (bf16[128,1664]{1,0:T(8,128)(2,1)S(1)}, bf16[128,1664]{1,0:T(8,128)(2,1)S(1)}, u32[]{:S(2)}, u32[]{:S(2)}) collective-permute-start(bf16[128,1664]{1,0:T(8,128)(2,1)S(1)} %fusion.39), channel_id=1, source_target_pairs={{0,2},{2,0},{1,3},{3,1},{4,6},{6,4},{5,7},{7,5},{8,10},{10,8},{9,1... | collective-permute-start | bytes 1277960 | tf_op jit(solution)/shard_map/ppermute | solution.py:98
  328.1 2.5 collective-permute-start.4
  328.2 3.4 %copy-start.1 = (s32[4,4,4]{2,1,0:T(4,128)S(1)}, s32[4,4,4]{2,1,0:T(4,128)}, u32[]{:S(2)}) copy-start(s32[4,4,4]{2,1,0:T(4,128)} %param.12) | copy-start | bytes 772
Sparse Core Ops, SparseCore 0:
  10.1 98.5 all-gather.4
  110.3 66.0 all-gather.6
  178.6 66.3 all-gather.8
  246.5 37.7 all-gather.10

commit v5 on v4

--- a/solution.py
+++ b/solution.py
@@ -13,7 +13,7 @@
 IMGS = 2
 MICRO = 4
 CHUNKS = 4
-PARTS = (3, 2, 2, 1)
+PARTS = (3, 1)
 AHEAD = 8
 RELAY = False
 

time: 342 us -> 326 us (0.953)
  matrix products: 50.5 us -> 34.4 us
  waiting for transfers between devices: 194 us -> 202 us
  Pallas kernels: 56.9 us -> 52.9 us
    dot_general x4 -> x2, matrix products: 13.7 us -> 6.12 us  [shards(): jnp.dot(all_rows, w_key, preferred_element_type=jnp.float32)]
    all_gather x4 -> x2, waiting for transfers between devices: 155 us -> 163 us  [fetch(): gathered[j] = lax.all_gather(stacked, 'micro', axis=1, tiled=True)]
    dot_general x4 -> x2, matrix products: 18.1 us -> 11.4 us  [shards(): jnp.dot(all_rows, w_value, preferred_element_type=jnp.float32)]
    pallas_call x4 -> x2, Pallas kernels: 56.9 us -> 52.9 us  [attend(): pl.pallas_call(attend_kernel, grid_spec=pltpu.PrefetchScalarGridSpec(num_...]
    dot_general x8 -> x4, matrix products: 18.7 us -> 16.8 us  [back_product(): lax.dot_general(grad_rows, weight, (((1,), (1,)), ((), ())), preferred_el...]
  transfers between devices with their start and end apart: 9 -> 7, of which waited for: 8 -> 6; matrix products, arithmetic and copies ran while one was open for 15% -> 10% of each run, Pallas kernels for 14% -> 12%
where the time goes in v5:
time: 326 us; the launch traced here: 323 us
  waiting for transfers between devices  202 us (62%)
  Pallas kernels  52.9 us (16%)
  matrix products  34.4 us (11%)
  between operations  14.9 us (5%)
  other arithmetic  7.17 us (2%)
  starting transfers between devices  6.36 us (2%)
  local copies, waits for them, and re-layouts  4.98 us (2%)
    all_gather x2, waiting for transfers between devices, fetch(): gathered[j] = lax.all_gather(stacked, 'micro', axis=1, tiled=True)  163 us
    pallas_call x2, Pallas kernels, attend(): pl.pallas_call(attend_kernel, grid_spec=pltpu.PrefetchScalarGridSpec(num_...  52.9 us
    ppermute x3, waiting for transfers between devices, exchange(): lax.ppermute(value.astype(jnp.bfloat16), axis, swap).astype(jnp.float32)  22.3 us
    ppermute x1, waiting for transfers between devices, shards(): partner = lax.ppermute(vision_tokens, 'layer', swap)  17 us
    dot_general x4, matrix products, back_product(): lax.dot_general(grad_rows, weight, (((1,), (1,)), ((), ())), preferred_el...  16.8 us
    dot_general x2, matrix products, shards(): jnp.dot(all_rows, w_value, preferred_element_type=jnp.float32)  11.4 us
  transfers between devices with their start and end apart: 7, of which 6 were waited for; matrix products, arithmetic and copies ran while one was open for 10% of the time, Pallas kernels for 12%

profile of v5, /device:TPU:0, one launch (start us, length us, event | category | flops | bytes accessed | tf_op | source)
XLA Modules:
  0.0 322.6 jit_solution(16020001332032004245)
XLA Ops:
  7.2 0.0 copy-start
  7.2 0.0 all-gather.3.cloned.1.call-start
  7.2 1.9 slice_bitcast_fusion.12
  9.1 1.7 pad_maximum_fusion
  10.8 0.0 all-gather.3.cloned.1.call-update
  10.8 0.0 copy-start.9
  10.8 0.0 copy-start.13
  10.8 0.0 all-gather.5.cloned.1.call-start
  10.9 1.3 slice_bitcast_fusion.14
  12.1 1.0 pad_maximum_fusion.1
  13.1 0.0 all-gather.5.cloned.1.call-update
  13.2 3.1 collective-permute-start
  16.2 0.6 dynamic_slice.9
  17.5 0.6 dynamic-slice_bitcast_fusion.vis_ref
  18.1 17.0 %collective-permute-done = bf16[256,1664]{1,0:T(8,128)(2,1)S(1)} collective-permute-done((bf16[256,1664]{1,0:T(8,128)(2,1)S(1)}, bf16[256,1664]{1,0:T(8,128)(2,1)S(1)}, u32[]{:S(2)}, u32[]{:S(2)}) %collective-permute-start) | collective-permute-done | bytes 852000 | tf_op jit(solution)/shard_map/ppermute | solution.py:142
  35.2 158.1 %all-gather.3.cloned.1.call-done = bf16[2,1664,1536]{2,1,0:T(8,128)(2,1)} async-done(((bf16[2,416,1536]{2,1,0:T(8,128)(2,1)}), bf16[2,1664,1536]{2,1,0:T(8,128)(2,1)}) %all-gather.3.cloned.1.call-update) | async-done | bytes 10223632 | tf_op jit(solution)/shard_map/all_gather | solution.py:178
  193.3 6.8 %fusion.5.v_ref = bf16[512,1536]{1,0:T(8,128)(2,1)} fusion(bf16[2,1664,1536]{2,1,0:T(8,128)(2,1)} %all-gather.3.cloned.1.call-done, bf16[256,1664]{1,0:T(8,128)(2,1)S(1)} %collective-permute-done, bf16[256,1664]{1,0:T(8,128)(2,1)S(1)} %copy-done.9, pred[]{:T(512)S(6)} %eq.4), kind=kOutput, calls=%fused_computation.9 | convolution fusion | flops 2625699840 | bytes 8388609 | tf_op jit(solution)/shard_map/dot_general | solution.py:190
  200.1 0.0 copy-done.11
  200.1 4.2 %fusion.6.k_ref = bf16[512,1536]{1,0:T(8,128)(2,1)} fusion(bf16[2,1664,1536]{2,1,0:T(8,128)(2,1)S(1)} %copy-done.7, bf16[256,1664]{1,0:T(8,128)(2,1)S(1)} %collective-permute-done, bf16[256,1664]{1,0:T(8,128)(2,1)S(1)} %copy-done.9, pred[]{:T(512)S(6)} %eq.4), kind=kOutput, calls=%fused_computation.10 | convolution fusion | flops 2625699840 | bytes 8388609 | tf_op jit(solution)/shard_map/dot_general | solution.py:189
  204.3 0.6 broadcast_in_dim.7.fac_ref
  204.9 38.8 %shard_map.86 = (bf16[1024,1536]{1,0:T(8,128)(2,1)}, bf16[512,1536]{1,0:T(8,128)(2,1)}, bf16[512,1536]{1,0:T(8,128)(2,1)}) custom-call(s32[4,4]{1,0:T(4,128)} %dynamic-slice_bitcast_fusion.vis_ref, f32[8,128]{1,0:T(8,128)} %broadcast_in_dim.7.fac_ref, bf16[1,1024,2048]{2,1,0:T(8,128)(2,1)} %q_ref.3, bf16[512,1536]{1,0:T(8,128)(2,1)} %fusion.6.k_ref, ...), custom_call_target="tpu_custom_call" | custom-call | tf_op jit(solution)/shard_map/pallas_call | solution.py:65
  243.7 6.1 %fusion = f32[512,1664]{1,0:T(8,128)S(1)} fusion(bf16[512,1536]{1,0:T(8,128)(2,1)} %get-tuple-element.10, bf16[2,1664,1536]{2,1,0:T(8,128)(2,1)} %all-gather.3.cloned.1.call-done), kind=kOutput, calls=%fused_computation.2 | convolution fusion | flops 2617245696 | bytes 10092544 | tf_op jit(solution)/shard_map/dot_general | solution.py:92
  249.8 7.2 %fusion.4 = f32[512,1664]{1,0:T(8,128)} fusion(f32[512,1664]{1,0:T(8,128)S(1)} %fusion, bf16[512,1536]{1,0:T(8,128)(2,1)S(1)} %copy-done.8, bf16[2,1664,1536]{2,1,0:T(8,128)(2,1)} %all-gather.3.cloned.1.call-done), kind=kOutput, calls=%fused_computation.8 | convolution fusion | flops 2618097664 | bytes 13500416 | tf_op jit(solution)/shard_map/dot_general | solution.py:92
  257.0 4.4 %all-gather.5.cloned.1.call-done = bf16[2,1664,512]{2,1,0:T(8,128)(2,1)} async-done(((bf16[2,416,512]{2,1,0:T(8,128)(2,1)}), bf16[2,1664,512]{2,1,0:T(8,128)(2,1)}) %all-gather.5.cloned.1.call-update) | async-done | bytes 3407888 | tf_op jit(solution)/shard_map/all_gather | solution.py:178
  261.4 4.7 %fusion.21.v_ref = bf16[512,512]{1,0:T(8,128)(2,1)} fusion(bf16[2,1664,512]{2,1,0:T(8,128)(2,1)} %all-gather.5.cloned.1.call-done, bf16[256,1664]{1,0:T(8,128)(2,1)} %copy-done.11, bf16[256,1664]{1,0:T(8,128)(2,1)} %param.7, pred[]{:T(512)S(6)} %eq.4), kind=kOutput, calls=%fused_computation.27 | convolution fusion | flops 880345088 | bytes 3932161 | tf_op jit(solution)/shard_map/dot_general | solution.py:190
  266.1 0.0 copy-done.12
  266.1 1.9 fusion.18.k_ref
  268.0 14.1 %shard_map.87 = (bf16[1024,512]{1,0:T(8,128)(2,1)}, bf16[512,512]{1,0:T(8,128)(2,1)}, bf16[512,512]{1,0:T(8,128)(2,1)}) custom-call(s32[4,4]{1,0:T(4,128)} %dynamic-slice_bitcast_fusion.vis_ref, f32[8,128]{1,0:T(8,128)} %broadcast_in_dim.7.fac_ref, bf16[1,1024,2048]{2,1,0:T(8,128)(2,1)} %q_ref.3, bf16[512,512]{1,0:T(8,128)(2,1)} %fusion.18.k_ref, ...), custom_call_target="tpu_custom_call" | custom-call | tf_op jit(solution)/shard_map/pallas_call | solution.py:65
  282.1 2.3 fusion.10
  284.5 1.2 add_add_fusion
  285.6 0.2 select_convert_fusion
  285.8 0.1 collective-permute-start.1
  285.9 2.4 collective-permute-done.1
  288.3 0.3 convert_add_fusion
  288.5 0.0 copy-start.4
  288.5 0.0 copy-start.5
  288.6 0.1 fusion.25
  288.6 1.5 collective-permute-start.2
  290.2 10.4 %collective-permute-done.2 = bf16[128,1664]{1,0:T(8,128)(2,1)S(1)} collective-permute-done((bf16[128,1664]{1,0:T(8,128)(2,1)S(1)}, bf16[128,1664]{1,0:T(8,128)(2,1)S(1)}, u32[]{:S(2)}, u32[]{:S(2)}) %collective-permute-start.2) | collective-permute-done | bytes 426016 | tf_op jit(solution)/shard_map/ppermute | solution.py:98
  300.6 0.1 fusion.24
  300.7 1.5 collective-permute-start.3
  302.2 9.5 %collective-permute-done.3 = bf16[128,1664]{1,0:T(8,128)(2,1)S(1)} collective-permute-done((bf16[128,1664]{1,0:T(8,128)(2,1)S(1)}, bf16[128,1664]{1,0:T(8,128)(2,1)S(1)}, u32[]{:S(2)}, u32[]{:S(2)}) %collective-permute-start.3) | collective-permute-done | bytes 426016 | tf_op jit(solution)/shard_map/ppermute | solution.py:98
  311.8 0.1 add_convert_fusion
  311.9 0.1 collective-permute-start.4
  312.0 0.0 copy-start.1
  312.0 2.7 maximum_bitcast_fusion
  314.7 0.0 collective-permute-done.4
  314.7 1.1 maximum_select_fusion.1
  (20 shorter events, 0.0 us)
Async XLA Ops:
  7.2 10.3 %copy-start = (s32[4,4,4]{2,1,0:T(4,128)S(1)}, s32[4,4,4]{2,1,0:T(4,128)}, u32[]{:S(2)}) copy-start(s32[4,4,4]{2,1,0:T(4,128)} %param.12) | copy-start | bytes 772
  7.2 186.1 %all-gather.3.cloned.1.call-start = ((), (), s32[]{:S(2)}) async-start(), calls=%async_computation | async-start | bytes 12779520 | tf_op jit(solution)/shard_map/all_gather | solution.py:178
  10.8 2.3 copy-start.9
  10.8 5.4 %copy-start.13 = (f32[2]{0:T(128)S(1)}, f32[2]{0:T(128)}, u32[]{:S(2)}) copy-start(f32[2]{0:T(128)} %param.11) | copy-start | bytes 28
  10.8 250.6 %all-gather.5.cloned.1.call-start = ((), (), s32[]{:S(2)}) async-start(), calls=%async_computation.1 | async-start | bytes 4259840 | tf_op jit(solution)/shard_map/all_gather | solution.py:178
  13.2 22.0 %collective-permute-start = (bf16[256,1664]{1,0:T(8,128)(2,1)S(1)}, bf16[256,1664]{1,0:T(8,128)(2,1)S(1)}, u32[]{:S(2)}, u32[]{:S(2)}) collective-permute-start(bf16[256,1664]{1,0:T(8,128)(2,1)S(1)} %copy-done.9), channel_id=1, source_target_pairs={{0,4},{4,0},{1,5},{5,1},{2,6},{6,2},{3,7},{7,3},{8,12},{12,8},{9,1... | collective-permute-start | bytes 2555912 | tf_op jit(solution)/shard_map/ppermute | solution.py:142
  35.2 164.9 %copy-start.11 = (bf16[256,1664]{1,0:T(8,128)(2,1)}, bf16[256,1664]{1,0:T(8,128)(2,1)S(1)}, u32[]{:S(2)}) copy-start(bf16[256,1664]{1,0:T(8,128)(2,1)S(1)} %collective-permute-done) | copy-start | bytes 2555908
  193.3 6.8 %copy-start.7 = (bf16[2,1664,1536]{2,1,0:T(8,128)(2,1)S(1)}, bf16[2,1664,1536]{2,1,0:T(8,128)(2,1)}, u32[]{:S(2)}) copy-start(bf16[2,1664,1536]{2,1,0:T(8,128)(2,1)} %all-gather.3.cloned.1.call-done) | copy-start | bytes 30670852
  243.7 6.1 %copy-start.8 = (bf16[512,1536]{1,0:T(8,128)(2,1)S(1)}, bf16[512,1536]{1,0:T(8,128)(2,1)}, u32[]{:S(2)}) copy-start(bf16[512,1536]{1,0:T(8,128)(2,1)} %get-tuple-element.11) | copy-start | bytes 4718596
  261.4 4.7 %copy-start.2 = (bf16[2,1664,512]{2,1,0:T(8,128)(2,1)S(1)}, bf16[2,1664,512]{2,1,0:T(8,128)(2,1)}, u32[]{:S(2)}) copy-start(bf16[2,1664,512]{2,1,0:T(8,128)(2,1)} %all-gather.5.cloned.1.call-done) | copy-start | bytes 10223620
  261.4 4.7 %copy-start.10 = (bf16[256,1664]{1,0:T(8,128)(2,1)S(1)}, bf16[256,1664]{1,0:T(8,128)(2,1)}, u32[]{:S(2)}) copy-start(bf16[256,1664]{1,0:T(8,128)(2,1)} %param.7) | copy-start | bytes 2555908
  261.4 4.7 %copy-start.12 = (bf16[256,1664]{1,0:T(8,128)(2,1)S(1)}, bf16[256,1664]{1,0:T(8,128)(2,1)}, u32[]{:S(2)}) copy-start(bf16[256,1664]{1,0:T(8,128)(2,1)} %copy-done.11) | copy-start | bytes 2555908
  282.1 2.3 copy-start.3
  282.1 2.4 copy-start.6
  285.8 2.4 collective-permute-start.1
  288.5 23.4 %copy-start.4 = (bf16[1024,1536]{1,0:T(8,128)(2,1)S(1)}, bf16[1024,1536]{1,0:T(8,128)(2,1)}, u32[]{:S(2)}) copy-start(bf16[1024,1536]{1,0:T(8,128)(2,1)} %get-tuple-element.9) | copy-start | bytes 9437188
  288.5 23.4 %copy-start.5 = (bf16[1024,512]{1,0:T(8,128)(2,1)S(1)}, bf16[1024,512]{1,0:T(8,128)(2,1)}, u32[]{:S(2)}) copy-start(bf16[1024,512]{1,0:T(8,128)(2,1)} %get-tuple-element.13) | copy-start | bytes 3145732
  288.6 11.9 %collective-permute-start.2 = (bf16[128,1664]{1,0:T(8,128)(2,1)S(1)}, bf16[128,1664]{1,0:T(8,128)(2,1)S(1)}, u32[]{:S(2)}, u32[]{:S(2)}) collective-permute-start(bf16[128,1664]{1,0:T(8,128)(2,1)S(1)} %fusion.25), channel_id=1, source_target_pairs={{0,4},{4,0},{1,5},{5,1},{2,6},{6,2},{3,7},{7,3},{8,12},{12,8},{9,1... | collective-permute-start | bytes 1277960 | tf_op jit(solution)/shard_map/ppermute | solution.py:98
  300.7 11.1 %collective-permute-start.3 = (bf16[128,1664]{1,0:T(8,128)(2,1)S(1)}, bf16[128,1664]{1,0:T(8,128)(2,1)S(1)}, u32[]{:S(2)}, u32[]{:S(2)}) collective-permute-start(bf16[128,1664]{1,0:T(8,128)(2,1)S(1)} %fusion.24), channel_id=1, source_target_pairs={{0,2},{2,0},{1,3},{3,1},{4,6},{6,4},{5,7},{7,5},{8,10},{10,8},{9,1... | collective-permute-start | bytes 1277960 | tf_op jit(solution)/shard_map/ppermute | solution.py:98
  311.9 2.8 collective-permute-start.4
  312.0 3.8 %copy-start.1 = (s32[4,4,4]{2,1,0:T(4,128)S(1)}, s32[4,4,4]{2,1,0:T(4,128)}, u32[]{:S(2)}) copy-start(s32[4,4,4]{2,1,0:T(4,128)} %param.12) | copy-start | bytes 772
Sparse Core Ops, SparseCore 0:
  10.9 182.3 all-gather.2
  195.4 65.9 all-gather.4

commit v6 on v5

--- a/solution.py
+++ b/solution.py
@@ -24,9 +24,6 @@
     keys = k_ref.shape[0]
     scale = 1.0 / HD**0.5
     factor = fac_ref[0:1, 0:1]
-    q = q_ref[...]
-    k = k_ref[...]
-    v = v_ref[...]
     rows = lax.broadcasted_iota(jnp.int32, (seq, keys), 0) // TBLOCK
     image = lax.broadcasted_iota(jnp.int32, (seq, keys), 1) // IMG_TOK
     sees = jnp.full((seq, keys), -1, jnp.int32)
@@ -34,25 +31,33 @@
         sees = jnp.where(rows == b, vis_ref[sample, b], sees)
     allowed = image == sees
     valid = sees >= 0
-    scores = lax.dot_general(q, k, (((1,), (1,)), ((), ())), preferred_element_type=jnp.float32) * scale
-    exponent = jnp.where(allowed, jnp.exp(scores), 0.0)
-    total = jnp.sum(exponent, axis=-1, keepdims=True)
-    probs = jnp.where(valid, exponent / jnp.where(valid, total, 1.0), 0.0)
-    probs_b = probs.astype(jnp.bfloat16)
-    mixed = jnp.dot(probs_b, v, preferred_element_type=jnp.float32)
-    att_ref[...] = (factor * mixed).astype(att_ref.dtype)
-    head_grad = (factor * g_ref[...].astype(jnp.float32)).astype(jnp.bfloat16)
-    vg_ref[...] = lax.dot_general(
-        probs_b, head_grad, (((0,), (0,)), ((), ())), preferred_element_type=jnp.float32
-    ).astype(vg_ref.dtype)
-    prob_grad = lax.dot_general(
-        head_grad, v, (((1,), (1,)), ((), ())), preferred_element_type=jnp.float32
-    )
-    delta = jnp.sum(probs * prob_grad, axis=-1, keepdims=True)
-    score_grad = (probs * (prob_grad - delta) * scale).astype(jnp.bfloat16)
-    kg_ref[...] = lax.dot_general(
-        score_grad, q, (((0,), (0,)), ((), ())), preferred_element_type=jnp.float32
-    ).astype(kg_ref.dtype)
+    for h in range(q_ref.shape[1] // HD):
+        cols = pl.ds(h * HD, HD)
+        q = q_ref[:, cols]
+        k = k_ref[:, cols]
+        v = v_ref[:, cols]
+        scores = (
+            lax.dot_general(q, k, (((1,), (1,)), ((), ())), preferred_element_type=jnp.float32)
+            * scale
+        )
+        exponent = jnp.where(allowed, jnp.exp(scores), 0.0)
+        total = jnp.sum(exponent, axis=-1, keepdims=True)
+        probs = jnp.where(valid, exponent / jnp.where(valid, total, 1.0), 0.0)
+        probs_b = probs.astype(jnp.bfloat16)
+        mixed = jnp.dot(probs_b, v, preferred_element_type=jnp.float32)
+        att_ref[:, cols] = (factor * mixed).astype(att_ref.dtype)
+        head_grad = (factor * g_ref[:, cols].astype(jnp.float32)).astype(jnp.bfloat16)
+        vg_ref[:, cols] = lax.dot_general(
+            probs_b, head_grad, (((0,), (0,)), ((), ())), preferred_element_type=jnp.float32
+        ).astype(vg_ref.dtype)
+        prob_grad = lax.dot_general(
+            head_grad, v, (((1,), (1,)), ((), ())), preferred_element_type=jnp.float32
+        )
+        delta = jnp.sum(probs * prob_grad, axis=-1, keepdims=True)
+        score_grad = (probs * (prob_grad - delta) * scale).astype(jnp.bfloat16)
+        kg_ref[:, cols] = lax.dot_general(
+            score_grad, q, (((0,), (0,)), ((), ())), preferred_element_type=jnp.float32
+        ).astype(kg_ref.dtype)
 
 
 def attend(key_rows, value_rows, query, cotangent, factor, visible, first_head, heads):
@@ -60,13 +65,17 @@
     seq = query.shape[1] // samples
     keys = key_rows.shape[0] // samples
     fac = jnp.full((8, 128), factor, jnp.float32)
-    text_spec = pl.BlockSpec((None, seq, HD), lambda s, h, vis: (0, s, first_head + h))
-    image_spec = pl.BlockSpec((keys, HD), lambda s, h, vis: (s, h))
+    group = heads if first_head % heads == 0 else 1
+    wide = group * HD
+    text_spec = pl.BlockSpec(
+        (None, seq, wide), lambda s, h, vis: (0, s, first_head // group + h)
+    )
+    image_spec = pl.BlockSpec((keys, wide), lambda s, h, vis: (s, h))
     return pl.pallas_call(
         attend_kernel,
         grid_spec=pltpu.PrefetchScalarGridSpec(
             num_scalar_prefetch=1,
-            grid=(samples, heads),
+            grid=(samples, heads // group),
             in_specs=[
                 pl.BlockSpec((8, 128), lambda s, h, vis: (0, 0)),
                 text_spec,
@@ -75,7 +84,7 @@
                 text_spec,
             ],
             out_specs=[
-                pl.BlockSpec((seq, HD), lambda s, h, vis: (s, h)),
+                pl.BlockSpec((seq, wide), lambda s, h, vis: (s, h)),
                 image_spec,
                 image_spec,
             ],

time: 326 us -> 318 us (0.975)
  Pallas kernels: 52.9 us -> 31 us
  waiting for transfers between devices: 202 us -> 219 us
    pallas_call x2, Pallas kernels: 52.9 us -> 31 us  [attend(): pl.pallas_call(attend_kernel, grid_spec=pltpu.PrefetchScalarGridSpec(num_...]
    all_gather x2, waiting for transfers between devices: 163 us -> 180 us  [fetch(): gathered[j] = lax.all_gather(stacked, 'micro', axis=1, tiled=True)]
  transfers between devices with their start and end apart: 7 -> 7, of which waited for: 6 -> 6; matrix products, arithmetic and copies ran while one was open for 10% -> 10% of each run, Pallas kernels for 12% -> 7%
where the time goes in v6:
time: 318 us
  waiting for transfers between devices  219 us (69%)
  matrix products  34.4 us (11%)
  Pallas kernels  31 us (10%)
  between operations  14.9 us (5%)
  other arithmetic  7.17 us (2%)
  starting transfers between devices  6.36 us (2%)
  local copies, waits for them, and re-layouts  4.98 us (2%)
    all_gather x2, waiting for transfers between devices, fetch(): gathered[j] = lax.all_gather(stacked, 'micro', axis=1, tiled=True)  180 us
    pallas_call x2, Pallas kernels, attend(): pl.pallas_call(attend_kernel, grid_spec=pltpu.PrefetchScalarGridSpec(num_...  31 us
    ppermute x3, waiting for transfers between devices, exchange(): lax.ppermute(value.astype(jnp.bfloat16), axis, swap).astype(jnp.float32)  22.3 us
    ppermute x1, waiting for transfers between devices, shards(): partner = lax.ppermute(vision_tokens, 'layer', swap)  17 us
    dot_general x4, matrix products, back_product(): lax.dot_general(grad_rows, weight, (((1,), (1,)), ((), ())), preferred_el...  16.8 us
    dot_general x2, matrix products, shards(): jnp.dot(all_rows, w_value, preferred_element_type=jnp.float32)  11.4 us
  transfers between devices with their start and end apart: 7, of which 6 were waited for; matrix products, arithmetic and copies ran while one was open for 10% of the time, Pallas kernels for 7%

profile of v6, /device:TPU:0, one launch (start us, length us, event | category | flops | bytes accessed | tf_op | source)
XLA Modules:
  0.0 317.7 jit_solution(954124951662277406)
XLA Ops:
  7.2 0.0 copy-start
  7.2 0.0 all-gather.3.cloned.1.call-start
  7.2 1.9 slice_bitcast_fusion.12
  9.1 1.7 pad_maximum_fusion
  10.8 0.0 all-gather.3.cloned.1.call-update
  10.8 0.0 copy-start.9
  10.8 0.0 copy-start.13
  10.8 0.0 all-gather.5.cloned.1.call-start
  10.9 1.3 slice_bitcast_fusion.14
  12.1 1.0 pad_maximum_fusion.1
  13.1 0.0 all-gather.5.cloned.1.call-update
  13.2 3.1 collective-permute-start
  16.2 0.6 dynamic_slice.9
  17.5 0.6 dynamic-slice_bitcast_fusion.vis_ref
  18.1 17.0 %collective-permute-done = bf16[256,1664]{1,0:T(8,128)(2,1)S(1)} collective-permute-done((bf16[256,1664]{1,0:T(8,128)(2,1)S(1)}, bf16[256,1664]{1,0:T(8,128)(2,1)S(1)}, u32[]{:S(2)}, u32[]{:S(2)}) %collective-permute-start) | collective-permute-done | bytes 852000 | tf_op jit(solution)/shard_map/ppermute | solution.py:151
  35.2 158.1 %all-gather.3.cloned.1.call-done = bf16[2,1664,1536]{2,1,0:T(8,128)(2,1)} async-done(((bf16[2,416,1536]{2,1,0:T(8,128)(2,1)}), bf16[2,1664,1536]{2,1,0:T(8,128)(2,1)}) %all-gather.3.cloned.1.call-update) | async-done | bytes 10223632 | tf_op jit(solution)/shard_map/all_gather | solution.py:187
  193.3 6.8 %fusion.5.v_ref = bf16[512,1536]{1,0:T(8,128)(2,1)} fusion(bf16[2,1664,1536]{2,1,0:T(8,128)(2,1)} %all-gather.3.cloned.1.call-done, bf16[256,1664]{1,0:T(8,128)(2,1)S(1)} %collective-permute-done, bf16[256,1664]{1,0:T(8,128)(2,1)S(1)} %copy-done.9, pred[]{:T(512)S(6)} %eq.4), kind=kOutput, calls=%fused_computation.9 | convolution fusion | flops 2625699840 | bytes 8388609 | tf_op jit(solution)/shard_map/dot_general | solution.py:199
  200.1 0.0 copy-done.11
  200.1 4.2 %fusion.6.k_ref = bf16[512,1536]{1,0:T(8,128)(2,1)} fusion(bf16[2,1664,1536]{2,1,0:T(8,128)(2,1)S(1)} %copy-done.7, bf16[256,1664]{1,0:T(8,128)(2,1)S(1)} %collective-permute-done, bf16[256,1664]{1,0:T(8,128)(2,1)S(1)} %copy-done.9, pred[]{:T(512)S(6)} %eq.4), kind=kOutput, calls=%fused_computation.10 | convolution fusion | flops 2625699840 | bytes 8388609 | tf_op jit(solution)/shard_map/dot_general | solution.py:198
  204.3 0.6 broadcast_in_dim.7.fac_ref
  204.9 21.8 %shard_map.86 = (bf16[1024,1536]{1,0:T(8,128)(2,1)}, bf16[512,1536]{1,0:T(8,128)(2,1)}, bf16[512,1536]{1,0:T(8,128)(2,1)}) custom-call(s32[4,4]{1,0:T(4,128)} %dynamic-slice_bitcast_fusion.vis_ref, f32[8,128]{1,0:T(8,128)} %broadcast_in_dim.7.fac_ref, bf16[1,1024,2048]{2,1,0:T(8,128)(2,1)} %q_ref.3, bf16[512,1536]{1,0:T(8,128)(2,1)} %fusion.6.k_ref, ...), custom_call_target="tpu_custom_call" | custom-call | tf_op jit(solution)/shard_map/pallas_call | solution.py:74
  226.6 6.1 %fusion = f32[512,1664]{1,0:T(8,128)S(1)} fusion(bf16[512,1536]{1,0:T(8,128)(2,1)} %get-tuple-element.10, bf16[2,1664,1536]{2,1,0:T(8,128)(2,1)} %all-gather.3.cloned.1.call-done), kind=kOutput, calls=%fused_computation.2 | convolution fusion | flops 2617245696 | bytes 10092544 | tf_op jit(solution)/shard_map/dot_general | solution.py:101
  232.7 7.2 %fusion.4 = f32[512,1664]{1,0:T(8,128)} fusion(f32[512,1664]{1,0:T(8,128)S(1)} %fusion, bf16[512,1536]{1,0:T(8,128)(2,1)S(1)} %copy-done.8, bf16[2,1664,1536]{2,1,0:T(8,128)(2,1)} %all-gather.3.cloned.1.call-done), kind=kOutput, calls=%fused_computation.8 | convolution fusion | flops 2618097664 | bytes 13500416 | tf_op jit(solution)/shard_map/dot_general | solution.py:101
  240.0 21.4 %all-gather.5.cloned.1.call-done = bf16[2,1664,512]{2,1,0:T(8,128)(2,1)} async-done(((bf16[2,416,512]{2,1,0:T(8,128)(2,1)}), bf16[2,1664,512]{2,1,0:T(8,128)(2,1)}) %all-gather.5.cloned.1.call-update) | async-done | bytes 3407888 | tf_op jit(solution)/shard_map/all_gather | solution.py:187
  261.4 4.7 %fusion.21.v_ref = bf16[512,512]{1,0:T(8,128)(2,1)} fusion(bf16[2,1664,512]{2,1,0:T(8,128)(2,1)} %all-gather.5.cloned.1.call-done, bf16[256,1664]{1,0:T(8,128)(2,1)} %copy-done.11, bf16[256,1664]{1,0:T(8,128)(2,1)} %param.7, pred[]{:T(512)S(6)} %eq.4), kind=kOutput, calls=%fused_computation.27 | convolution fusion | flops 880345088 | bytes 3932161 | tf_op jit(solution)/shard_map/dot_general | solution.py:199
  266.1 0.0 copy-done.12
  266.1 1.9 fusion.18.k_ref
  268.0 9.2 %shard_map.87 = (bf16[1024,512]{1,0:T(8,128)(2,1)}, bf16[512,512]{1,0:T(8,128)(2,1)}, bf16[512,512]{1,0:T(8,128)(2,1)}) custom-call(s32[4,4]{1,0:T(4,128)} %dynamic-slice_bitcast_fusion.vis_ref, f32[8,128]{1,0:T(8,128)} %broadcast_in_dim.7.fac_ref, bf16[1,1024,2048]{2,1,0:T(8,128)(2,1)} %q_ref.3, bf16[512,512]{1,0:T(8,128)(2,1)} %fusion.18.k_ref, ...), custom_call_target="tpu_custom_call" | custom-call | tf_op jit(solution)/shard_map/pallas_call | solution.py:74
  277.2 2.3 fusion.10
  279.6 1.1 add_add_fusion
  280.8 0.2 select_convert_fusion
  280.9 0.1 collective-permute-start.1
  281.0 2.4 collective-permute-done.1
  283.4 0.3 convert_add_fusion
  283.7 0.0 copy-start.4
  283.7 0.0 copy-start.5
  283.7 0.1 fusion.25
  283.8 1.5 collective-permute-start.2
  285.3 10.4 %collective-permute-done.2 = bf16[128,1664]{1,0:T(8,128)(2,1)S(1)} collective-permute-done((bf16[128,1664]{1,0:T(8,128)(2,1)S(1)}, bf16[128,1664]{1,0:T(8,128)(2,1)S(1)}, u32[]{:S(2)}, u32[]{:S(2)}) %collective-permute-start.2) | collective-permute-done | bytes 426016 | tf_op jit(solution)/shard_map/ppermute | solution.py:107
  295.7 0.1 fusion.24
  295.8 1.5 collective-permute-start.3
  297.4 9.5 %collective-permute-done.3 = bf16[128,1664]{1,0:T(8,128)(2,1)S(1)} collective-permute-done((bf16[128,1664]{1,0:T(8,128)(2,1)S(1)}, bf16[128,1664]{1,0:T(8,128)(2,1)S(1)}, u32[]{:S(2)}, u32[]{:S(2)}) %collective-permute-start.3) | collective-permute-done | bytes 426016 | tf_op jit(solution)/shard_map/ppermute | solution.py:107
  306.9 0.1 add_convert_fusion
  307.0 0.1 collective-permute-start.4
  307.1 0.0 copy-start.1
  307.1 2.7 maximum_bitcast_fusion
  309.8 0.0 collective-permute-done.4
  309.8 1.1 maximum_select_fusion.1
  (20 shorter events, 0.0 us)
Async XLA Ops:
  7.2 10.3 %copy-start = (s32[4,4,4]{2,1,0:T(4,128)S(1)}, s32[4,4,4]{2,1,0:T(4,128)}, u32[]{:S(2)}) copy-start(s32[4,4,4]{2,1,0:T(4,128)} %param.12) | copy-start | bytes 772
  7.2 186.1 %all-gather.3.cloned.1.call-start = ((), (), s32[]{:S(2)}) async-start(), calls=%async_computation | async-start | bytes 12779520 | tf_op jit(solution)/shard_map/all_gather | solution.py:187
  10.8 2.3 copy-start.9
  10.8 5.4 %copy-start.13 = (f32[2]{0:T(128)S(1)}, f32[2]{0:T(128)}, u32[]{:S(2)}) copy-start(f32[2]{0:T(128)} %param.11) | copy-start | bytes 28
  10.8 250.6 %all-gather.5.cloned.1.call-start = ((), (), s32[]{:S(2)}) async-start(), calls=%async_computation.1 | async-start | bytes 4259840 | tf_op jit(solution)/shard_map/all_gather | solution.py:187
  13.2 22.0 %collective-permute-start = (bf16[256,1664]{1,0:T(8,128)(2,1)S(1)}, bf16[256,1664]{1,0:T(8,128)(2,1)S(1)}, u32[]{:S(2)}, u32[]{:S(2)}) collective-permute-start(bf16[256,1664]{1,0:T(8,128)(2,1)S(1)} %copy-done.9), channel_id=1, source_target_pairs={{0,4},{4,0},{1,5},{5,1},{2,6},{6,2},{3,7},{7,3},{8,12},{12,8},{9,1... | collective-permute-start | bytes 2555912 | tf_op jit(solution)/shard_map/ppermute | solution.py:151
  35.2 164.9 %copy-start.11 = (bf16[256,1664]{1,0:T(8,128)(2,1)}, bf16[256,1664]{1,0:T(8,128)(2,1)S(1)}, u32[]{:S(2)}) copy-start(bf16[256,1664]{1,0:T(8,128)(2,1)S(1)} %collective-permute-done) | copy-start | bytes 2555908
  193.3 6.8 %copy-start.7 = (bf16[2,1664,1536]{2,1,0:T(8,128)(2,1)S(1)}, bf16[2,1664,1536]{2,1,0:T(8,128)(2,1)}, u32[]{:S(2)}) copy-start(bf16[2,1664,1536]{2,1,0:T(8,128)(2,1)} %all-gather.3.cloned.1.call-done) | copy-start | bytes 30670852
  226.6 6.1 %copy-start.8 = (bf16[512,1536]{1,0:T(8,128)(2,1)S(1)}, bf16[512,1536]{1,0:T(8,128)(2,1)}, u32[]{:S(2)}) copy-start(bf16[512,1536]{1,0:T(8,128)(2,1)} %get-tuple-element.11) | copy-start | bytes 4718596
  261.4 4.7 %copy-start.2 = (bf16[2,1664,512]{2,1,0:T(8,128)(2,1)S(1)}, bf16[2,1664,512]{2,1,0:T(8,128)(2,1)}, u32[]{:S(2)}) copy-start(bf16[2,1664,512]{2,1,0:T(8,128)(2,1)} %all-gather.5.cloned.1.call-done) | copy-start | bytes 10223620
  261.4 4.7 %copy-start.10 = (bf16[256,1664]{1,0:T(8,128)(2,1)S(1)}, bf16[256,1664]{1,0:T(8,128)(2,1)}, u32[]{:S(2)}) copy-start(bf16[256,1664]{1,0:T(8,128)(2,1)} %param.7) | copy-start | bytes 2555908
  261.4 4.7 %copy-start.12 = (bf16[256,1664]{1,0:T(8,128)(2,1)S(1)}, bf16[256,1664]{1,0:T(8,128)(2,1)}, u32[]{:S(2)}) copy-start(bf16[256,1664]{1,0:T(8,128)(2,1)} %copy-done.11) | copy-start | bytes 2555908
  277.2 2.4 copy-start.3
  277.2 2.4 copy-start.6
  280.9 2.4 collective-permute-start.1
  283.7 23.4 %copy-start.4 = (bf16[1024,1536]{1,0:T(8,128)(2,1)S(1)}, bf16[1024,1536]{1,0:T(8,128)(2,1)}, u32[]{:S(2)}) copy-start(bf16[1024,1536]{1,0:T(8,128)(2,1)} %get-tuple-element.9) | copy-start | bytes 9437188
  283.7 23.4 %copy-start.5 = (bf16[1024,512]{1,0:T(8,128)(2,1)S(1)}, bf16[1024,512]{1,0:T(8,128)(2,1)}, u32[]{:S(2)}) copy-start(bf16[1024,512]{1,0:T(8,128)(2,1)} %get-tuple-element.13) | copy-start | bytes 3145732
  283.8 11.9 %collective-permute-start.2 = (bf16[128,1664]{1,0:T(8,128)(2,1)S(1)}, bf16[128,1664]{1,0:T(8,128)(2,1)S(1)}, u32[]{:S(2)}, u32[]{:S(2)}) collective-permute-start(bf16[128,1664]{1,0:T(8,128)(2,1)S(1)} %fusion.25), channel_id=1, source_target_pairs={{0,4},{4,0},{1,5},{5,1},{2,6},{6,2},{3,7},{7,3},{8,12},{12,8},{9,1... | collective-permute-start | bytes 1277960 | tf_op jit(solution)/shard_map/ppermute | solution.py:107
  295.8 11.1 %collective-permute-start.3 = (bf16[128,1664]{1,0:T(8,128)(2,1)S(1)}, bf16[128,1664]{1,0:T(8,128)(2,1)S(1)}, u32[]{:S(2)}, u32[]{:S(2)}) collective-permute-start(bf16[128,1664]{1,0:T(8,128)(2,1)S(1)} %fusion.24), channel_id=1, source_target_pairs={{0,2},{2,0},{1,3},{3,1},{4,6},{6,4},{5,7},{7,5},{8,10},{10,8},{9,1... | collective-permute-start | bytes 1277960 | tf_op jit(solution)/shard_map/ppermute | solution.py:107
  307.0 2.8 collective-permute-start.4
  307.1 3.8 %copy-start.1 = (s32[4,4,4]{2,1,0:T(4,128)S(1)}, s32[4,4,4]{2,1,0:T(4,128)}, u32[]{:S(2)}) copy-start(s32[4,4,4]{2,1,0:T(4,128)} %param.12) | copy-start | bytes 772
Sparse Core Ops, SparseCore 0:
  10.9 182.3 all-gather.2
  195.4 65.9 all-gather.4

commit v7 on v6

--- a/solution.py
+++ b/solution.py
@@ -116,11 +116,20 @@
     keep = jnp.where(core == 0, even, odd)
     give = jnp.where(core == 0, odd, even)
     halves = keep + exchange(give, "core", swap)
-    mine = jnp.where(layer == 0, halves[0], halves[1])
-    other = jnp.where(layer == 0, halves[1], halves[0])
+    split = (halves.shape[2] // HD * 5 // 8) * HD
+    first = halves[:, :, :split]
+    second = halves[:, :, split:]
+    mine = jnp.where(layer == 0, first[0], first[1])
+    other = jnp.where(layer == 0, first[1], first[0])
     summed = mine + exchange(other, "layer", swap)
     rounded = summed.astype(jnp.bfloat16).astype(jnp.float32)
-    total = (rounded + exchange(summed, "tx", swap)).astype(jnp.bfloat16)
+    total_first = rounded + exchange(summed, "tx", swap)
+    rounded = second.astype(jnp.bfloat16).astype(jnp.float32)
+    across = rounded + exchange(second, "tx", swap)
+    mine = jnp.where(layer == 0, across[0], across[1])
+    other = jnp.where(layer == 0, across[1], across[0])
+    total_second = mine + exchange(other, "layer", swap)
+    total = jnp.concatenate([total_first, total_second], axis=1).astype(jnp.bfloat16)
     partner = lax.ppermute(total, "core", swap)
     return jnp.where(
         core == 0,

time: 318 us -> 314 us (0.987)
  waiting for transfers between devices: 219 us -> 211 us
    ppermute x3 -> x5, waiting for transfers between devices: 22.3 us -> 14.8 us  [exchange(): lax.ppermute(value.astype(jnp.bfloat16), axis, swap).astype(jnp.float32)]
  transfers between devices with their start and end apart: 7 -> 9, of which waited for: 6 -> 7; matrix products, arithmetic and copies ran while one was open for 10% -> 10% of each run, Pallas kernels for 7% -> 7%
where the time goes in v7:
time: 314 us; the launch traced here: 313 us
  waiting for transfers between devices  211 us (67%)
  matrix products  34.4 us (11%)
  Pallas kernels  31 us (10%)
  between operations  14.9 us (5%)
  starting transfers between devices  9.42 us (3%)
  other arithmetic  7.23 us (2%)
  local copies, waits for them, and re-layouts  4.97 us (2%)
    all_gather x2, waiting for transfers between devices, fetch(): gathered[j] = lax.all_gather(stacked, 'micro', axis=1, tiled=True)  180 us
    pallas_call x2, Pallas kernels, attend(): pl.pallas_call(attend_kernel, grid_spec=pltpu.PrefetchScalarGridSpec(num_...  31 us
    ppermute x1, waiting for transfers between devices, shards(): partner = lax.ppermute(vision_tokens, 'layer', swap)  17.2 us
    dot_general x4, matrix products, back_product(): lax.dot_general(grad_rows, weight, (((1,), (1,)), ((), ())), preferred_el...  16.8 us
    ppermute x5, waiting for transfers between devices, exchange(): lax.ppermute(value.astype(jnp.bfloat16), axis, swap).astype(jnp.float32)  14.8 us
    dot_general x2, matrix products, shards(): jnp.dot(all_rows, w_value, preferred_element_type=jnp.float32)  11.5 us
  transfers between devices with their start and end apart: 9, of which 7 were waited for; matrix products, arithmetic and copies ran while one was open for 10% of the time, Pallas kernels for 7%

profile of v7, /device:TPU:0, one launch (start us, length us, event | category | flops | bytes accessed | tf_op | source)
XLA Modules:
  0.0 313.4 jit_solution(3308710449551707555)
XLA Ops:
  7.2 0.0 copy-start
  7.2 0.0 all-gather.3.cloned.1.call-start
  7.2 1.9 slice_bitcast_fusion.12
  9.1 1.7 pad_maximum_fusion
  10.8 0.0 all-gather.3.cloned.1.call-update
  10.8 0.0 copy-start.9
  10.8 0.0 copy-start.13
  10.8 0.0 all-gather.5.cloned.1.call-start
  10.9 1.3 slice_bitcast_fusion.14
  12.1 1.0 pad_maximum_fusion.1
  13.1 0.0 all-gather.5.cloned.1.call-update
  13.2 3.1 collective-permute-start
  16.2 0.6 dynamic_slice.9
  17.4 0.6 dynamic-slice_bitcast_fusion.vis_ref
  18.0 17.2 %collective-permute-done = bf16[256,1664]{1,0:T(8,128)(2,1)S(1)} collective-permute-done((bf16[256,1664]{1,0:T(8,128)(2,1)S(1)}, bf16[256,1664]{1,0:T(8,128)(2,1)S(1)}, u32[]{:S(2)}, u32[]{:S(2)}) %collective-permute-start) | collective-permute-done | bytes 852000 | tf_op jit(solution)/shard_map/ppermute | solution.py:160
  35.2 158.1 %all-gather.3.cloned.1.call-done = bf16[2,1664,1536]{2,1,0:T(8,128)(2,1)} async-done(((bf16[2,416,1536]{2,1,0:T(8,128)(2,1)}), bf16[2,1664,1536]{2,1,0:T(8,128)(2,1)}) %all-gather.3.cloned.1.call-update) | async-done | bytes 10223632 | tf_op jit(solution)/shard_map/all_gather | solution.py:196
  193.3 6.8 %fusion.5.v_ref = bf16[512,1536]{1,0:T(8,128)(2,1)} fusion(bf16[2,1664,1536]{2,1,0:T(8,128)(2,1)} %all-gather.3.cloned.1.call-done, bf16[256,1664]{1,0:T(8,128)(2,1)S(1)} %collective-permute-done, bf16[256,1664]{1,0:T(8,128)(2,1)S(1)} %copy-done.9, pred[]{:T(512)S(6)} %eq.4), kind=kOutput, calls=%fused_computation.9 | convolution fusion | flops 2625699840 | bytes 8388609 | tf_op jit(solution)/shard_map/dot_general | solution.py:208
  200.1 4.2 %fusion.6.k_ref = bf16[512,1536]{1,0:T(8,128)(2,1)} fusion(bf16[2,1664,1536]{2,1,0:T(8,128)(2,1)S(1)} %copy-done.7, bf16[256,1664]{1,0:T(8,128)(2,1)S(1)} %collective-permute-done, bf16[256,1664]{1,0:T(8,128)(2,1)S(1)} %copy-done.9, pred[]{:T(512)S(6)} %eq.4), kind=kOutput, calls=%fused_computation.10 | convolution fusion | flops 2625699840 | bytes 8388609 | tf_op jit(solution)/shard_map/dot_general | solution.py:207
  204.3 0.6 broadcast_in_dim.7.fac_ref
  204.9 21.8 %shard_map.86 = (bf16[1024,1536]{1,0:T(8,128)(2,1)}, bf16[512,1536]{1,0:T(8,128)(2,1)}, bf16[512,1536]{1,0:T(8,128)(2,1)}) custom-call(s32[4,4]{1,0:T(4,128)} %dynamic-slice_bitcast_fusion.vis_ref, f32[8,128]{1,0:T(8,128)} %broadcast_in_dim.7.fac_ref, bf16[1,1024,2048]{2,1,0:T(8,128)(2,1)} %q_ref.3, bf16[512,1536]{1,0:T(8,128)(2,1)} %fusion.6.k_ref, ...), custom_call_target="tpu_custom_call" | custom-call | tf_op jit(solution)/shard_map/pallas_call | solution.py:74
  226.7 6.1 %fusion = f32[512,1664]{1,0:T(8,128)S(1)} fusion(bf16[512,1536]{1,0:T(8,128)(2,1)} %get-tuple-element.10, bf16[2,1664,1536]{2,1,0:T(8,128)(2,1)} %all-gather.3.cloned.1.call-done), kind=kOutput, calls=%fused_computation.2 | convolution fusion | flops 2617245696 | bytes 10092544 | tf_op jit(solution)/shard_map/dot_general | solution.py:101
  232.8 7.2 %fusion.4 = f32[512,1664]{1,0:T(8,128)} fusion(f32[512,1664]{1,0:T(8,128)S(1)} %fusion, bf16[512,1536]{1,0:T(8,128)(2,1)S(1)} %copy-done.8, bf16[2,1664,1536]{2,1,0:T(8,128)(2,1)} %all-gather.3.cloned.1.call-done), kind=kOutput, calls=%fused_computation.8 | convolution fusion | flops 2618097664 | bytes 13500416 | tf_op jit(solution)/shard_map/dot_general | solution.py:101
  240.0 21.4 %all-gather.5.cloned.1.call-done = bf16[2,1664,512]{2,1,0:T(8,128)(2,1)} async-done(((bf16[2,416,512]{2,1,0:T(8,128)(2,1)}), bf16[2,1664,512]{2,1,0:T(8,128)(2,1)}) %all-gather.5.cloned.1.call-update) | async-done | bytes 3407888 | tf_op jit(solution)/shard_map/all_gather | solution.py:196
  261.4 4.7 %fusion.21.v_ref = bf16[512,512]{1,0:T(8,128)(2,1)} fusion(bf16[2,1664,512]{2,1,0:T(8,128)(2,1)} %all-gather.5.cloned.1.call-done, bf16[256,1664]{1,0:T(8,128)(2,1)} %copy-done.11, bf16[256,1664]{1,0:T(8,128)(2,1)} %param.7, pred[]{:T(512)S(6)} %eq.4), kind=kOutput, calls=%fused_computation.27 | convolution fusion | flops 880345088 | bytes 3932161 | tf_op jit(solution)/shard_map/dot_general | solution.py:208
  266.1 1.9 fusion.18.k_ref
  268.0 9.2 %shard_map.87 = (bf16[1024,512]{1,0:T(8,128)(2,1)}, bf16[512,512]{1,0:T(8,128)(2,1)}, bf16[512,512]{1,0:T(8,128)(2,1)}) custom-call(s32[4,4]{1,0:T(4,128)} %dynamic-slice_bitcast_fusion.vis_ref, f32[8,128]{1,0:T(8,128)} %broadcast_in_dim.7.fac_ref, bf16[1,1024,2048]{2,1,0:T(8,128)(2,1)} %q_ref.3, bf16[512,512]{1,0:T(8,128)(2,1)} %fusion.18.k_ref, ...), custom_call_target="tpu_custom_call" | custom-call | tf_op jit(solution)/shard_map/pallas_call | solution.py:74
  277.3 2.3 fusion.10
  279.6 1.2 add_add_fusion
  280.8 0.2 select_convert_fusion
  281.0 0.1 collective-permute-start.1
  281.0 2.4 collective-permute-done.1
  283.4 0.3 convert_add_fusion
  283.7 1.5 collective-permute-start.4
  285.3 1.5 collective-permute-start.2
  286.9 6.7 %collective-permute-done.4 = bf16[2,128,640]{2,1,0:T(8,128)(2,1)S(1)} collective-permute-done((bf16[2,128,640]{2,1,0:T(8,128)(2,1)S(1)}, bf16[2,128,640]{2,1,0:T(8,128)(2,1)S(1)}, u32[]{:S(2)}, u32[]{:S(2)}) %collective-permute-start.4) | collective-permute-done | bytes 327712 | tf_op jit(solution)/shard_map/ppermute | solution.py:107
  293.6 0.1 convert_add_fusion.1
  293.7 1.5 collective-permute-start.5
  295.2 0.0 collective-permute-done.2
  295.2 0.1 fusion.24
  295.3 1.5 collective-permute-start.3
  296.9 2.3 collective-permute-done.5
  299.2 3.4 %collective-permute-done.3 = bf16[128,1024]{1,0:T(8,128)(2,1)S(1)} collective-permute-done((bf16[128,1024]{1,0:T(8,128)(2,1)S(1)}, bf16[128,1024]{1,0:T(8,128)(2,1)S(1)}, u32[]{:S(2)}, u32[]{:S(2)}) %collective-permute-start.3) | collective-permute-done | bytes 262176 | tf_op jit(solution)/shard_map/ppermute | solution.py:107
  302.6 0.1 add_convert_fusion
  302.7 0.1 collective-permute-start.6
  302.8 0.0 copy-start.1
  302.8 2.7 maximum_bitcast_fusion
  305.5 0.0 collective-permute-done.6
  305.5 1.1 maximum_select_fusion.1
  (29 shorter events, 0.2 us)
Async XLA Ops:
  7.2 10.2 %copy-start = (s32[4,4,4]{2,1,0:T(4,128)S(1)}, s32[4,4,4]{2,1,0:T(4,128)}, u32[]{:S(2)}) copy-start(s32[4,4,4]{2,1,0:T(4,128)} %param.12) | copy-start | bytes 772
  7.2 186.1 %all-gather.3.cloned.1.call-start = ((), (), s32[]{:S(2)}) async-start(), calls=%async_computation | async-start | bytes 12779520 | tf_op jit(solution)/shard_map/all_gather | solution.py:196
  10.8 2.3 copy-start.9
  10.8 5.4 %copy-start.13 = (f32[2]{0:T(128)S(1)}, f32[2]{0:T(128)}, u32[]{:S(2)}) copy-start(f32[2]{0:T(128)} %param.11) | copy-start | bytes 28
  10.8 250.6 %all-gather.5.cloned.1.call-start = ((), (), s32[]{:S(2)}) async-start(), calls=%async_computation.1 | async-start | bytes 4259840 | tf_op jit(solution)/shard_map/all_gather | solution.py:196
  13.2 22.0 %collective-permute-start = (bf16[256,1664]{1,0:T(8,128)(2,1)S(1)}, bf16[256,1664]{1,0:T(8,128)(2,1)S(1)}, u32[]{:S(2)}, u32[]{:S(2)}) collective-permute-start(bf16[256,1664]{1,0:T(8,128)(2,1)S(1)} %copy-done.9), channel_id=1, source_target_pairs={{0,4},{4,0},{1,5},{5,1},{2,6},{6,2},{3,7},{7,3},{8,12},{12,8},{9,1... | collective-permute-start | bytes 2555912 | tf_op jit(solution)/shard_map/ppermute | solution.py:160
  35.2 164.9 %copy-start.11 = (bf16[256,1664]{1,0:T(8,128)(2,1)}, bf16[256,1664]{1,0:T(8,128)(2,1)S(1)}, u32[]{:S(2)}) copy-start(bf16[256,1664]{1,0:T(8,128)(2,1)S(1)} %collective-permute-done) | copy-start | bytes 2555908
  193.3 6.8 %copy-start.7 = (bf16[2,1664,1536]{2,1,0:T(8,128)(2,1)S(1)}, bf16[2,1664,1536]{2,1,0:T(8,128)(2,1)}, u32[]{:S(2)}) copy-start(bf16[2,1664,1536]{2,1,0:T(8,128)(2,1)} %all-gather.3.cloned.1.call-done) | copy-start | bytes 30670852
  226.7 6.1 %copy-start.8 = (bf16[512,1536]{1,0:T(8,128)(2,1)S(1)}, bf16[512,1536]{1,0:T(8,128)(2,1)}, u32[]{:S(2)}) copy-start(bf16[512,1536]{1,0:T(8,128)(2,1)} %get-tuple-element.11) | copy-start | bytes 4718596
  261.4 4.7 %copy-start.2 = (bf16[2,1664,512]{2,1,0:T(8,128)(2,1)S(1)}, bf16[2,1664,512]{2,1,0:T(8,128)(2,1)}, u32[]{:S(2)}) copy-start(bf16[2,1664,512]{2,1,0:T(8,128)(2,1)} %all-gather.5.cloned.1.call-done) | copy-start | bytes 10223620
  261.4 4.7 %copy-start.10 = (bf16[256,1664]{1,0:T(8,128)(2,1)S(1)}, bf16[256,1664]{1,0:T(8,128)(2,1)}, u32[]{:S(2)}) copy-start(bf16[256,1664]{1,0:T(8,128)(2,1)} %param.7) | copy-start | bytes 2555908
  261.4 4.7 %copy-start.12 = (bf16[256,1664]{1,0:T(8,128)(2,1)S(1)}, bf16[256,1664]{1,0:T(8,128)(2,1)}, u32[]{:S(2)}) copy-start(bf16[256,1664]{1,0:T(8,128)(2,1)} %copy-done.11) | copy-start | bytes 2555908
  277.3 2.3 copy-start.3
  277.3 2.4 copy-start.6
  281.0 2.4 collective-permute-start.1
  283.7 9.8 %collective-permute-start.4 = (bf16[2,128,640]{2,1,0:T(8,128)(2,1)S(1)}, bf16[2,128,640]{2,1,0:T(8,128)(2,1)S(1)}, u32[]{:S(2)}, u32[]{:S(2)}) collective-permute-start(bf16[2,128,640]{2,1,0:T(8,128)(2,1)S(1)} %slice.132), channel_id=1, source_target_pairs={{0,2},{2,0},{1,3},{3,1},{4,6},{6,4},{5,7},{7,5},{8,10},{10,8},{9,1... | collective-permute-start | bytes 983048 | tf_op jit(solution)/shard_map/ppermute | solution.py:107
  285.3 9.9 %collective-permute-start.2 = (bf16[128,1024]{1,0:T(8,128)(2,1)S(1)}, bf16[128,1024]{1,0:T(8,128)(2,1)S(1)}, u32[]{:S(2)}, u32[]{:S(2)}) collective-permute-start(bf16[128,1024]{1,0:T(8,128)(2,1)S(1)} %fusion.26), channel_id=1, source_target_pairs={{0,4},{4,0},{1,5},{5,1},{2,6},{6,2},{3,7},{7,3},{8,12},{12,8},{9,1... | collective-permute-start | bytes 786440 | tf_op jit(solution)/shard_map/ppermute | solution.py:107
  293.6 9.2 %copy-start.4 = (bf16[1024,1536]{1,0:T(8,128)(2,1)S(1)}, bf16[1024,1536]{1,0:T(8,128)(2,1)}, u32[]{:S(2)}) copy-start(bf16[1024,1536]{1,0:T(8,128)(2,1)} %get-tuple-element.9) | copy-start | bytes 9437188
  293.6 9.2 %copy-start.5 = (bf16[1024,512]{1,0:T(8,128)(2,1)S(1)}, bf16[1024,512]{1,0:T(8,128)(2,1)}, u32[]{:S(2)}) copy-start(bf16[1024,512]{1,0:T(8,128)(2,1)} %get-tuple-element.13) | copy-start | bytes 3145732
  293.7 5.5 %collective-permute-start.5 = (bf16[128,640]{1,0:T(8,128)(2,1)S(1)}, bf16[128,640]{1,0:T(8,128)(2,1)S(1)}, u32[]{:S(2)}, u32[]{:S(2)}) collective-permute-start(bf16[128,640]{1,0:T(8,128)(2,1)S(1)} %fusion.27), channel_id=1, source_target_pairs={{0,4},{4,0},{1,5},{5,1},{2,6},{6,2},{3,7},{7,3},{8,12},{12,8},{9,1... | collective-permute-start | bytes 491528 | tf_op jit(solution)/shard_map/ppermute | solution.py:107
  295.3 7.3 %collective-permute-start.3 = (bf16[128,1024]{1,0:T(8,128)(2,1)S(1)}, bf16[128,1024]{1,0:T(8,128)(2,1)S(1)}, u32[]{:S(2)}, u32[]{:S(2)}) collective-permute-start(bf16[128,1024]{1,0:T(8,128)(2,1)S(1)} %fusion.24), channel_id=1, source_target_pairs={{0,2},{2,0},{1,3},{3,1},{4,6},{6,4},{5,7},{7,5},{8,10},{10,8},{9,1... | collective-permute-start | bytes 786440 | tf_op jit(solution)/shard_map/ppermute | solution.py:107
  302.7 2.8 collective-permute-start.6
  302.8 3.8 %copy-start.1 = (s32[4,4,4]{2,1,0:T(4,128)S(1)}, s32[4,4,4]{2,1,0:T(4,128)}, u32[]{:S(2)}) copy-start(s32[4,4,4]{2,1,0:T(4,128)} %param.12) | copy-start | bytes 772
Sparse Core Ops, SparseCore 0:
  10.9 182.3 all-gather.2
  195.4 65.9 all-gather.4

commit v8 on v7

--- a/solution.py
+++ b/solution.py
@@ -204,10 +204,11 @@
             stacked, _ = lax.optimization_barrier((stacked, term))
         w_key = stacked[0]
         w_value = stacked[1]
-        key_rows = jnp.dot(all_rows, w_key, preferred_element_type=jnp.float32).astype(jnp.bfloat16)
-        value_rows = jnp.dot(all_rows, w_value, preferred_element_type=jnp.float32).astype(
-            jnp.bfloat16
-        )
+        projected = jnp.einsum(
+            "td,sdc->stc", all_rows, stacked, preferred_element_type=jnp.float32
+        ).astype(jnp.bfloat16)
+        key_rows = projected[0]
+        value_rows = projected[1]
         attended, key_grad, value_grad = attend(
             key_rows,
             value_rows,

time: 314 us -> 312 us (level)
  matrix products: 34.4 us -> 29.4 us
    dot_general x4 -> x2, matrix products: 17.6 us -> 12.6 us  [shards(): jnp.einsum('td,sdc->stc', all_rows, stacked, preferred_element_type=jnp.f...]
where the time goes in v8:
time: 312 us
  waiting for transfers between devices  212 us (68%)
  Pallas kernels  31.1 us (10%)
  matrix products  29.4 us (9%)
  between operations  15 us (5%)
  starting transfers between devices  9.42 us (3%)
  local copies, waits for them, and re-layouts  7.93 us (3%)
  other arithmetic  7.23 us (2%)
    all_gather x2, waiting for transfers between devices, fetch(): gathered[j] = lax.all_gather(stacked, 'micro', axis=1, tiled=True)  180 us
    pallas_call x2, Pallas kernels, attend(): pl.pallas_call(attend_kernel, grid_spec=pltpu.PrefetchScalarGridSpec(num_...  31.1 us
    ppermute x1, waiting for transfers between devices, shards(): partner = lax.ppermute(vision_tokens, 'layer', swap)  17.1 us
    dot_general x4, matrix products, back_product(): lax.dot_general(grad_rows, weight, (((1,), (1,)), ((), ())), preferred_el...  16.9 us
    ppermute x5, waiting for transfers between devices, exchange(): lax.ppermute(value.astype(jnp.bfloat16), axis, swap).astype(jnp.float32)  14.8 us
    dot_general x2, matrix products, shards(): jnp.einsum('td,sdc->stc', all_rows, stacked, preferred_element_type=jnp.f...  12.6 us
  transfers between devices with their start and end apart: 9, of which 7 were waited for; matrix products, arithmetic and copies ran while one was open for 10% of the time, Pallas kernels for 7%

profile of v8, /device:TPU:0, one launch (start us, length us, event | category | flops | bytes accessed | tf_op | source)
XLA Modules:
  0.0 312.2 jit_solution(5650106738413195816)
XLA Ops:
  7.2 0.0 copy-start
  7.2 0.0 all-gather.3.cloned.1.call-start
  7.2 1.9 slice_bitcast_fusion.8
  9.1 1.7 pad_maximum_fusion
  10.8 0.0 all-gather.3.cloned.1.call-update
  10.8 0.0 copy-start.8
  10.8 0.0 copy-start.9
  10.8 0.0 all-gather.5.cloned.1.call-start
  10.9 1.3 slice_bitcast_fusion.12
  12.1 1.0 pad_maximum_fusion.1
  13.1 0.0 all-gather.5.cloned.1.call-update
  13.2 3.1 collective-permute-start
  16.2 0.6 dynamic_slice.9
  17.5 0.6 dynamic-slice_bitcast_fusion.vis_ref
  18.1 17.1 %collective-permute-done = bf16[256,1664]{1,0:T(8,128)(2,1)S(1)} collective-permute-done((bf16[256,1664]{1,0:T(8,128)(2,1)S(1)}, bf16[256,1664]{1,0:T(8,128)(2,1)S(1)}, u32[]{:S(2)}, u32[]{:S(2)}) %collective-permute-start) | collective-permute-done | bytes 852000 | tf_op jit(solution)/shard_map/ppermute | solution.py:160
  35.2 158.1 %all-gather.3.cloned.1.call-done = bf16[2,1664,1536]{2,1,0:T(8,128)(2,1)} async-done(((bf16[2,416,1536]{2,1,0:T(8,128)(2,1)}), bf16[2,1664,1536]{2,1,0:T(8,128)(2,1)}) %all-gather.3.cloned.1.call-update) | async-done | bytes 10223632 | tf_op jit(solution)/shard_map/all_gather | solution.py:196
  193.3 8.6 %fusion.2 = bf16[2,512,1536]{2,1,0:T(8,128)(2,1)S(1)} fusion(bf16[2,1664,1536]{2,1,0:T(8,128)(2,1)} %all-gather.3.cloned.1.call-done, bf16[256,1664]{1,0:T(8,128)(2,1)S(1)} %collective-permute-done, bf16[256,1664]{1,0:T(8,128)(2,1)S(1)} %copy-done.8, pred[]{:T(512)S(6)} %eq.4), kind=kOutput, calls=%fused_computation.7 | convolution fusion | flops 5243731968 | bytes 15073281 | tf_op jit(solution)/shard_map/td,sdc->stc/dot_general | solution.py:207
  201.9 1.9 slice_bitcast_fusion.6
  203.8 0.6 broadcast_in_dim.7.fac_ref
  204.4 21.6 %shard_map.86 = (bf16[1024,1536]{1,0:T(8,128)(2,1)}, bf16[512,1536]{1,0:T(8,128)(2,1)}, bf16[512,1536]{1,0:T(8,128)(2,1)}) custom-call(s32[4,4]{1,0:T(4,128)} %dynamic-slice_bitcast_fusion.vis_ref, f32[8,128]{1,0:T(8,128)} %broadcast_in_dim.7.fac_ref, bf16[1,1024,2048]{2,1,0:T(8,128)(2,1)} %q_ref.3, bf16[512,1536]{1,0:T(8,128)(2,1)} %get-tuple-element.17.k_ref, ...), custom_call_target="tpu_custom_call" | custom-call | tf_op jit(solution)/shard_map/pallas_call | solution.py:74
  225.9 6.1 %fusion = f32[512,1664]{1,0:T(8,128)S(1)} fusion(bf16[512,1536]{1,0:T(8,128)(2,1)} %get-tuple-element.11, bf16[2,1664,1536]{2,1,0:T(8,128)(2,1)} %all-gather.3.cloned.1.call-done), kind=kOutput, calls=%fused_computation.1 | convolution fusion | flops 2617245696 | bytes 10092544 | tf_op jit(solution)/shard_map/dot_general | solution.py:101
  232.1 7.2 %fusion.3 = f32[512,1664]{1,0:T(8,128)} fusion(f32[512,1664]{1,0:T(8,128)S(1)} %fusion, bf16[512,1536]{1,0:T(8,128)(2,1)S(1)} %copy-done.7, bf16[2,1664,1536]{2,1,0:T(8,128)(2,1)} %all-gather.3.cloned.1.call-done), kind=kOutput, calls=%fused_computation.8 | convolution fusion | flops 2618097664 | bytes 13500416 | tf_op jit(solution)/shard_map/dot_general | solution.py:101
  239.3 22.1 %all-gather.5.cloned.1.call-done = bf16[2,1664,512]{2,1,0:T(8,128)(2,1)} async-done(((bf16[2,416,512]{2,1,0:T(8,128)(2,1)}), bf16[2,1664,512]{2,1,0:T(8,128)(2,1)}) %all-gather.5.cloned.1.call-update) | async-done | bytes 3407888 | tf_op jit(solution)/shard_map/all_gather | solution.py:196
  261.4 4.0 %fusion.10 = bf16[2,512,512]{2,1,0:T(8,128)(2,1)S(1)} fusion(bf16[2,1664,512]{2,1,0:T(8,128)(2,1)} %all-gather.5.cloned.1.call-done, bf16[256,1664]{1,0:T(8,128)(2,1)S(1)} %collective-permute-done, bf16[256,1664]{1,0:T(8,128)(2,1)S(1)} %copy-done.8, pred[]{:T(512)S(6)} %eq.4), kind=kOutput, calls=%fused_computation.22 | convolution fusion | flops 1753022464 | bytes 6160385 | tf_op jit(solution)/shard_map/td,sdc->stc/dot_general | solution.py:207
  265.4 1.0 slice_bitcast_fusion.10
  266.5 9.6 %shard_map.87 = (bf16[1024,512]{1,0:T(8,128)(2,1)}, bf16[512,512]{1,0:T(8,128)(2,1)}, bf16[512,512]{1,0:T(8,128)(2,1)}) custom-call(s32[4,4]{1,0:T(4,128)} %dynamic-slice_bitcast_fusion.vis_ref, f32[8,128]{1,0:T(8,128)} %broadcast_in_dim.7.fac_ref, bf16[1,1024,2048]{2,1,0:T(8,128)(2,1)} %q_ref.3, bf16[512,512]{1,0:T(8,128)(2,1)} %get-tuple-element.19.k_ref, ...), custom_call_target="tpu_custom_call" | custom-call | tf_op jit(solution)/shard_map/pallas_call | solution.py:74
  276.1 2.3 fusion.6
  278.4 1.2 add_add_fusion
  279.6 0.2 select_convert_fusion
  279.8 0.1 collective-permute-start.1
  279.8 2.4 collective-permute-done.1
  282.2 0.3 convert_add_fusion
  282.5 1.5 collective-permute-start.4
  284.1 1.5 collective-permute-start.2
  285.7 6.7 %collective-permute-done.4 = bf16[2,128,640]{2,1,0:T(8,128)(2,1)S(1)} collective-permute-done((bf16[2,128,640]{2,1,0:T(8,128)(2,1)S(1)}, bf16[2,128,640]{2,1,0:T(8,128)(2,1)S(1)}, u32[]{:S(2)}, u32[]{:S(2)}) %collective-permute-start.4) | collective-permute-done | bytes 327712 | tf_op jit(solution)/shard_map/ppermute | solution.py:107
  292.3 0.1 convert_add_fusion.1
  292.5 1.5 collective-permute-start.5
  294.0 0.0 collective-permute-done.2
  294.0 0.1 fusion.13
  294.1 1.5 collective-permute-start.3
  295.7 2.3 collective-permute-done.5
  298.0 3.4 %collective-permute-done.3 = bf16[128,1024]{1,0:T(8,128)(2,1)S(1)} collective-permute-done((bf16[128,1024]{1,0:T(8,128)(2,1)S(1)}, bf16[128,1024]{1,0:T(8,128)(2,1)S(1)}, u32[]{:S(2)}, u32[]{:S(2)}) %collective-permute-start.3) | collective-permute-done | bytes 262176 | tf_op jit(solution)/shard_map/ppermute | solution.py:107
  301.4 0.1 add_convert_fusion
  301.5 0.1 collective-permute-start.6
  301.6 0.0 copy-start.1
  301.6 2.7 maximum_bitcast_fusion
  304.3 0.0 collective-permute-done.6
  304.3 1.1 maximum_select_fusion.1
  (21 shorter events, 0.2 us)
Async XLA Ops:
  7.2 10.3 %copy-start = (s32[4,4,4]{2,1,0:T(4,128)S(1)}, s32[4,4,4]{2,1,0:T(4,128)}, u32[]{:S(2)}) copy-start(s32[4,4,4]{2,1,0:T(4,128)} %param.12) | copy-start | bytes 772
  7.2 186.1 %all-gather.3.cloned.1.call-start = ((), (), s32[]{:S(2)}) async-start(), calls=%async_computation | async-start | bytes 12779520 | tf_op jit(solution)/shard_map/all_gather | solution.py:196
  10.8 2.3 copy-start.8
  10.8 5.4 %copy-start.9 = (f32[2]{0:T(128)S(1)}, f32[2]{0:T(128)}, u32[]{:S(2)}) copy-start(f32[2]{0:T(128)} %param.11) | copy-start | bytes 28
  10.8 250.6 %all-gather.5.cloned.1.call-start = ((), (), s32[]{:S(2)}) async-start(), calls=%async_computation.1 | async-start | bytes 4259840 | tf_op jit(solution)/shard_map/all_gather | solution.py:196
  13.2 22.0 %collective-permute-start = (bf16[256,1664]{1,0:T(8,128)(2,1)S(1)}, bf16[256,1664]{1,0:T(8,128)(2,1)S(1)}, u32[]{:S(2)}, u32[]{:S(2)}) collective-permute-start(bf16[256,1664]{1,0:T(8,128)(2,1)S(1)} %copy-done.8), channel_id=1, source_target_pairs={{0,4},{4,0},{1,5},{5,1},{2,6},{6,2},{3,7},{7,3},{8,12},{12,8},{9,1... | collective-permute-start | bytes 2555912 | tf_op jit(solution)/shard_map/ppermute | solution.py:160
  225.9 6.1 %copy-start.7 = (bf16[512,1536]{1,0:T(8,128)(2,1)S(1)}, bf16[512,1536]{1,0:T(8,128)(2,1)}, u32[]{:S(2)}) copy-start(bf16[512,1536]{1,0:T(8,128)(2,1)} %get-tuple-element.10) | copy-start | bytes 4718596
  266.5 9.6 %copy-start.2 = (bf16[2,1664,512]{2,1,0:T(8,128)(2,1)S(1)}, bf16[2,1664,512]{2,1,0:T(8,128)(2,1)}, u32[]{:S(2)}) copy-start(bf16[2,1664,512]{2,1,0:T(8,128)(2,1)} %all-gather.5.cloned.1.call-done) | copy-start | bytes 10223620
  276.1 2.4 copy-start.3
  276.1 2.4 copy-start.6
  279.8 2.4 collective-permute-start.1
  282.5 9.8 %collective-permute-start.4 = (bf16[2,128,640]{2,1,0:T(8,128)(2,1)S(1)}, bf16[2,128,640]{2,1,0:T(8,128)(2,1)S(1)}, u32[]{:S(2)}, u32[]{:S(2)}) collective-permute-start(bf16[2,128,640]{2,1,0:T(8,128)(2,1)S(1)} %slice.138), channel_id=1, source_target_pairs={{0,2},{2,0},{1,3},{3,1},{4,6},{6,4},{5,7},{7,5},{8,10},{10,8},{9,1... | collective-permute-start | bytes 983048 | tf_op jit(solution)/shard_map/ppermute | solution.py:107
  284.1 9.9 %collective-permute-start.2 = (bf16[128,1024]{1,0:T(8,128)(2,1)S(1)}, bf16[128,1024]{1,0:T(8,128)(2,1)S(1)}, u32[]{:S(2)}, u32[]{:S(2)}) collective-permute-start(bf16[128,1024]{1,0:T(8,128)(2,1)S(1)} %fusion.15), channel_id=1, source_target_pairs={{0,4},{4,0},{1,5},{5,1},{2,6},{6,2},{3,7},{7,3},{8,12},{12,8},{9,1... | collective-permute-start | bytes 786440 | tf_op jit(solution)/shard_map/ppermute | solution.py:107
  292.4 9.2 %copy-start.4 = (bf16[1024,1536]{1,0:T(8,128)(2,1)S(1)}, bf16[1024,1536]{1,0:T(8,128)(2,1)}, u32[]{:S(2)}) copy-start(bf16[1024,1536]{1,0:T(8,128)(2,1)} %get-tuple-element.9) | copy-start | bytes 9437188
  292.4 9.2 %copy-start.5 = (bf16[1024,512]{1,0:T(8,128)(2,1)S(1)}, bf16[1024,512]{1,0:T(8,128)(2,1)}, u32[]{:S(2)}) copy-start(bf16[1024,512]{1,0:T(8,128)(2,1)} %get-tuple-element.13) | copy-start | bytes 3145732
  292.5 5.5 %collective-permute-start.5 = (bf16[128,640]{1,0:T(8,128)(2,1)S(1)}, bf16[128,640]{1,0:T(8,128)(2,1)S(1)}, u32[]{:S(2)}, u32[]{:S(2)}) collective-permute-start(bf16[128,640]{1,0:T(8,128)(2,1)S(1)} %fusion.16), channel_id=1, source_target_pairs={{0,4},{4,0},{1,5},{5,1},{2,6},{6,2},{3,7},{7,3},{8,12},{12,8},{9,1... | collective-permute-start | bytes 491528 | tf_op jit(solution)/shard_map/ppermute | solution.py:107
  294.1 7.3 %collective-permute-start.3 = (bf16[128,1024]{1,0:T(8,128)(2,1)S(1)}, bf16[128,1024]{1,0:T(8,128)(2,1)S(1)}, u32[]{:S(2)}, u32[]{:S(2)}) collective-permute-start(bf16[128,1024]{1,0:T(8,128)(2,1)S(1)} %fusion.13), channel_id=1, source_target_pairs={{0,2},{2,0},{1,3},{3,1},{4,6},{6,4},{5,7},{7,5},{8,10},{10,8},{9,1... | collective-permute-start | bytes 786440 | tf_op jit(solution)/shard_map/ppermute | solution.py:107
  301.5 2.8 collective-permute-start.6
  301.6 3.8 %copy-start.1 = (s32[4,4,4]{2,1,0:T(4,128)S(1)}, s32[4,4,4]{2,1,0:T(4,128)}, u32[]{:S(2)}) copy-start(s32[4,4,4]{2,1,0:T(4,128)} %param.12) | copy-start | bytes 772
Sparse Core Ops, SparseCore 0:
  10.9 182.3 all-gather.2
  195.4 65.9 all-gather.4

commit v9 on v8

--- a/solution.py
+++ b/solution.py
@@ -18,7 +18,8 @@
 RELAY = False
 
 
-def attend_kernel(vis_ref, fac_ref, q_ref, k_ref, v_ref, g_ref, att_ref, kg_ref, vg_ref):
+def attend_kernel(vis_ref, fac_ref, q_ref, k_ref, v_ref, g_ref, *rest):
+    att_ref, kg_ref, vg_ref = rest[-3:]
     sample = pl.program_id(0)
     seq = q_ref.shape[0]
     keys = k_ref.shape[0]
@@ -60,7 +61,7 @@
         ).astype(kg_ref.dtype)
 
 
-def attend(key_rows, value_rows, query, cotangent, factor, visible, first_head, heads):
+def attend(key_rows, value_rows, query, cotangent, factor, visible, first_head, heads, previous):
     samples = visible.shape[0]
     seq = query.shape[1] // samples
     keys = key_rows.shape[0] // samples
@@ -82,19 +83,21 @@
                 image_spec,
                 image_spec,
                 text_spec,
-            ],
+            ]
+            + [pl.BlockSpec(memory_space=pl.ANY)] * len(previous),
             out_specs=[
-                pl.BlockSpec((seq, wide), lambda s, h, vis: (s, h)),
+                pl.BlockSpec((seq, wide), lambda s, h, vis: (s, first_head // group + h)),
                 image_spec,
                 image_spec,
             ],
         ),
         out_shape=[
-            jax.ShapeDtypeStruct((query.shape[1], heads * HD), jnp.bfloat16),
+            jax.ShapeDtypeStruct(query.shape[1:], jnp.bfloat16),
             jax.ShapeDtypeStruct(key_rows.shape, jnp.bfloat16),
             jax.ShapeDtypeStruct(key_rows.shape, jnp.bfloat16),
         ],
-    )(visible, fac, query, key_rows, value_rows, cotangent)
+        input_output_aliases={6: 0} if previous else {},
+    )(visible, fac, query, key_rows, value_rows, cotangent, *previous)
 
 
 def back_product(grad_rows, weight):
@@ -218,13 +221,14 @@
             own_visible,
             starts[j] // HD,
             sizes[j] // HD,
-        )
-        pieces.append(attended)
+            pieces[-1:],
+        )
+        pieces = [attended]
         part = back_product(key_grad, w_key) + back_product(value_grad, w_value)
         term = part if term is None else term + part
         if j + AHEAD < chunks:
             fetch(j + AHEAD, term)
-    attended = jnp.concatenate(pieces, axis=1)
+    attended = pieces[0]
     if paired and lax.axis_size("tx") == 2 and lax.axis_size("core") == 2:
         owned = chip_reduce(term, layer, swap)
     else:

time: 312 us -> 312 us (level)
  transfers between devices with their start and end apart: 9 -> 9, of which waited for: 7 -> 8; matrix products, arithmetic and copies ran while one was open for 10% -> 9% of each run, Pallas kernels for 7% -> 7%
where the time goes in v9:
time: 312 us; the launch traced here: 311 us
  waiting for transfers between devices  214 us (69%)
  Pallas kernels  31.1 us (10%)
  matrix products  29.4 us (9%)
  between operations  15 us (5%)
  starting transfers between devices  9.34 us (3%)
  local copies, waits for them, and re-layouts  8.34 us (3%)
  other arithmetic  4.58 us (1%)
    all_gather x2, waiting for transfers between devices, fetch(): gathered[j] = lax.all_gather(stacked, 'micro', axis=1, tiled=True)  180 us
    pallas_call x2, Pallas kernels, attend(): pl.pallas_call(attend_kernel, grid_spec=pltpu.PrefetchScalarGridSpec(num_...  31.1 us
    ppermute x1, waiting for transfers between devices, shards(): partner = lax.ppermute(vision_tokens, 'layer', swap)  16.9 us
    dot_general x4, matrix products, back_product(): lax.dot_general(grad_rows, weight, (((1,), (1,)), ((), ())), preferred_el...  16.8 us
    ppermute x5, waiting for transfers between devices, exchange(): lax.ppermute(value.astype(jnp.bfloat16), axis, swap).astype(jnp.float32)  14.8 us
    dot_general x2, matrix products, shards(): jnp.einsum('td,sdc->stc', all_rows, stacked, preferred_element_type=jnp.f...  12.6 us
  transfers between devices with their start and end apart: 9, of which 8 were waited for; matrix products, arithmetic and copies ran while one was open for 9% of the time, Pallas kernels for 7%

profile of v9, /device:TPU:0, one launch (start us, length us, event | category | flops | bytes accessed | tf_op | source)
XLA Modules:
  0.0 311.2 jit_solution(3423038125146583711)
XLA Ops:
  7.2 0.0 copy-start
  7.2 0.0 all-gather.5.cloned.1.call-start
  7.2 1.9 slice_bitcast_fusion.8
  9.1 1.7 pad_maximum_fusion
  10.8 0.0 all-gather.5.cloned.1.call-update
  10.8 0.0 all-gather.3.cloned.1.call-start
  10.9 1.2 slice_bitcast_fusion.12
  12.1 0.0 copy-start.6
  12.1 0.0 copy-start.7
  12.1 1.0 pad_maximum_fusion.1
  13.1 0.0 all-gather.3.cloned.1.call-update
  13.1 0.4 copy-done.6
  13.5 3.0 collective-permute-start
  16.5 0.7 dynamic_slice.9
  17.9 0.6 dynamic-slice_bitcast_fusion.vis_ref
  18.5 16.9 %collective-permute-done = bf16[256,1664]{1,0:T(8,128)(2,1)S(1)} collective-permute-done((bf16[256,1664]{1,0:T(8,128)(2,1)S(1)}, bf16[256,1664]{1,0:T(8,128)(2,1)S(1)}, u32[]{:S(2)}, u32[]{:S(2)}) %collective-permute-start) | collective-permute-done | bytes 852000 | tf_op jit(solution)/shard_map/ppermute | solution.py:163
  35.5 157.8 %all-gather.5.cloned.1.call-done = bf16[2,1664,1536]{2,1,0:T(8,128)(2,1)} async-done(((bf16[2,416,1536]{2,1,0:T(8,128)(2,1)}), bf16[2,1664,1536]{2,1,0:T(8,128)(2,1)}) %all-gather.5.cloned.1.call-update) | async-done | bytes 10223632 | tf_op jit(solution)/shard_map/all_gather | solution.py:199
  193.3 8.6 %fusion.2 = bf16[2,512,1536]{2,1,0:T(8,128)(2,1)S(1)} fusion(bf16[2,1664,1536]{2,1,0:T(8,128)(2,1)} %all-gather.5.cloned.1.call-done, bf16[256,1664]{1,0:T(8,128)(2,1)S(1)} %collective-permute-done, bf16[256,1664]{1,0:T(8,128)(2,1)S(1)} %copy-done.6, pred[]{:T(512)S(6)} %eq.4), kind=kOutput, calls=%fused_computation.6 | convolution fusion | flops 5243731968 | bytes 15073281 | tf_op jit(solution)/shard_map/td,sdc->stc/dot_general | solution.py:210
  201.9 1.9 slice_bitcast_fusion.6
  203.7 0.6 broadcast_in_dim.7.fac_ref
  204.3 21.5 %shard_map.86 = (bf16[1024,2048]{1,0:T(8,128)(2,1)}, bf16[512,1536]{1,0:T(8,128)(2,1)}, bf16[512,1536]{1,0:T(8,128)(2,1)}) custom-call(s32[4,4]{1,0:T(4,128)} %dynamic-slice_bitcast_fusion.vis_ref, f32[8,128]{1,0:T(8,128)} %broadcast_in_dim.7.fac_ref, bf16[1,1024,2048]{2,1,0:T(8,128)(2,1)} %q_ref.3, bf16[512,1536]{1,0:T(8,128)(2,1)} %get-tuple-element.17.k_ref, ...), custom_call_target="tpu_custom_call" | custom-call | tf_op jit(solution)/shard_map/pallas_call | solution.py:75
  225.9 6.1 %fusion = f32[512,1664]{1,0:T(8,128)S(1)} fusion(bf16[512,1536]{1,0:T(8,128)(2,1)} %get-tuple-element.10, bf16[2,1664,1536]{2,1,0:T(8,128)(2,1)} %all-gather.5.cloned.1.call-done), kind=kOutput, calls=%fused_computation.1 | convolution fusion | flops 2617245696 | bytes 10092544 | tf_op jit(solution)/shard_map/dot_general | solution.py:104
  232.0 7.2 %fusion.3 = f32[512,1664]{1,0:T(8,128)} fusion(f32[512,1664]{1,0:T(8,128)S(1)} %fusion, bf16[512,1536]{1,0:T(8,128)(2,1)S(1)} %copy-done.5, bf16[2,1664,1536]{2,1,0:T(8,128)(2,1)} %all-gather.5.cloned.1.call-done), kind=kOutput, calls=%fused_computation.7 | convolution fusion | flops 2618097664 | bytes 13500416 | tf_op jit(solution)/shard_map/dot_general | solution.py:104
  239.2 22.2 %all-gather.3.cloned.1.call-done = bf16[2,1664,512]{2,1,0:T(8,128)(2,1)} async-done(((bf16[2,416,512]{2,1,0:T(8,128)(2,1)}), bf16[2,1664,512]{2,1,0:T(8,128)(2,1)}) %all-gather.3.cloned.1.call-update) | async-done | bytes 3407888 | tf_op jit(solution)/shard_map/all_gather | solution.py:199
  261.4 4.0 %fusion.10 = bf16[2,512,512]{2,1,0:T(8,128)(2,1)S(1)} fusion(bf16[2,1664,512]{2,1,0:T(8,128)(2,1)} %all-gather.3.cloned.1.call-done, bf16[256,1664]{1,0:T(8,128)(2,1)S(1)} %collective-permute-done, bf16[256,1664]{1,0:T(8,128)(2,1)S(1)} %copy-done.6, pred[]{:T(512)S(6)} %eq.4), kind=kOutput, calls=%fused_computation.21 | convolution fusion | flops 1753022464 | bytes 6160385 | tf_op jit(solution)/shard_map/td,sdc->stc/dot_general | solution.py:210
  265.4 1.1 slice_bitcast_fusion.10
  266.5 9.5 %shard_map.87 = (bf16[1024,2048]{1,0:T(8,128)(2,1)}, bf16[512,512]{1,0:T(8,128)(2,1)}, bf16[512,512]{1,0:T(8,128)(2,1)}) custom-call(s32[4,4]{1,0:T(4,128)} %dynamic-slice_bitcast_fusion.vis_ref, f32[8,128]{1,0:T(8,128)} %broadcast_in_dim.7.fac_ref, bf16[1,1024,2048]{2,1,0:T(8,128)(2,1)} %q_ref.3, ...), custom_call_target="tpu_custom_call", output_to_operand_aliasing={{0}: (6, {})} | custom-call | tf_op jit(solution)/shard_map/pallas_call | solution.py:75
  276.1 2.3 fusion.6
  278.4 1.1 add_add_fusion
  279.6 0.2 select_convert_fusion
  279.7 0.1 collective-permute-start.1
  279.8 2.4 collective-permute-done.1
  282.2 0.3 convert_add_fusion
  282.5 1.5 collective-permute-start.4
  284.1 1.5 collective-permute-start.2
  285.6 6.7 %collective-permute-done.4 = bf16[2,128,640]{2,1,0:T(8,128)(2,1)S(1)} collective-permute-done((bf16[2,128,640]{2,1,0:T(8,128)(2,1)S(1)}, bf16[2,128,640]{2,1,0:T(8,128)(2,1)S(1)}, u32[]{:S(2)}, u32[]{:S(2)}) %collective-permute-start.4) | collective-permute-done | bytes 327712 | tf_op jit(solution)/shard_map/ppermute | solution.py:110
  292.3 0.1 convert_add_fusion.1
  292.4 1.5 collective-permute-start.5
  294.0 0.0 collective-permute-done.2
  294.0 0.1 fusion.13
  294.1 1.5 collective-permute-start.3
  295.6 2.3 collective-permute-done.5
  297.9 0.1 fusion.14
  298.0 3.4 %collective-permute-done.3 = bf16[128,1024]{1,0:T(8,128)(2,1)S(1)} collective-permute-done((bf16[128,1024]{1,0:T(8,128)(2,1)S(1)}, bf16[128,1024]{1,0:T(8,128)(2,1)S(1)}, u32[]{:S(2)}, u32[]{:S(2)}) %collective-permute-start.3) | collective-permute-done | bytes 262176 | tf_op jit(solution)/shard_map/ppermute | solution.py:110
  301.4 0.1 add_convert_fusion
  301.5 0.1 collective-permute-start.6
  301.5 1.8 collective-permute-done.6
  303.3 1.1 maximum_select_fusion.1
  (16 shorter events, 0.2 us)
Async XLA Ops:
  7.2 10.8 %copy-start = (s32[4,4,4]{2,1,0:T(4,128)S(1)}, s32[4,4,4]{2,1,0:T(4,128)}, u32[]{:S(2)}) copy-start(s32[4,4,4]{2,1,0:T(4,128)} %param.12) | copy-start | bytes 772
  7.2 186.1 %all-gather.5.cloned.1.call-start = ((), (), s32[]{:S(2)}) async-start(), calls=%async_computation.1 | async-start | bytes 12779520 | tf_op jit(solution)/shard_map/all_gather | solution.py:199
  10.8 250.6 %all-gather.3.cloned.1.call-start = ((), (), s32[]{:S(2)}) async-start(), calls=%async_computation | async-start | bytes 4259840 | tf_op jit(solution)/shard_map/all_gather | solution.py:199
  12.1 1.5 copy-start.6
  12.1 4.5 %copy-start.7 = (f32[2]{0:T(128)S(1)}, f32[2]{0:T(128)}, u32[]{:S(2)}) copy-start(f32[2]{0:T(128)} %param.11) | copy-start | bytes 28
  13.5 21.9 %collective-permute-start = (bf16[256,1664]{1,0:T(8,128)(2,1)S(1)}, bf16[256,1664]{1,0:T(8,128)(2,1)S(1)}, u32[]{:S(2)}, u32[]{:S(2)}) collective-permute-start(bf16[256,1664]{1,0:T(8,128)(2,1)S(1)} %copy-done.6), channel_id=1, source_target_pairs={{0,4},{4,0},{1,5},{5,1},{2,6},{6,2},{3,7},{7,3},{8,12},{12,8},{9,1... | collective-permute-start | bytes 2555912 | tf_op jit(solution)/shard_map/ppermute | solution.py:163
  225.9 6.1 %copy-start.5 = (bf16[512,1536]{1,0:T(8,128)(2,1)S(1)}, bf16[512,1536]{1,0:T(8,128)(2,1)}, u32[]{:S(2)}) copy-start(bf16[512,1536]{1,0:T(8,128)(2,1)} %get-tuple-element.9) | copy-start | bytes 4718596
  266.5 9.5 %copy-start.2 = (bf16[2,1664,512]{2,1,0:T(8,128)(2,1)S(1)}, bf16[2,1664,512]{2,1,0:T(8,128)(2,1)}, u32[]{:S(2)}) copy-start(bf16[2,1664,512]{2,1,0:T(8,128)(2,1)} %all-gather.3.cloned.1.call-done) | copy-start | bytes 10223620
  276.0 2.4 copy-start.3
  276.0 2.4 copy-start.4
  279.7 2.4 collective-permute-start.1
  282.5 9.8 %collective-permute-start.4 = (bf16[2,128,640]{2,1,0:T(8,128)(2,1)S(1)}, bf16[2,128,640]{2,1,0:T(8,128)(2,1)S(1)}, u32[]{:S(2)}, u32[]{:S(2)}) collective-permute-start(bf16[2,128,640]{2,1,0:T(8,128)(2,1)S(1)} %slice.138), channel_id=1, source_target_pairs={{0,2},{2,0},{1,3},{3,1},{4,6},{6,4},{5,7},{7,5},{8,10},{10,8},{9,1... | collective-permute-start | bytes 983048 | tf_op jit(solution)/shard_map/ppermute | solution.py:110
  284.1 9.9 %collective-permute-start.2 = (bf16[128,1024]{1,0:T(8,128)(2,1)S(1)}, bf16[128,1024]{1,0:T(8,128)(2,1)S(1)}, u32[]{:S(2)}, u32[]{:S(2)}) collective-permute-start(bf16[128,1024]{1,0:T(8,128)(2,1)S(1)} %fusion.15), channel_id=1, source_target_pairs={{0,4},{4,0},{1,5},{5,1},{2,6},{6,2},{3,7},{7,3},{8,12},{12,8},{9,1... | collective-permute-start | bytes 786440 | tf_op jit(solution)/shard_map/ppermute | solution.py:110
  292.4 5.5 %collective-permute-start.5 = (bf16[128,640]{1,0:T(8,128)(2,1)S(1)}, bf16[128,640]{1,0:T(8,128)(2,1)S(1)}, u32[]{:S(2)}, u32[]{:S(2)}) collective-permute-start(bf16[128,640]{1,0:T(8,128)(2,1)S(1)} %fusion.16), channel_id=1, source_target_pairs={{0,4},{4,0},{1,5},{5,1},{2,6},{6,2},{3,7},{7,3},{8,12},{12,8},{9,1... | collective-permute-start | bytes 491528 | tf_op jit(solution)/shard_map/ppermute | solution.py:110
  294.1 7.3 %collective-permute-start.3 = (bf16[128,1024]{1,0:T(8,128)(2,1)S(1)}, bf16[128,1024]{1,0:T(8,128)(2,1)S(1)}, u32[]{:S(2)}, u32[]{:S(2)}) collective-permute-start(bf16[128,1024]{1,0:T(8,128)(2,1)S(1)} %fusion.13), channel_id=1, source_target_pairs={{0,2},{2,0},{1,3},{3,1},{4,6},{6,4},{5,7},{7,5},{8,10},{10,8},{9,1... | collective-permute-start | bytes 786440 | tf_op jit(solution)/shard_map/ppermute | solution.py:110
  297.9 6.5 %copy-start.1 = (s32[4,4,4]{2,1,0:T(4,128)S(1)}, s32[4,4,4]{2,1,0:T(4,128)}, u32[]{:S(2)}) copy-start(s32[4,4,4]{2,1,0:T(4,128)} %param.12) | copy-start | bytes 772
  301.5 1.8 collective-permute-start.6
Sparse Core Ops, SparseCore 0:
  10.9 182.3 all-gather.4
  195.4 65.9 all-gather.2
